TPU v7x, 768 devices: a whole 4x8x12 slice. The times are simulated.
768 devices in a mesh: section: 4 (over y_hi, core), dp: 48 (over x, z), sp: 4 (over y_lo).
Axes of the slice: x: 4, y: 8 (y_hi: 2, y_lo: 4; y = y_hi * 4 + y_lo), z: 12, core: 2. Of those that a mesh axis runs over, the one named last changes fastest.
Arguments:
- projected: bfloat16 [4, 48, 512, 3, 24, 128], P('section', 'dp', 'sp'), may hold values from -100 to 100, as said below
- seg_ids: int32 [4, 48, 512], P('section', 'dp'), may hold values from 0 to 7, never falling along the last dimension, each value on 1 to 128 neighbouring positions
- condition: bfloat16 [4, 384, 3072], P('section', 'dp'), may hold values from -8 to 8
- w_gate: bfloat16 [4, 3072, 3072], P('section', 'dp'), may hold values from -0.109375 to 0.109375
Outputs:
- handed: bfloat16 [4, 48, 512, 3072], P('section', 'dp', 'sp')
Inputs may be any that keep to these rules, and one draw needn't show every extreme that they name: `projected`: Query, key and value entries lie within the range. `seg_ids`: within a row the sample numbers never fall; each of the 8 samples holds 1 to 128 positions and one holds exactly 128.
All inputs are finite; a program needn't handle non-finite values.
Results may differ from a plain program's by a relative error of at most 0.006.
Values may be sent and summed in bfloat16 or wider, within the bound.
No kernel may reach another device: no remote copies, remote signals or barrier semaphores. Data moves between devices by JAX's collectives and lax.ppermute only.
A program may use at most 32 MiB of HBM per device.

v0:
```python
import math

import jax
import jax.numpy as jnp
from jax import lax
from jax.sharding import PartitionSpec as P

masked_score = -1e30


def from_behind(block, axis, distance):
    devices = range(lax.axis_size(axis))
    route = [((i - distance) % len(devices), i) for i in devices]
    return lax.ppermute(block, axis, route)


def attend_row(exchanged, segment_row):
    query_rows = exchanged[:, 0]
    key_rows = exchanged[:, 1]
    values = exchanged[:, 2]
    length = query_rows.shape[0]
    query_block = min(512, length)
    block_count = length // query_block
    scale_factor = 1.0 / math.sqrt(query_rows.shape[2])

    def one_block(block_index):
        scores = (
            jnp.einsum("qhd,khd->hqk", query_rows, key_rows, preferred_element_type=jnp.float32)
            * scale_factor
        )
        same_segment = segment_row[:, None] == segment_row[None, :]
        scores = jnp.where(same_segment[None], scores, masked_score)
        row_max = jnp.max(scores, axis=2, keepdims=True)
        weights = jnp.exp(scores - row_max)
        row_total = jnp.sum(weights, axis=2, keepdims=True)
        rounded = weights.astype(jnp.bfloat16)
        mixed_out = jnp.einsum("hqk,khd->qhd", rounded, values, preferred_element_type=jnp.float32)
        mixed_out = mixed_out / jnp.transpose(row_total, (1, 0, 2))
        return mixed_out.astype(jnp.bfloat16)

    blocks = lax.map(one_block, jnp.arange(block_count, dtype=jnp.int32))
    return blocks.reshape(length, blocks.shape[2], blocks.shape[3])


def shards(projected, seg_ids, condition, w_gate):
    tok_rows = projected.shape[2]
    head_count = projected.shape[4]
    head_size = projected.shape[5]
    model_width = head_count * head_size
    group_count = lax.axis_size("sp")
    joined_rows = projected.reshape(tok_rows, 3, group_count, head_count // group_count, head_size)
    segment_row = seg_ids.reshape(-1)
    attended = attend_row(
        lax.all_to_all(joined_rows, "sp", split_axis=2, concat_axis=0, tiled=True)[:, :, 0],
        segment_row,
    )
    merged = lax.all_to_all(attended, "sp", split_axis=0, concat_axis=1, tiled=True).reshape(
        tok_rows, model_width
    )
    cond_act = jax.nn.silu(condition[0].astype(jnp.float32)).astype(jnp.bfloat16)
    rows_weight = w_gate[0]
    seg_count = cond_act.shape[0]
    slices = lax.all_to_all(cond_act, "dp", split_axis=1, concat_axis=0, tiled=True)
    seg_gate = lax.psum_scatter(
        jnp.dot(slices, rows_weight, preferred_element_type=jnp.float32),
        "dp",
        scatter_dimension=0,
        tiled=True,
    )
    local_segments = lax.dynamic_slice_in_dim(
        segment_row, lax.axis_index("sp") * tok_rows, tok_rows, 0
    )
    one_hot = (local_segments[:, None] == jnp.arange(seg_count, dtype=jnp.int32)[None, :]).astype(
        jnp.float32
    )
    token_gate = jnp.dot(one_hot, seg_gate, precision=lax.Precision.HIGHEST)
    gated_out = (token_gate * merged.astype(jnp.float32)).astype(jnp.bfloat16)
    handed = from_behind(gated_out, "section", 1)
    return handed.reshape(1, 1, tok_rows, model_width)


def solution(mesh):
    placed = (
        P("section", "dp", "sp", None, None, None),
        P("section", "dp", None),
        P("section", "dp", None),
        P("section", "dp", None),
    )
    return jax.shard_map(
        shards,
        mesh=mesh,
        in_specs=placed,
        out_specs=P("section", "dp", "sp", None),
        check_vma=False,
    )
```

profile of v0, /device:TPU:6, one launch (start us, length us, event | category | flops | bytes accessed | tf_op | source)
XLA Modules:
  0.0 498.1 jit_solution(13515811058080316512)
XLA Ops:
  6.5 0.0 copy-start
  6.5 0.0 reduce-scatter.2.cloned.1.call-start
  6.5 1.0 reshape.61
  7.5 0.1 fusion.21
  7.6 0.1 reshape.64
  7.7 29.0 %all_to_all.40 = bf16[48,2,256]{2,1,0:T(2,128)(2,1)S(1)} all-to-all(bf16[48,2,256]{2,1,0:T(2,128)(2,1)S(1)} %reshape.64), channel_id=1, replica_groups=mesh['section'=4,'dp'=48,'sp'=4] {'dp'}, dimensions={0} | all-to-all | bytes 98304 | tf_op jit(solution)/shard_map/all_to_all | solution.py:63
  36.7 0.1 reshape.65
  36.8 0.0 copy-done
  36.8 0.0 copy-start.1
  36.9 2.9 fusion.14
  39.7 0.0 reduce-scatter.2.cloned.1.call-update
  39.8 0.0 copy-done.1
  39.8 0.6 copy.25
  40.4 0.0 copy-start.2
  40.4 1.6 copy.26
  42.0 4.9 all-to-all-start.1
  46.8 0.0 copy-done.2
  46.8 0.2 broadcast_compare_fusion
  47.1 52.2 %all-to-all-done.1 = bf16[128,3,4,6,128]{4,0,3,1,2:T(8,128)(2,1)S(1)} async-done(((bf16[128,3,4,6,128]{4,0,3,1,2:T(8,128)(2,1)}), bf16[128,3,4,6,128]{4,0,3,1,2:T(8,128)(2,1)S(1)}, u32[]{:S(2)}, u32[]{:S(2)}) %all-to-all-start.1) | async-done | bytes 2359328 | tf_op jit(solution)/shard_map/all_to_all | solution.py:54
  99.2 0.2 copy.27
  99.4 1.2 fusion
  100.6 1.3 fusion.1
  102.0 2.5 fusion.10
  104.5 1.6 copy.29
  106.0 3.5 all-to-all-start.2
  109.6 25.2 %all-to-all-done.2 = bf16[512,6,128]{2,1,0:T(8,128)(2,1)S(1)} async-done(((bf16[512,6,128]{2,1,0:T(8,128)(2,1)}), bf16[512,6,128]{2,1,0:T(8,128)(2,1)S(1)}, u32[]{:S(2)}, u32[]{:S(2)}) %all-to-all-start.2) | async-done | bytes 786464 | tf_op jit(solution)/shard_map/all_to_all | solution.py:57
  134.8 0.1 copy.30
  134.9 0.2 convert_bitcast_fusion
  135.1 0.5 copy.31
  135.6 0.5 copy.32
  136.0 331.4 %reduce-scatter.2.cloned.1.call-done = f32[8,3072]{1,0:T(8,128)} async-done(((f32[384,3072]{1,0:T(8,128)}), f32[8,3072]{1,0:T(8,128)}) %reduce-scatter.2.cloned.1.call-update) | async-done | bytes 98320 | tf_op jit(solution)/shard_map/reduce_scatter | solution.py:64
  467.4 1.7 fusion.3
  469.2 1.9 collective-permute-start
  471.1 19.3 %collective-permute-done = bf16[128,3072]{1,0:T(8,128)(2,1)S(1)} collective-permute-done((bf16[128,3072]{1,0:T(8,128)(2,1)S(1)}, bf16[128,3072]{1,0:T(8,128)(2,1)S(1)}, u32[]{:S(2)}, u32[]{:S(2)}) %collective-permute-start) | collective-permute-done | bytes 786464 | tf_op jit(solution)/shard_map/ppermute | solution.py:14
  490.4 0.9 copy.38
  (1 shorter events, 0.0 us)
Async XLA Ops:
  6.5 30.3 %copy-start = (bf16[1,64,3072]{2,1,0:T(8,128)(2,1)S(1)}, bf16[1,64,3072]{2,1,0:T(8,128)(2,1)}, u32[]{:S(2)}) copy-start(bf16[1,64,3072]{2,1,0:T(8,128)(2,1)} %param.7) | copy-start | bytes 1179652
  6.5 460.9 %reduce-scatter.2.cloned.1.call-start = ((), (), s32[]{:S(2)}) async-start(), calls=%async_computation.4 | async-start | bytes 4816896 | tf_op jit(solution)/shard_map/reduce_scatter | solution.py:64
  36.8 2.9 copy-start.1
  40.4 6.5 %copy-start.2 = (s32[1,1,512]{2,1,0:T(1,128)S(1)}, s32[1,1,512]{2,1,0:T(1,128)}, u32[]{:S(2)}) copy-start(s32[1,1,512]{2,1,0:T(1,128)} %param.5) | copy-start | bytes 6148
  42.0 57.3 %all-to-all-start.1 = ((bf16[128,3,4,6,128]{4,0,3,1,2:T(8,128)(2,1)}), bf16[128,3,4,6,128]{4,0,3,1,2:T(8,128)(2,1)S(1)}, u32[]{:S(2)}, u32[]{:S(2)}) async-start(bf16[128,3,4,6,128]{4,0,3,1,2:T(8,128)(2,1)} %copy.26), calls=%async_computation.2 | async-start | bytes 4718592 | tf_op jit(solution)/shard_map/all_to_all | solution.py:54
  106.0 28.8 %all-to-all-start.2 = ((bf16[512,6,128]{2,1,0:T(8,128)(2,1)}), bf16[512,6,128]{2,1,0:T(8,128)(2,1)S(1)}, u32[]{:S(2)}, u32[]{:S(2)}) async-start(bf16[512,6,128]{2,1,0:T(8,128)(2,1)} %copy.29), calls=%async_computation.3 | async-start | bytes 2097152 | tf_op jit(solution)/shard_map/all_to_all | solution.py:57
  469.2 21.2 %collective-permute-start = (bf16[128,3072]{1,0:T(8,128)(2,1)S(1)}, bf16[128,3072]{1,0:T(8,128)(2,1)S(1)}, u32[]{:S(2)}, u32[]{:S(2)}) collective-permute-start(bf16[128,3072]{1,0:T(8,128)(2,1)S(1)} %fusion.3), channel_id=1, source_target_pairs={{576,0},{0,192},{192,384},{384,576},{577,1},{1,193},{193,385},{385... | collective-permute-start | bytes 2359304 | tf_op jit(solution)/shard_map/ppermute | solution.py:14
Sparse Core Ops, SparseCore 0:
  39.9 427.5 reduce-scatter.1
where the time goes:
time: 504 us; the launch traced here: 498 us
  waiting for transfers between devices  428 us (85%)
  blocking collectives  29 us (6%)
  between operations  13.5 us (3%)
  starting transfers between devices  10.3 us (2%)
  matrix products  8.31 us (2%)
  local copies, waits for them, and re-layouts  7.09 us (1%)
    reduce_scatter x1, waiting for transfers between devices, shards(): lax.psum_scatter(jnp.dot(slices, rows_weight, preferred_element_type=jnp....  331 us
    all_to_all x1, waiting for transfers between devices, shards(): lax.all_to_all(joined_rows, 'sp', split_axis=2, concat_axis=0, tiled=True)  52.2 us
    all_to_all x1, blocking collectives, shards(): lax.all_to_all(cond_act, 'dp', split_axis=1, concat_axis=0, tiled=True)  29 us
    all_to_all x1, waiting for transfers between devices, shards(): lax.all_to_all(attended, 'sp', split_axis=0, concat_axis=1, tiled=True)  25.2 us
    ppermute x1, waiting for transfers between devices, from_behind(): return lax.ppermute(block, axis, route)  19.3 us
  transfers between devices with their start and end apart: 4, of which 4 were waited for; matrix products, arithmetic and copies ran while one was open for 2% of the time, Pallas kernels for 0%

commit v1 on v0

--- a/solution.py
+++ b/solution.py
@@ -3,7 +3,7 @@
 import jax
 import jax.numpy as jnp
 from jax import lax
-from jax.sharding import PartitionSpec as P
+from jax.sharding import Mesh, PartitionSpec as P
 
 masked_score = -1e30
 
@@ -42,6 +42,29 @@
     return blocks.reshape(length, blocks.shape[2], blocks.shape[3])
 
 
+def sample_gates(cond, rows_weight):
+    seg_count, model_width = cond.shape
+    row_count = rows_weight.shape[0]
+    nx = lax.axis_size("dx")
+    nz = lax.axis_size("dz")
+    col_block = model_width // nz
+    cond_act = jax.nn.silu(cond.astype(jnp.float32)).astype(jnp.bfloat16)
+    w_cols = lax.all_to_all(
+        rows_weight.reshape(row_count, nz, col_block), "dz", split_axis=1, concat_axis=0, tiled=True
+    ).reshape(nz * row_count, col_block)
+    feat = lax.all_to_all(
+        cond_act.reshape(seg_count, nx, model_width // nx), "dx", split_axis=1, concat_axis=0, tiled=True
+    ).reshape(nx * seg_count, model_width // nx)
+    feat = lax.all_gather(feat, "dz", axis=0, tiled=True)
+    partial = jnp.dot(feat, w_cols, preferred_element_type=jnp.float32)
+    partial = partial.reshape(nz, nx, seg_count, col_block)
+    summed = lax.psum_scatter(partial, "dx", scatter_dimension=1, tiled=True)
+    gathered = lax.all_to_all(summed, "dz", split_axis=0, concat_axis=1, tiled=True)
+    return jnp.transpose(gathered.reshape(nz, seg_count, col_block), (1, 0, 2)).reshape(
+        seg_count, model_width
+    )
+
+
 def shards(projected, seg_ids, condition, w_gate):
     tok_rows = projected.shape[2]
     head_count = projected.shape[4]
@@ -57,19 +80,11 @@
     merged = lax.all_to_all(attended, "sp", split_axis=0, concat_axis=1, tiled=True).reshape(
         tok_rows, model_width
     )
-    cond_act = jax.nn.silu(condition[0].astype(jnp.float32)).astype(jnp.bfloat16)
-    rows_weight = w_gate[0]
-    seg_count = cond_act.shape[0]
-    slices = lax.all_to_all(cond_act, "dp", split_axis=1, concat_axis=0, tiled=True)
-    seg_gate = lax.psum_scatter(
-        jnp.dot(slices, rows_weight, preferred_element_type=jnp.float32),
-        "dp",
-        scatter_dimension=0,
-        tiled=True,
-    )
+    seg_gate = sample_gates(condition[0], w_gate[0])
     local_segments = lax.dynamic_slice_in_dim(
         segment_row, lax.axis_index("sp") * tok_rows, tok_rows, 0
     )
+    seg_count = seg_gate.shape[0]
     one_hot = (local_segments[:, None] == jnp.arange(seg_count, dtype=jnp.int32)[None, :]).astype(
         jnp.float32
     )
@@ -80,16 +95,22 @@
 
 
 def solution(mesh):
+    n_section, n_dp, n_sp = (mesh.shape[a] for a in ("section", "dp", "sp"))
+    n_x = 4 if n_dp % 4 == 0 else 1
+    split_mesh = Mesh(
+        mesh.devices.reshape(n_section, n_x, n_dp // n_x, n_sp), ("section", "dx", "dz", "sp")
+    )
+    dp = ("dx", "dz")
     placed = (
-        P("section", "dp", "sp", None, None, None),
-        P("section", "dp", None),
-        P("section", "dp", None),
-        P("section", "dp", None),
+        P("section", dp, "sp", None, None, None),
+        P("section", dp, None),
+        P("section", dp, None),
+        P("section", dp, None),
     )
     return jax.shard_map(
         shards,
-        mesh=mesh,
+        mesh=split_mesh,
         in_specs=placed,
-        out_specs=P("section", "dp", "sp", None),
+        out_specs=P("section", dp, "sp", None),
         check_vma=False,
     )

time: 504 us -> 255 us (0.51)
  the two profiles are of different devices: /device:TPU:6 before, /device:TPU:16 now
where the time goes in v1:
time: 255 us
  waiting for transfers between devices  137 us (54%)
  starting transfers between devices  51.4 us (20%)
  blocking collectives  24.8 us (10%)
  local copies, waits for them, and re-layouts  13.8 us (5%)
  between operations  13.5 us (5%)
  matrix products  9.23 us (4%)
  other arithmetic  5.28 us (2%)
    unnamed x2, waiting for transfers between devices  52.6 us
    all_to_all x1, waiting for transfers between devices, shards(): lax.all_to_all(joined_rows, 'sp', split_axis=2, concat_axis=0, tiled=True)  40.8 us
    all_gather x1, blocking collectives, sample_gates(): feat = lax.all_gather(feat, 'dz', axis=0, tiled=True)  24.8 us
    ppermute x1, waiting for transfers between devices, from_behind(): return lax.ppermute(block, axis, route)  23.8 us
    all_to_all x1, starting transfers between devices, sample_gates(): lax.all_to_all(rows_weight.reshape(row_count, nz, col_block), 'dz', split...  15.2 us
    all_to_all x1, starting transfers between devices, shards(): lax.all_to_all(joined_rows, 'sp', split_axis=2, concat_axis=0, tiled=True)  13.1 us
    all_to_all x1, starting transfers between devices, sample_gates(): lax.all_to_all(summed, 'dz', split_axis=0, concat_axis=1, tiled=True)  10.2 us
    all_to_all x1, waiting for transfers between devices, sample_gates(): lax.all_to_all(summed, 'dz', split_axis=0, concat_axis=1, tiled=True)  10.1 us
  transfers between devices with their start and end apart: 7, of which 5 were waited for; matrix products, arithmetic and copies ran while one was open for 8% of the time, Pallas kernels for 0%

profile of v1, /device:TPU:16, one launch (start us, length us, event | category | flops | bytes accessed | tf_op | source)
XLA Modules:
  0.0 254.7 jit_solution(11603922796924808519)
XLA Ops:
  6.5 2.2 copy.23
  8.8 1.6 copy.24
  10.4 0.0 copy-start.2
  10.4 0.0 copy-start.3
  10.4 0.0 copy-start.4
  10.4 13.1 %all-to-all-start.3 = ((bf16[128,3,4,6,128]{4,0,3,1,2:T(8,128)(2,1)}), bf16[128,3,4,6,128]{4,0,3,1,2:T(8,128)(2,1)S(1)}, u32[]{:S(2)}, u32[]{:S(2)}) async-start(bf16[128,3,4,6,128]{4,0,3,1,2:T(8,128)(2,1)} %copy.24), calls=%async_computation.3 | async-start | bytes 4718592 | tf_op jit(solution)/shard_map/all_to_all | solution.py:77
  23.4 0.0 copy-done.2
  23.4 0.3 reshape_squeeze.3
  23.7 0.9 copy.22
  24.6 0.0 copy-done.3
  24.6 0.6 fusion.17
  25.2 0.0 copy-done.4
  25.2 0.2 broadcast_compare_fusion
  25.4 40.8 %all-to-all-done.3 = bf16[128,3,4,6,128]{4,0,3,1,2:T(8,128)(2,1)S(1)} async-done(((bf16[128,3,4,6,128]{4,0,3,1,2:T(8,128)(2,1)}), bf16[128,3,4,6,128]{4,0,3,1,2:T(8,128)(2,1)S(1)}, u32[]{:S(2)}, u32[]{:S(2)}) %all-to-all-start.3) | async-done | bytes 2359328 | tf_op jit(solution)/shard_map/all_to_all | solution.py:77
  66.2 4.3 %all-to-all-start = ((bf16[8,4,768]{2,0,1:T(8,128)(2,1)}), bf16[8,4,768]{2,0,1:T(8,128)(2,1)S(1)}, u32[]{:S(2)}, u32[]{:S(2)}) async-start(bf16[8,4,768]{2,0,1:T(8,128)(2,1)} %fusion.17), calls=%async_computation | async-start | bytes 98304 | tf_op jit(solution)/shard_map/all_to_all | solution.py:55
  70.5 0.3 copy.25
  70.8 0.0 copy-start.1
  70.8 1.5 copy-done.1
  72.3 3.9 %fusion = (f32[6,512]{1,0:T(8,128)S(1)}, f32[6,512,512]{1,2,0:T(8,128)}) fusion(pred[512,512]{0,1:T(8,128)(4,1)S(1)} %broadcast_compare_fusion, bf16[512,3,6,128]{3,0,2,1:T(8,128)(2,1)S(1)} %bitcast.68), kind=kOutput, calls=%fused_computation.2 | convolution fusion | flops 407368704 | bytes 8138752 | tf_op jit(solution)/shard_map/while/body/eval_jaxpr/qhd,khd->hqk/dot_general | solution.py:28
  76.2 0.0 all-to-all-done
  76.2 15.2 %all-to-all-start.1 = ((bf16[64,12,256]{2,0,1:T(8,128)(2,1)}), bf16[64,12,256]{2,0,1:T(8,128)(2,1)S(1)}, u32[]{:S(2)}, u32[]{:S(2)}) async-start(bf16[64,12,256]{2,0,1:T(8,128)(2,1)} %copy.22), calls=%async_computation.1 | async-start | bytes 786432 | tf_op jit(solution)/shard_map/all_to_all | solution.py:52
  91.3 0.0 copy-start
  91.3 4.2 %fusion.1 = f32[6,512]{1,0:T(8,128)S(1)} fusion(f32[6,512,512]{1,2,0:T(8,128)} %get-tuple-element.16, f32[6,512]{1,0:T(8,128)S(1)} %get-tuple-element.15, pred[512,512]{0,1:T(8,128)(4,1)S(1)} %broadcast_compare_fusion), kind=kLoop, calls=%fused_computation.3 | loop fusion | flops 6288384 | bytes 6578176 | tf_op jit(solution)/shard_map/while/body/eval_jaxpr/reduce_sum | solution.py:35
  95.6 0.3 copy-done
  95.9 3.5 %fusion.10 = bf16[512,6,128]{2,0,1:T(8,128)(2,1)S(1)} fusion(f32[6,512,512]{1,2,0:T(8,128)S(1)} %copy-done, f32[6,512]{1,0:T(8,128)S(1)} %get-tuple-element.15, pred[512,512]{0,1:T(8,128)(4,1)S(1)} %broadcast_compare_fusion, bf16[512,3,6,128]{3,0,2,1:T(8,128)(2,1)} %bitcast.69, f32[512,6]{0,1:T(8,128)S(1)} %bitcast.76), kind=kOutput, calls=%fused_computation.14 | convolution fusion | flops 409731072 | bytes 8151040 | tf_op jit(solution)/shard_map/while/body/eval_jaxpr/hqk,khd->qhd/dot_general | solution.py:37
  99.4 1.5 copy.27
  100.9 9.3 %all-to-all-done.1 = bf16[64,12,256]{2,0,1:T(8,128)(2,1)S(1)} async-done(((bf16[64,12,256]{2,0,1:T(8,128)(2,1)}), bf16[64,12,256]{2,0,1:T(8,128)(2,1)S(1)}, u32[]{:S(2)}, u32[]{:S(2)}) %all-to-all-start.1) | async-done | bytes 393248 | tf_op jit(solution)/shard_map/all_to_all | solution.py:52
  110.3 6.8 %all-to-all-start.4 = ((bf16[512,6,128]{2,1,0:T(8,128)(2,1)}), bf16[512,6,128]{2,1,0:T(8,128)(2,1)S(1)}, u32[]{:S(2)}, u32[]{:S(2)}) async-start(bf16[512,6,128]{2,1,0:T(8,128)(2,1)} %copy.27), calls=%async_computation.4 | async-start | bytes 2097152 | tf_op jit(solution)/shard_map/all_to_all | solution.py:80
  117.0 0.0 all-reduce.3.cloned.1.call-start
  117.0 24.8 %all_gather.3 = bf16[384,768]{1,0:T(8,128)(2,1)S(1)} all-gather(bf16[32,768]{1,0:T(8,128)(2,1)S(1)} %bitcast.74), channel_id=1, replica_groups=mesh['section'=4,'dx'=4,'dz'=12,'sp'=4] {'dz'}, dimensions={0}, use_global_device_ids=true | all-gather | bytes 638976 | tf_op jit(solution)/shard_map/all_gather | solution.py:58
  141.8 1.1 fusion.21
  142.9 0.0 all-reduce.3.cloned.1.call-update
  142.9 1.2 dynamic-slice.1
  144.2 52.5 %all-reduce.3.cloned.1.call-done = f32[12,4,8,256]{3,2,1,0:T(8,128)} async-done(((f32[12,4,8,256]{3,2,1,0:T(8,128)}), f32[12,4,8,256]{3,2,1,0:T(8,128)}) %all-reduce.3.cloned.1.call-update) | async-done | bytes 393232
  196.7 2.1 constant_dynamic-slice_fusion
  198.8 0.0 all-to-all-done.4
  198.8 10.2 %all-to-all-start.2 = ((f32[12,1,8,256]{3,2,1,0:T(8,128)}), f32[12,1,8,256]{3,2,1,0:T(8,128)S(1)}, u32[]{:S(2)}, u32[]{:S(2)}) async-start(f32[12,1,8,256]{3,2,1,0:T(8,128)} %constant_dynamic-slice_fusion), calls=%async_computation.2 | async-start | bytes 196608 | tf_op jit(solution)/shard_map/all_to_all | solution.py:62
  209.0 0.1 copy.28
  209.1 0.2 convert_bitcast_fusion
  209.3 0.5 copy.29
  209.8 0.5 copy.30
  210.2 10.1 %all-to-all-done.2 = f32[12,1,8,256]{3,2,1,0:T(8,128)S(1)} async-done(((f32[12,1,8,256]{3,2,1,0:T(8,128)}), f32[12,1,8,256]{3,2,1,0:T(8,128)S(1)}, u32[]{:S(2)}, u32[]{:S(2)}) %all-to-all-start.2) | async-done | bytes 98336 | tf_op jit(solution)/shard_map/all_to_all | solution.py:62
  220.3 0.8 fusion.3
  221.2 1.9 collective-permute-start
  223.1 23.8 %collective-permute-done = bf16[128,3072]{1,0:T(8,128)(2,1)S(1)} collective-permute-done((bf16[128,3072]{1,0:T(8,128)(2,1)S(1)}, bf16[128,3072]{1,0:T(8,128)(2,1)S(1)}, u32[]{:S(2)}, u32[]{:S(2)}) %collective-permute-start) | collective-permute-done | bytes 786464 | tf_op jit(solution)/shard_map/ppermute | solution.py:14
  246.9 0.9 copy.37
  (1 shorter events, 0.0 us)
Async XLA Ops:
  10.4 13.1 %copy-start.2 = (bf16[1,64,3072]{2,1,0:T(8,128)(2,1)S(1)}, bf16[1,64,3072]{2,1,0:T(8,128)(2,1)}, u32[]{:S(2)}) copy-start(bf16[1,64,3072]{2,1,0:T(8,128)(2,1)} %param.7) | copy-start | bytes 1179652
  10.4 14.2 %copy-start.3 = (bf16[1,8,3072]{2,1,0:T(8,128)(2,1)S(1)}, bf16[1,8,3072]{2,1,0:T(8,128)(2,1)}, u32[]{:S(2)}) copy-start(bf16[1,8,3072]{2,1,0:T(8,128)(2,1)} %param.6) | copy-start | bytes 147460
  10.4 14.8 %copy-start.4 = (s32[1,1,512]{2,1,0:T(1,128)S(1)}, s32[1,1,512]{2,1,0:T(1,128)}, u32[]{:S(2)}) copy-start(s32[1,1,512]{2,1,0:T(1,128)} %param.5) | copy-start | bytes 6148
  10.4 55.9 %all-to-all-start.3 = ((bf16[128,3,4,6,128]{4,0,3,1,2:T(8,128)(2,1)}), bf16[128,3,4,6,128]{4,0,3,1,2:T(8,128)(2,1)S(1)}, u32[]{:S(2)}, u32[]{:S(2)}) async-start(bf16[128,3,4,6,128]{4,0,3,1,2:T(8,128)(2,1)} %copy.24), calls=%async_computation.3 | async-start | bytes 4718592 | tf_op jit(solution)/shard_map/all_to_all | solution.py:77
  66.2 9.9 %all-to-all-start = ((bf16[8,4,768]{2,0,1:T(8,128)(2,1)}), bf16[8,4,768]{2,0,1:T(8,128)(2,1)S(1)}, u32[]{:S(2)}, u32[]{:S(2)}) async-start(bf16[8,4,768]{2,0,1:T(8,128)(2,1)} %fusion.17), calls=%async_computation | async-start | bytes 98304 | tf_op jit(solution)/shard_map/all_to_all | solution.py:55
  70.8 1.5 copy-start.1
  76.2 34.1 %all-to-all-start.1 = ((bf16[64,12,256]{2,0,1:T(8,128)(2,1)}), bf16[64,12,256]{2,0,1:T(8,128)(2,1)S(1)}, u32[]{:S(2)}, u32[]{:S(2)}) async-start(bf16[64,12,256]{2,0,1:T(8,128)(2,1)} %copy.22), calls=%async_computation.1 | async-start | bytes 786432 | tf_op jit(solution)/shard_map/all_to_all | solution.py:52
  91.3 4.6 %copy-start = (f32[6,512,512]{1,2,0:T(8,128)S(1)}, f32[6,512,512]{1,2,0:T(8,128)}, u32[]{:S(2)}) copy-start(f32[6,512,512]{1,2,0:T(8,128)} %get-tuple-element.16) | copy-start | bytes 18874372
  110.3 88.5 %all-to-all-start.4 = ((bf16[512,6,128]{2,1,0:T(8,128)(2,1)}), bf16[512,6,128]{2,1,0:T(8,128)(2,1)S(1)}, u32[]{:S(2)}, u32[]{:S(2)}) async-start(bf16[512,6,128]{2,1,0:T(8,128)(2,1)} %copy.27), calls=%async_computation.4 | async-start | bytes 2097152 | tf_op jit(solution)/shard_map/all_to_all | solution.py:80
  117.0 79.7 %all-reduce.3.cloned.1.call-start = ((), (), s32[]{:S(2)}) async-start(), calls=%async_computation.5 | async-start | bytes 786432
  198.8 21.5 %all-to-all-start.2 = ((f32[12,1,8,256]{3,2,1,0:T(8,128)}), f32[12,1,8,256]{3,2,1,0:T(8,128)S(1)}, u32[]{:S(2)}, u32[]{:S(2)}) async-start(f32[12,1,8,256]{3,2,1,0:T(8,128)} %constant_dynamic-slice_fusion), calls=%async_computation.2 | async-start | bytes 196608 | tf_op jit(solution)/shard_map/all_to_all | solution.py:62
  221.2 25.8 %collective-permute-start = (bf16[128,3072]{1,0:T(8,128)(2,1)S(1)}, bf16[128,3072]{1,0:T(8,128)(2,1)S(1)}, u32[]{:S(2)}, u32[]{:S(2)}) collective-permute-start(bf16[128,3072]{1,0:T(8,128)(2,1)S(1)} %fusion.3), channel_id=1, source_target_pairs={{576,0},{0,192},{192,384},{384,576},{577,1},{1,193},{193,385},{385... | collective-permute-start | bytes 2359304 | tf_op jit(solution)/shard_map/ppermute | solution.py:14
Sparse Core Ops, SparseCore 0:
  143.0 53.6 all-reduce.2

commit v2 on v1

v2 whole, which is shorter than its diff:
```python
import math

import jax
import jax.numpy as jnp
from jax import lax
from jax.sharding import Mesh, PartitionSpec as P

masked_score = -1e30


def from_behind(block, axis, distance):
    devices = range(lax.axis_size(axis))
    route = [((i - distance) % len(devices), i) for i in devices]
    return lax.ppermute(block, axis, route)


def neighbour_keys(kv, axis):
    count = lax.axis_size(axis)
    from_left = lax.ppermute(kv, axis, [(i, i + 1) for i in range(count - 1)])
    from_right = lax.ppermute(kv, axis, [(i + 1, i) for i in range(count - 1)])
    return jnp.concatenate([from_left, kv, from_right], axis=0)


def attend_chunk(local, segment_row, axis):
    rows = local.shape[0]
    chunk = lax.axis_index(axis)
    total_rows = segment_row.shape[0]
    query_rows = local[:, 0]
    keys = neighbour_keys(local[:, 1:3], axis)
    key_rows = keys[:, 0]
    values = keys[:, 1]
    scale_factor = 1.0 / math.sqrt(query_rows.shape[2])
    query_seg = lax.dynamic_slice_in_dim(segment_row, chunk * rows, rows, 0)
    key_pos = (chunk - 1) * rows + jnp.arange(3 * rows, dtype=jnp.int32)
    key_valid = (key_pos >= 0) & (key_pos < total_rows)
    key_seg = jnp.take(segment_row, jnp.clip(key_pos, 0, total_rows - 1), axis=0)
    same_segment = (query_seg[:, None] == key_seg[None, :]) & key_valid[None, :]
    scores = (
        jnp.einsum("qhd,khd->hqk", query_rows, key_rows, preferred_element_type=jnp.float32)
        * scale_factor
    )
    scores = jnp.where(same_segment[None], scores, masked_score)
    row_max = jnp.max(scores, axis=2, keepdims=True)
    weights = jnp.exp(scores - row_max)
    row_total = jnp.sum(weights, axis=2, keepdims=True)
    rounded = weights.astype(jnp.bfloat16)
    mixed_out = jnp.einsum("hqk,khd->qhd", rounded, values, preferred_element_type=jnp.float32)
    mixed_out = mixed_out / jnp.transpose(row_total, (1, 0, 2))
    return mixed_out.astype(jnp.bfloat16), query_seg


def sample_gates(cond, rows_weight):
    dp = ("dx", "dz")
    seg_count, model_width = cond.shape
    row_count = rows_weight.shape[0]
    nx = lax.axis_size("dx")
    nz = lax.axis_size("dz")
    col_block = model_width // nz
    feat_block = model_width // nx
    cond_act = jax.nn.silu(cond.astype(jnp.float32)).astype(jnp.bfloat16)
    w_cols = lax.all_to_all(
        rows_weight.reshape(row_count, nz, col_block), "dz", split_axis=1, concat_axis=0, tiled=True
    ).reshape(nz * row_count, col_block)
    sent = jnp.transpose(cond_act.reshape(seg_count, nx, feat_block), (1, 0, 2))
    sent = jnp.broadcast_to(sent[:, None], (nx, nz, seg_count, feat_block))
    feat = lax.all_to_all(
        sent.reshape(nx * nz, seg_count, feat_block), dp, split_axis=0, concat_axis=0, tiled=True
    ).reshape(nx * nz * seg_count, feat_block)
    partial = jnp.dot(feat, w_cols, preferred_element_type=jnp.float32)
    parts = lax.all_to_all(
        partial.reshape(nx * nz, seg_count, col_block), dp, split_axis=0, concat_axis=0, tiled=True
    ).reshape(nx, nz, seg_count, col_block)
    summed = jnp.sum(parts, axis=0)
    return jnp.transpose(summed, (1, 0, 2)).reshape(seg_count, model_width)


def shards(projected, seg_ids, condition, w_gate):
    tok_rows = projected.shape[2]
    head_count = projected.shape[4]
    head_size = projected.shape[5]
    model_width = head_count * head_size
    segment_row = seg_ids.reshape(-1)
    attended, local_segments = attend_chunk(projected[0, 0], segment_row, "sp")
    merged = attended.reshape(tok_rows, model_width)
    seg_gate = sample_gates(condition[0], w_gate[0])
    seg_count = seg_gate.shape[0]
    one_hot = (local_segments[:, None] == jnp.arange(seg_count, dtype=jnp.int32)[None, :]).astype(
        jnp.float32
    )
    token_gate = jnp.dot(one_hot, seg_gate, precision=lax.Precision.HIGHEST)
    gated_out = (token_gate * merged.astype(jnp.float32)).astype(jnp.bfloat16)
    handed = from_behind(gated_out, "section", 1)
    return handed.reshape(1, 1, tok_rows, model_width)


def solution(mesh):
    n_section, n_dp, n_sp = (mesh.shape[a] for a in ("section", "dp", "sp"))
    n_x = 4 if n_dp % 4 == 0 else 1
    split_mesh = Mesh(
        mesh.devices.reshape(n_section, n_x, n_dp // n_x, n_sp), ("section", "dx", "dz", "sp")
    )
    dp = ("dx", "dz")
    placed = (
        P("section", dp, "sp", None, None, None),
        P("section", dp, None),
        P("section", dp, None),
        P("section", dp, None),
    )
    return jax.shard_map(
        shards,
        mesh=split_mesh,
        in_specs=placed,
        out_specs=P("section", dp, "sp", None),
        check_vma=False,
    )
```

time: 255 us -> 132 us (0.52)
  the two profiles are of different devices: /device:TPU:16 before, /device:TPU:6 now
where the time goes in v2:
time: 132 us; the launch traced here: 131 us
  waiting for transfers between devices  63.4 us (48%)
  starting transfers between devices  42 us (32%)
  local copies, waits for them, and re-layouts  14.1 us (11%)
  matrix products  7.66 us (6%)
  other arithmetic  4.07 us (3%)
    ppermute x1, waiting for transfers between devices, from_behind(): return lax.ppermute(block, axis, route)  23.9 us
    all_to_all x1, starting transfers between devices, sample_gates(): lax.all_to_all(rows_weight.reshape(row_count, nz, col_block), 'dz', split...  15.2 us
    all_to_all x1, waiting for transfers between devices, sample_gates(): lax.all_to_all(partial.reshape(nx * nz, seg_count, col_block), dp, split_...  13.4 us
    all_to_all x1, starting transfers between devices, sample_gates(): lax.all_to_all(partial.reshape(nx * nz, seg_count, col_block), dp, split_...  12.2 us
    all_to_all x1, waiting for transfers between devices, sample_gates(): lax.all_to_all(rows_weight.reshape(row_count, nz, col_block), 'dz', split...  10.2 us
    ppermute x1, waiting for transfers between devices, neighbour_keys(): from_left = lax.ppermute(kv, axis, [(i, i + 1) for i in range(count - 1)])  10.2 us
    all_to_all x1, starting transfers between devices, sample_gates(): lax.all_to_all(sent.reshape(nx * nz, seg_count, feat_block), dp, split_ax...  6.83 us
    unnamed x10, local copies, waits for them, and re-layouts  6.53 us
  transfers between devices with their start and end apart: 6, of which 6 were waited for; matrix products, arithmetic and copies ran while one was open for 13% of the time, Pallas kernels for 0%

profile of v2, /device:TPU:6, one launch (start us, length us, event | category | flops | bytes accessed | tf_op | source)
XLA Modules:
  0.0 131.5 jit_solution(7380605932874560899)
XLA Ops:
  0.0 0.0 copy-start
  0.0 1.3 reshape_squeeze.3
  1.3 0.0 copy-start.3
  1.3 0.9 copy.15
  2.2 15.2 %all-to-all-start.1 = ((bf16[64,12,256]{2,0,1:T(8,128)(2,1)}), bf16[64,12,256]{2,0,1:T(8,128)(2,1)S(1)}, u32[]{:S(2)}, u32[]{:S(2)}) async-start(bf16[64,12,256]{2,0,1:T(8,128)(2,1)} %copy.15), calls=%async_computation.1 | async-start | bytes 786432 | tf_op jit(solution)/shard_map/all_to_all | solution.py:61
  17.3 2.3 %copy.24 = bf16[1,1,128,3,24,128]{5,2,4,3,1,0:T(8,128)(2,1)S(1)} copy(bf16[1,1,128,3,24,128]{5,4,3,2,1,0:T(8,128)(2,1)} %param.4) | data formatting | bytes 4718592 | tf_op args[0]
  19.6 1.3 slice.18
  20.9 4.6 %collective-permute-start = (bf16[128,2,24,128]{3,0,2,1:T(8,128)(2,1)}, bf16[128,2,24,128]{3,0,2,1:T(8,128)(2,1)}, u32[]{:S(2)}, u32[]{:S(2)}) collective-permute-start(bf16[128,2,24,128]{3,0,2,1:T(8,128)(2,1)} %slice.18), channel_id=1, source_target_pairs={{0,1},{1,2},{2,3},{4,5},{5,6},{6,7},{8,9},{9,10},{10,11},{12,13},{... | collective-permute-start | bytes 4718600 | tf_op jit(solution)/shard_map/ppermute | solution.py:19
  25.5 1.3 collective-permute-start.1
  26.8 0.0 copy-done.3
  26.9 10.2 %all-to-all-done.1 = bf16[64,12,256]{2,0,1:T(8,128)(2,1)S(1)} async-done(((bf16[64,12,256]{2,0,1:T(8,128)(2,1)}), bf16[64,12,256]{2,0,1:T(8,128)(2,1)S(1)}, u32[]{:S(2)}, u32[]{:S(2)}) %all-to-all-start.1) | async-done | bytes 393248 | tf_op jit(solution)/shard_map/all_to_all | solution.py:61
  37.1 0.9 broadcast_in_dim.22
  38.0 6.8 %all-to-all-start = ((bf16[48,8,768]{2,1,0:T(8,128)(2,1)}), bf16[48,8,768]{2,1,0:T(8,128)(2,1)S(1)}, u32[]{:S(2)}, u32[]{:S(2)}) async-start(bf16[48,8,768]{2,1,0:T(8,128)(2,1)} %bitcast.4), calls=%async_computation | async-start | bytes 1179648 | tf_op jit(solution)/shard_map/all_to_all | solution.py:66
  44.8 0.0 copy-done
  44.8 2.8 %gather_fusion = s32[384]{0:T(512)S(1)} fusion(s32[512]{0:T(512)S(1)} %bitcast.64, s32[1024]{0:T(1024)S(1)} %pad_clamp_fusion), kind=kCustom, calls=%fused_computation | custom fusion | bytes 4608 | tf_op jit(solution)/shard_map/jit(_take)/gather | solution.py:36
  47.7 0.2 compare_and_fusion
  47.8 10.2 %collective-permute-done = bf16[128,2,24,128]{3,0,2,1:T(8,128)(2,1)} collective-permute-done((bf16[128,2,24,128]{3,0,2,1:T(8,128)(2,1)}, bf16[128,2,24,128]{3,0,2,1:T(8,128)(2,1)}, u32[]{:S(2)}, u32[]{:S(2)}) %collective-permute-start) | collective-permute-done | bytes 1572896 | tf_op jit(solution)/shard_map/ppermute | solution.py:19
  58.0 5.3 %collective-permute-done.1 = bf16[128,2,24,128]{3,0,2,1:T(8,128)(2,1)} collective-permute-done((bf16[128,2,24,128]{3,0,2,1:T(8,128)(2,1)}, bf16[128,2,24,128]{3,0,2,1:T(8,128)(2,1)}, u32[]{:S(2)}, u32[]{:S(2)}) %collective-permute-start.1) | collective-permute-done | bytes 1572896 | tf_op jit(solution)/shard_map/ppermute | solution.py:20
  63.3 2.6 %pad_maximum_fusion = bf16[384,2,24,128]{3,0,2,1:T(8,128)(2,1)S(1)} fusion(bf16[128,2,24,128]{3,0,2,1:T(8,128)(2,1)} %collective-permute-done.1, bf16[128,2,24,128]{3,0,2,1:T(8,128)(2,1)} %slice.18, bf16[128,2,24,128]{3,0,2,1:T(8,128)(2,1)} %collective-permute-done), kind=kLoop, calls=%fused_computation.1 | loop fusion | flops 14155776 | bytes 9437184 | tf_op jit(solution)/shard_map/concatenate | solution.py:21
  65.9 0.0 copy-start.1
  65.9 0.9 fusion.3
  66.8 1.3 copy-done.1
  68.1 0.0 copy-start.2
  68.1 2.1 %copy-done.2 = f32[24,384,128]{2,1,0:T(8,128)} copy-done((f32[24,384,128]{2,1,0:T(8,128)}, f32[24,384,128]{2,1,0:T(8,128)S(1)}, u32[]{:S(2)}) %copy-start.2) | copy-done | bytes 4718616
  70.2 1.0 fusion
  71.2 0.5 all-to-all-done
  71.7 1.1 fusion.26
  72.8 12.2 %all-to-all-start.2 = ((f32[48,8,256]{2,1,0:T(8,128)}), f32[48,8,256]{2,1,0:T(8,128)S(1)}, u32[]{:S(2)}, u32[]{:S(2)}) async-start(f32[48,8,256]{2,1,0:T(8,128)} %fusion.26), calls=%async_computation.2 | async-start | bytes 786432 | tf_op jit(solution)/shard_map/all_to_all | solution.py:70
  85.0 4.8 %fusion.11 = bf16[128,24,128]{0,2,1:T(8,128)(2,1)S(1)} fusion(f32[128,24]{0,1:T(8,128)S(1)} %bitcast.72, f32[24,384,128]{2,1,0:T(8,128)} %copy-done.2, f32[24,128]{1,0:T(8,128)S(1)} %get-tuple-element.5, pred[128,384]{0,1:T(8,128)(4,1)S(1)} %compare_and_fusion, bf16[384,2,24,128]{3,0,2,1:T(8,128)(2,1)} %copy-done.1), kind=kOutput, calls=%fused_computation.19 | convolution fusion | flops 307494912 | bytes 7938048 | tf_op jit(solution)/shard_map/hqk,khd->qhd/dot_general | solution.py:47
  89.8 0.2 bitcast_convert_fusion
  90.0 0.5 copy.22
  90.5 13.4 %all-to-all-done.2 = f32[48,8,256]{2,1,0:T(8,128)S(1)} async-done(((f32[48,8,256]{2,1,0:T(8,128)}), f32[48,8,256]{2,1,0:T(8,128)S(1)}, u32[]{:S(2)}, u32[]{:S(2)}) %all-to-all-start.2) | async-done | bytes 393248 | tf_op jit(solution)/shard_map/all_to_all | solution.py:70
  103.9 0.9 fusion.2
  104.8 1.9 %collective-permute-start.2 = (bf16[128,3072]{1,0:T(8,128)(2,1)S(1)}, bf16[128,3072]{1,0:T(8,128)(2,1)S(1)}, u32[]{:S(2)}, u32[]{:S(2)}) collective-permute-start(bf16[128,3072]{1,0:T(8,128)(2,1)S(1)} %fusion.2), channel_id=1, source_target_pairs={{576,0},{0,192},{192,384},{384,576},{577,1},{1,193},{193,385},{385... | collective-permute-start | bytes 2359304 | tf_op jit(solution)/shard_map/ppermute | solution.py:14
  106.7 23.9 %collective-permute-done.2 = bf16[128,3072]{1,0:T(8,128)(2,1)S(1)} collective-permute-done((bf16[128,3072]{1,0:T(8,128)(2,1)S(1)}, bf16[128,3072]{1,0:T(8,128)(2,1)S(1)}, u32[]{:S(2)}, u32[]{:S(2)}) %collective-permute-start.2) | collective-permute-done | bytes 786464 | tf_op jit(solution)/shard_map/ppermute | solution.py:14
  130.6 0.9 copy.26
  (7 shorter events, 0.1 us)
Async XLA Ops:
  0.0 44.8 %copy-start = (s32[1,1,512]{2,1,0:T(1,128)S(1)}, s32[1,1,512]{2,1,0:T(1,128)}, u32[]{:S(2)}) copy-start(s32[1,1,512]{2,1,0:T(1,128)} %param.5) | copy-start | bytes 6148
  1.3 25.5 %copy-start.3 = (bf16[1,8,3072]{2,1,0:T(8,128)(2,1)S(1)}, bf16[1,8,3072]{2,1,0:T(8,128)(2,1)}, u32[]{:S(2)}) copy-start(bf16[1,8,3072]{2,1,0:T(8,128)(2,1)} %param.6) | copy-start | bytes 147460
  2.2 34.9 %all-to-all-start.1 = ((bf16[64,12,256]{2,0,1:T(8,128)(2,1)}), bf16[64,12,256]{2,0,1:T(8,128)(2,1)S(1)}, u32[]{:S(2)}, u32[]{:S(2)}) async-start(bf16[64,12,256]{2,0,1:T(8,128)(2,1)} %copy.15), calls=%async_computation.1 | async-start | bytes 786432 | tf_op jit(solution)/shard_map/all_to_all | solution.py:61
  20.9 37.1 %collective-permute-start = (bf16[128,2,24,128]{3,0,2,1:T(8,128)(2,1)}, bf16[128,2,24,128]{3,0,2,1:T(8,128)(2,1)}, u32[]{:S(2)}, u32[]{:S(2)}) collective-permute-start(bf16[128,2,24,128]{3,0,2,1:T(8,128)(2,1)} %slice.18), channel_id=1, source_target_pairs={{0,1},{1,2},{2,3},{4,5},{5,6},{6,7},{8,9},{9,10},{10,11},{12,13},{... | collective-permute-start | bytes 4718600 | tf_op jit(solution)/shard_map/ppermute | solution.py:19
  25.5 37.8 %collective-permute-start.1 = (bf16[128,2,24,128]{3,0,2,1:T(8,128)(2,1)}, bf16[128,2,24,128]{3,0,2,1:T(8,128)(2,1)}, u32[]{:S(2)}, u32[]{:S(2)}) collective-permute-start(bf16[128,2,24,128]{3,0,2,1:T(8,128)(2,1)} %slice.18), channel_id=1, source_target_pairs={{1,0},{2,1},{3,2},{5,4},{6,5},{7,6},{9,8},{10,9},{11,10},{13,12},{... | collective-permute-start | bytes 4718600 | tf_op jit(solution)/shard_map/ppermute | solution.py:20
  38.0 33.8 %all-to-all-start = ((bf16[48,8,768]{2,1,0:T(8,128)(2,1)}), bf16[48,8,768]{2,1,0:T(8,128)(2,1)S(1)}, u32[]{:S(2)}, u32[]{:S(2)}) async-start(bf16[48,8,768]{2,1,0:T(8,128)(2,1)} %bitcast.4), calls=%async_computation | async-start | bytes 1179648 | tf_op jit(solution)/shard_map/all_to_all | solution.py:66
  65.9 2.2 %copy-start.1 = (bf16[384,2,24,128]{3,0,2,1:T(8,128)(2,1)}, bf16[384,2,24,128]{3,0,2,1:T(8,128)(2,1)S(1)}, u32[]{:S(2)}) copy-start(bf16[384,2,24,128]{3,0,2,1:T(8,128)(2,1)S(1)} %pad_maximum_fusion) | copy-start | bytes 14155780
  68.1 2.1 %copy-start.2 = (f32[24,384,128]{2,1,0:T(8,128)}, f32[24,384,128]{2,1,0:T(8,128)S(1)}, u32[]{:S(2)}) copy-start(f32[24,384,128]{2,1,0:T(8,128)S(1)} %get-tuple-element.6) | copy-start | bytes 14155780
  72.8 31.1 %all-to-all-start.2 = ((f32[48,8,256]{2,1,0:T(8,128)}), f32[48,8,256]{2,1,0:T(8,128)S(1)}, u32[]{:S(2)}, u32[]{:S(2)}) async-start(f32[48,8,256]{2,1,0:T(8,128)} %fusion.26), calls=%async_computation.2 | async-start | bytes 786432 | tf_op jit(solution)/shard_map/all_to_all | solution.py:70
  104.8 25.8 %collective-permute-start.2 = (bf16[128,3072]{1,0:T(8,128)(2,1)S(1)}, bf16[128,3072]{1,0:T(8,128)(2,1)S(1)}, u32[]{:S(2)}, u32[]{:S(2)}) collective-permute-start(bf16[128,3072]{1,0:T(8,128)(2,1)S(1)} %fusion.2), channel_id=1, source_target_pairs={{576,0},{0,192},{192,384},{384,576},{577,1},{1,193},{193,385},{385... | collective-permute-start | bytes 2359304 | tf_op jit(solution)/shard_map/ppermute | solution.py:14

commit v3 on v2

--- a/solution.py
+++ b/solution.py
@@ -82,14 +82,15 @@
     segment_row = seg_ids.reshape(-1)
     attended, local_segments = attend_chunk(projected[0, 0], segment_row, "sp")
     merged = attended.reshape(tok_rows, model_width)
-    seg_gate = sample_gates(condition[0], w_gate[0])
+    merged = from_behind(merged, "section", 1)
+    local_segments = from_behind(local_segments, "section", 1)
+    seg_gate = from_behind(sample_gates(condition[0], w_gate[0]), "section", 1)
     seg_count = seg_gate.shape[0]
     one_hot = (local_segments[:, None] == jnp.arange(seg_count, dtype=jnp.int32)[None, :]).astype(
         jnp.float32
     )
     token_gate = jnp.dot(one_hot, seg_gate, precision=lax.Precision.HIGHEST)
-    gated_out = (token_gate * merged.astype(jnp.float32)).astype(jnp.bfloat16)
-    handed = from_behind(gated_out, "section", 1)
+    handed = (token_gate * merged.astype(jnp.float32)).astype(jnp.bfloat16)
     return handed.reshape(1, 1, tok_rows, model_width)
 
 

time: 132 us -> 120 us (0.909)
  waiting for transfers between devices: 63.4 us -> 43.4 us
  starting transfers between devices: 42 us -> 50.8 us
    ppermute x1 -> x3, waiting for transfers between devices: 23.9 us -> 5.37 us  [from_behind(): return lax.ppermute(block, axis, route)]
    ppermute x1 -> x3, starting transfers between devices: 1.92 us -> 10.8 us  [from_behind(): return lax.ppermute(block, axis, route)]
    all_to_all x1, waiting for transfers between devices: 13.4 us -> 11.8 us  [sample_gates(): lax.all_to_all(partial.reshape(nx * nz, seg_count, col_block), dp, split_...]
    unnamed x10 -> x9, local copies, waits for them, and re-layouts: 6.53 us -> 5.65 us
  transfers between devices with their start and end apart: 6 -> 8, of which waited for: 6 -> 6; matrix products, arithmetic and copies ran while one was open for 13% -> 14% of each run, Pallas kernels for 0% -> 0%
where the time goes in v3:
time: 120 us
  starting transfers between devices  50.8 us (42%)
  waiting for transfers between devices  43.4 us (36%)
  local copies, waits for them, and re-layouts  13 us (11%)
  matrix products  8.52 us (7%)
  other arithmetic  3.91 us (3%)
    all_to_all x1, starting transfers between devices, sample_gates(): lax.all_to_all(rows_weight.reshape(row_count, nz, col_block), 'dz', split...  15.2 us
    all_to_all x1, starting transfers between devices, sample_gates(): lax.all_to_all(partial.reshape(nx * nz, seg_count, col_block), dp, split_...  12.2 us
    all_to_all x1, waiting for transfers between devices, sample_gates(): lax.all_to_all(partial.reshape(nx * nz, seg_count, col_block), dp, split_...  11.8 us
    ppermute x3, starting transfers between devices, from_behind(): return lax.ppermute(block, axis, route)  10.8 us
    all_to_all x1, waiting for transfers between devices, sample_gates(): lax.all_to_all(rows_weight.reshape(row_count, nz, col_block), 'dz', split...  10.2 us
    ppermute x1, waiting for transfers between devices, neighbour_keys(): from_left = lax.ppermute(kv, axis, [(i, i + 1) for i in range(count - 1)])  10.2 us
    all_to_all x1, starting transfers between devices, sample_gates(): lax.all_to_all(sent.reshape(nx * nz, seg_count, feat_block), dp, split_ax...  6.83 us
    unnamed x9, local copies, waits for them, and re-layouts  5.65 us
  transfers between devices with their start and end apart: 8, of which 6 were waited for; matrix products, arithmetic and copies ran while one was open for 14% of the time, Pallas kernels for 0%

profile of v3, /device:TPU:6, one launch (start us, length us, event | category | flops | bytes accessed | tf_op | source)
XLA Modules:
  0.0 119.9 jit_solution(15958242583098894737)
XLA Ops:
  0.0 0.0 copy-start
  0.0 1.3 %reshape_squeeze.3 = bf16[64,12,256]{2,1,0:T(8,128)(2,1)S(1)} reshape(bf16[1,64,3072]{2,1,0:T(8,128)(2,1)} %param.7) | data formatting | bytes 786432 | tf_op jit(solution)/shard_map/reshape;squeeze | solution.py:62
  1.3 0.0 copy-start.3
  1.3 0.9 copy.15
  2.2 15.2 %all-to-all-start.1 = ((bf16[64,12,256]{2,0,1:T(8,128)(2,1)}), bf16[64,12,256]{2,0,1:T(8,128)(2,1)S(1)}, u32[]{:S(2)}, u32[]{:S(2)}) async-start(bf16[64,12,256]{2,0,1:T(8,128)(2,1)} %copy.15), calls=%async_computation.1 | async-start | bytes 786432 | tf_op jit(solution)/shard_map/all_to_all | solution.py:61
  17.3 2.3 %copy.24 = bf16[1,1,128,3,24,128]{5,2,4,3,1,0:T(8,128)(2,1)S(1)} copy(bf16[1,1,128,3,24,128]{5,4,3,2,1,0:T(8,128)(2,1)} %param.4) | data formatting | bytes 4718592 | tf_op args[0]
  19.6 1.3 %slice.18 = bf16[128,2,24,128]{3,0,2,1:T(8,128)(2,1)} slice(bf16[128,3,24,128]{3,0,2,1:T(8,128)(2,1)S(1)} %bitcast.64), slice={[0:128], [1:3], [0:24], [0:128]} | slice | bytes 3145728 | tf_op jit(solution)/shard_map/slice | solution.py:29
  20.9 4.6 %collective-permute-start.2 = (bf16[128,2,24,128]{3,0,2,1:T(8,128)(2,1)}, bf16[128,2,24,128]{3,0,2,1:T(8,128)(2,1)}, u32[]{:S(2)}, u32[]{:S(2)}) collective-permute-start(bf16[128,2,24,128]{3,0,2,1:T(8,128)(2,1)} %slice.18), channel_id=1, source_target_pairs={{0,1},{1,2},{2,3},{4,5},{5,6},{6,7},{8,9},{9,10},{10,11},{12,13},{... | collective-permute-start | bytes 4718600 | tf_op jit(solution)/shard_map/ppermute | solution.py:19
  25.5 1.3 %collective-permute-start.3 = (bf16[128,2,24,128]{3,0,2,1:T(8,128)(2,1)}, bf16[128,2,24,128]{3,0,2,1:T(8,128)(2,1)}, u32[]{:S(2)}, u32[]{:S(2)}) collective-permute-start(bf16[128,2,24,128]{3,0,2,1:T(8,128)(2,1)} %slice.18), channel_id=1, source_target_pairs={{1,0},{2,1},{3,2},{5,4},{6,5},{7,6},{9,8},{10,9},{11,10},{13,12},{... | collective-permute-start | bytes 4718600 | tf_op jit(solution)/shard_map/ppermute | solution.py:20
  26.8 0.0 copy-done.3
  26.9 10.2 %all-to-all-done.1 = bf16[64,12,256]{2,0,1:T(8,128)(2,1)S(1)} async-done(((bf16[64,12,256]{2,0,1:T(8,128)(2,1)}), bf16[64,12,256]{2,0,1:T(8,128)(2,1)S(1)}, u32[]{:S(2)}, u32[]{:S(2)}) %all-to-all-start.1) | async-done | bytes 393248 | tf_op jit(solution)/shard_map/all_to_all | solution.py:61
  37.1 0.9 broadcast_in_dim.22
  38.0 6.8 %all-to-all-start = ((bf16[48,8,768]{2,1,0:T(8,128)(2,1)}), bf16[48,8,768]{2,1,0:T(8,128)(2,1)S(1)}, u32[]{:S(2)}, u32[]{:S(2)}) async-start(bf16[48,8,768]{2,1,0:T(8,128)(2,1)} %bitcast.4), calls=%async_computation | async-start | bytes 1179648 | tf_op jit(solution)/shard_map/all_to_all | solution.py:66
  44.8 0.0 copy-done
  44.8 2.8 %gather_fusion = s32[384]{0:T(512)S(1)} fusion(s32[512]{0:T(512)S(1)} %bitcast.63, s32[1024]{0:T(1024)S(1)} %pad_clamp_fusion), kind=kCustom, calls=%fused_computation | custom fusion | bytes 4608 | tf_op jit(solution)/shard_map/jit(_take)/gather | solution.py:36
  47.7 0.2 compare_and_fusion
  47.8 10.2 %collective-permute-done.2 = bf16[128,2,24,128]{3,0,2,1:T(8,128)(2,1)} collective-permute-done((bf16[128,2,24,128]{3,0,2,1:T(8,128)(2,1)}, bf16[128,2,24,128]{3,0,2,1:T(8,128)(2,1)}, u32[]{:S(2)}, u32[]{:S(2)}) %collective-permute-start.2) | collective-permute-done | bytes 1572896 | tf_op jit(solution)/shard_map/ppermute | solution.py:19
  58.0 5.2 %collective-permute-done.3 = bf16[128,2,24,128]{3,0,2,1:T(8,128)(2,1)} collective-permute-done((bf16[128,2,24,128]{3,0,2,1:T(8,128)(2,1)}, bf16[128,2,24,128]{3,0,2,1:T(8,128)(2,1)}, u32[]{:S(2)}, u32[]{:S(2)}) %collective-permute-start.3) | collective-permute-done | bytes 1572896 | tf_op jit(solution)/shard_map/ppermute | solution.py:20
  63.3 2.6 %pad_maximum_fusion = bf16[384,2,24,128]{3,0,2,1:T(8,128)(2,1)S(1)} fusion(bf16[128,2,24,128]{3,0,2,1:T(8,128)(2,1)} %collective-permute-done.3, bf16[128,2,24,128]{3,0,2,1:T(8,128)(2,1)} %slice.18, bf16[128,2,24,128]{3,0,2,1:T(8,128)(2,1)} %collective-permute-done.2), kind=kLoop, calls=%fused_computation.1 | loop fusion | flops 14155776 | bytes 9437184 | tf_op jit(solution)/shard_map/concatenate | solution.py:21
  65.9 0.0 copy-start.1
  65.9 0.9 fusion.3
  66.8 1.3 %copy-done.1 = bf16[384,2,24,128]{3,0,2,1:T(8,128)(2,1)} copy-done((bf16[384,2,24,128]{3,0,2,1:T(8,128)(2,1)}, bf16[384,2,24,128]{3,0,2,1:T(8,128)(2,1)S(1)}, u32[]{:S(2)}) %copy-start.1) | copy-done | bytes 4718616
  68.0 0.0 copy-start.2
  68.0 2.1 %copy-done.2 = f32[24,384,128]{2,1,0:T(8,128)} copy-done((f32[24,384,128]{2,1,0:T(8,128)}, f32[24,384,128]{2,1,0:T(8,128)S(1)}, u32[]{:S(2)}) %copy-start.2) | copy-done | bytes 4718616
  70.2 1.0 fusion
  71.2 0.6 all-to-all-done
  71.7 1.1 fusion.27
  72.8 12.2 %all-to-all-start.2 = ((f32[48,8,256]{2,1,0:T(8,128)}), f32[48,8,256]{2,1,0:T(8,128)S(1)}, u32[]{:S(2)}, u32[]{:S(2)}) async-start(f32[48,8,256]{2,1,0:T(8,128)} %fusion.27), calls=%async_computation.2 | async-start | bytes 786432 | tf_op jit(solution)/shard_map/all_to_all | solution.py:70
  85.0 4.8 %fusion.12 = bf16[128,24,128]{0,2,1:T(8,128)(2,1)S(1)} fusion(f32[128,24]{0,1:T(8,128)S(1)} %bitcast.71, f32[24,384,128]{2,1,0:T(8,128)} %copy-done.2, f32[24,128]{1,0:T(8,128)S(1)} %get-tuple-element.5, pred[128,384]{0,1:T(8,128)(4,1)S(1)} %compare_and_fusion, bf16[384,2,24,128]{3,0,2,1:T(8,128)(2,1)} %copy-done.1), kind=kOutput, calls=%fused_computation.20 | convolution fusion | flops 307494912 | bytes 7938048 | tf_op jit(solution)/shard_map/hqk,khd->qhd/dot_general | solution.py:47
  89.8 0.3 copy.22
  90.1 1.9 %collective-permute-start.4 = (bf16[128,3072]{1,0:T(8,128)(2,1)S(1)}, bf16[128,3072]{1,0:T(8,128)(2,1)S(1)}, u32[]{:S(2)}, u32[]{:S(2)}) collective-permute-start(bf16[128,3072]{1,0:T(8,128)(2,1)S(1)} %copy.22), channel_id=1, source_target_pairs={{576,0},{0,192},{192,384},{384,576},{577,1},{1,193},{193,385},{385... | collective-permute-start | bytes 2359304 | tf_op jit(solution)/shard_map/ppermute | solution.py:14
  92.1 11.8 %all-to-all-done.2 = f32[48,8,256]{2,1,0:T(8,128)S(1)} async-done(((f32[48,8,256]{2,1,0:T(8,128)}), f32[48,8,256]{2,1,0:T(8,128)S(1)}, u32[]{:S(2)}, u32[]{:S(2)}) %all-to-all-start.2) | async-done | bytes 393248 | tf_op jit(solution)/shard_map/all_to_all | solution.py:70
  103.9 1.9 %collective-permute-start.1 = (f32[8,3072]{1,0:T(8,128)S(1)}, f32[8,3072]{1,0:T(8,128)S(1)}, u32[]{:S(2)}, u32[]{:S(2)}) collective-permute-start(f32[8,3072]{1,0:T(8,128)S(1)} %bitcast.69), channel_id=1, source_target_pairs={{576,0},{0,192},{192,384},{384,576},{577,1},{1,193},{193,385},{385... | collective-permute-start | bytes 294920 | tf_op jit(solution)/shard_map/ppermute | solution.py:14
  105.8 6.9 %collective-permute-start = (s32[128]{0:T(128)S(1)}, s32[128]{0:T(128)S(1)}, u32[]{:S(2)}, u32[]{:S(2)}) collective-permute-start(s32[128]{0:T(128)S(1)} %dynamic-slice_bitcast_fusion), channel_id=1, source_target_pairs={{576,0},{0,192},{192,384},{384,576},{577,1},{1,193},{193,385},{385... | collective-permute-start | bytes 1544 | tf_op jit(solution)/shard_map/ppermute | solution.py:14
  112.8 5.4 %collective-permute-done = s32[128]{0:T(128)S(1)} collective-permute-done((s32[128]{0:T(128)S(1)}, s32[128]{0:T(128)S(1)}, u32[]{:S(2)}, u32[]{:S(2)}) %collective-permute-start) | collective-permute-done | bytes 544 | tf_op jit(solution)/shard_map/ppermute | solution.py:14
  118.1 0.0 collective-permute-done.4
  118.1 0.0 collective-permute-done.1
  118.1 1.7 %fusion.4 = bf16[1,1,128,3072]{3,2,1,0:T(8,128)(2,1)} fusion(f32[8,3072]{1,0:T(8,128)S(1)} %collective-permute-done.1, bf16[128,3072]{1,0:T(8,128)(2,1)S(1)} %collective-permute-done.4, s32[128]{0:T(128)S(1)} %collective-permute-done), kind=kOutput, calls=%fused_computation.9 | convolution fusion | flops 38929408 | bytes 1671680 | tf_op jit(solution)/shard_map/dot_general | solution.py:92
  (7 shorter events, 0.1 us)
Async XLA Ops:
  0.0 44.8 %copy-start = (s32[1,1,512]{2,1,0:T(1,128)S(1)}, s32[1,1,512]{2,1,0:T(1,128)}, u32[]{:S(2)}) copy-start(s32[1,1,512]{2,1,0:T(1,128)} %param.5) | copy-start | bytes 6148
  1.3 25.5 %copy-start.3 = (bf16[1,8,3072]{2,1,0:T(8,128)(2,1)S(1)}, bf16[1,8,3072]{2,1,0:T(8,128)(2,1)}, u32[]{:S(2)}) copy-start(bf16[1,8,3072]{2,1,0:T(8,128)(2,1)} %param.6) | copy-start | bytes 147460
  2.2 34.9 %all-to-all-start.1 = ((bf16[64,12,256]{2,0,1:T(8,128)(2,1)}), bf16[64,12,256]{2,0,1:T(8,128)(2,1)S(1)}, u32[]{:S(2)}, u32[]{:S(2)}) async-start(bf16[64,12,256]{2,0,1:T(8,128)(2,1)} %copy.15), calls=%async_computation.1 | async-start | bytes 786432 | tf_op jit(solution)/shard_map/all_to_all | solution.py:61
  20.9 37.1 %collective-permute-start.2 = (bf16[128,2,24,128]{3,0,2,1:T(8,128)(2,1)}, bf16[128,2,24,128]{3,0,2,1:T(8,128)(2,1)}, u32[]{:S(2)}, u32[]{:S(2)}) collective-permute-start(bf16[128,2,24,128]{3,0,2,1:T(8,128)(2,1)} %slice.18), channel_id=1, source_target_pairs={{0,1},{1,2},{2,3},{4,5},{5,6},{6,7},{8,9},{9,10},{10,11},{12,13},{... | collective-permute-start | bytes 4718600 | tf_op jit(solution)/shard_map/ppermute | solution.py:19
  25.5 37.8 %collective-permute-start.3 = (bf16[128,2,24,128]{3,0,2,1:T(8,128)(2,1)}, bf16[128,2,24,128]{3,0,2,1:T(8,128)(2,1)}, u32[]{:S(2)}, u32[]{:S(2)}) collective-permute-start(bf16[128,2,24,128]{3,0,2,1:T(8,128)(2,1)} %slice.18), channel_id=1, source_target_pairs={{1,0},{2,1},{3,2},{5,4},{6,5},{7,6},{9,8},{10,9},{11,10},{13,12},{... | collective-permute-start | bytes 4718600 | tf_op jit(solution)/shard_map/ppermute | solution.py:20
  38.0 33.8 %all-to-all-start = ((bf16[48,8,768]{2,1,0:T(8,128)(2,1)}), bf16[48,8,768]{2,1,0:T(8,128)(2,1)S(1)}, u32[]{:S(2)}, u32[]{:S(2)}) async-start(bf16[48,8,768]{2,1,0:T(8,128)(2,1)} %bitcast.4), calls=%async_computation | async-start | bytes 1179648 | tf_op jit(solution)/shard_map/all_to_all | solution.py:66
  65.9 2.2 %copy-start.1 = (bf16[384,2,24,128]{3,0,2,1:T(8,128)(2,1)}, bf16[384,2,24,128]{3,0,2,1:T(8,128)(2,1)S(1)}, u32[]{:S(2)}) copy-start(bf16[384,2,24,128]{3,0,2,1:T(8,128)(2,1)S(1)} %pad_maximum_fusion) | copy-start | bytes 14155780
  68.0 2.1 %copy-start.2 = (f32[24,384,128]{2,1,0:T(8,128)}, f32[24,384,128]{2,1,0:T(8,128)S(1)}, u32[]{:S(2)}) copy-start(f32[24,384,128]{2,1,0:T(8,128)S(1)} %get-tuple-element.6) | copy-start | bytes 14155780
  72.8 31.1 %all-to-all-start.2 = ((f32[48,8,256]{2,1,0:T(8,128)}), f32[48,8,256]{2,1,0:T(8,128)S(1)}, u32[]{:S(2)}, u32[]{:S(2)}) async-start(f32[48,8,256]{2,1,0:T(8,128)} %fusion.27), calls=%async_computation.2 | async-start | bytes 786432 | tf_op jit(solution)/shard_map/all_to_all | solution.py:70
  90.1 28.0 %collective-permute-start.4 = (bf16[128,3072]{1,0:T(8,128)(2,1)S(1)}, bf16[128,3072]{1,0:T(8,128)(2,1)S(1)}, u32[]{:S(2)}, u32[]{:S(2)}) collective-permute-start(bf16[128,3072]{1,0:T(8,128)(2,1)S(1)} %copy.22), channel_id=1, source_target_pairs={{576,0},{0,192},{192,384},{384,576},{577,1},{1,193},{193,385},{385... | collective-permute-start | bytes 2359304 | tf_op jit(solution)/shard_map/ppermute | solution.py:14
  103.9 14.2 %collective-permute-start.1 = (f32[8,3072]{1,0:T(8,128)S(1)}, f32[8,3072]{1,0:T(8,128)S(1)}, u32[]{:S(2)}, u32[]{:S(2)}) collective-permute-start(f32[8,3072]{1,0:T(8,128)S(1)} %bitcast.69), channel_id=1, source_target_pairs={{576,0},{0,192},{192,384},{384,576},{577,1},{1,193},{193,385},{385... | collective-permute-start | bytes 294920 | tf_op jit(solution)/shard_map/ppermute | solution.py:14
  105.8 12.3 %collective-permute-start = (s32[128]{0:T(128)S(1)}, s32[128]{0:T(128)S(1)}, u32[]{:S(2)}, u32[]{:S(2)}) collective-permute-start(s32[128]{0:T(128)S(1)} %dynamic-slice_bitcast_fusion), channel_id=1, source_target_pairs={{576,0},{0,192},{192,384},{384,576},{577,1},{1,193},{193,385},{385... | collective-permute-start | bytes 1544 | tf_op jit(solution)/shard_map/ppermute | solution.py:14

commit v4 on v3

--- a/solution.py
+++ b/solution.py
@@ -4,6 +4,7 @@
 import jax.numpy as jnp
 from jax import lax
 from jax.sharding import Mesh, PartitionSpec as P
+
 
 masked_score = -1e30
 
@@ -25,8 +26,11 @@
     rows = local.shape[0]
     chunk = lax.axis_index(axis)
     total_rows = segment_row.shape[0]
-    query_rows = local[:, 0]
     keys = neighbour_keys(local[:, 1:3], axis)
+    return attend_keys(local[:, 0], keys, segment_row, chunk, rows, total_rows)
+
+
+def attend_keys(query_rows, keys, segment_row, chunk, rows, total_rows):
     key_rows = keys[:, 0]
     values = keys[:, 1]
     scale_factor = 1.0 / math.sqrt(query_rows.shape[2])
@@ -69,12 +73,13 @@
     partial = jnp.dot(feat, w_cols, preferred_element_type=jnp.float32)
     parts = lax.all_to_all(
         partial.reshape(nx * nz, seg_count, col_block), dp, split_axis=0, concat_axis=0, tiled=True
-    ).reshape(nx, nz, seg_count, col_block)
+    )
+    parts = parts.reshape(nx, nz, seg_count, col_block)
     summed = jnp.sum(parts, axis=0)
     return jnp.transpose(summed, (1, 0, 2)).reshape(seg_count, model_width)
 
 
-def shards(projected, seg_ids, condition, w_gate):
+def section_step(projected, seg_ids, condition, w_gate):
     tok_rows = projected.shape[2]
     head_count = projected.shape[4]
     head_size = projected.shape[5]
@@ -82,8 +87,12 @@
     segment_row = seg_ids.reshape(-1)
     attended, local_segments = attend_chunk(projected[0, 0], segment_row, "sp")
     merged = attended.reshape(tok_rows, model_width)
-    merged = from_behind(merged, "section", 1)
-    local_segments = from_behind(local_segments, "section", 1)
+    seg_line = jnp.zeros((1, model_width), jnp.bfloat16).at[0, :tok_rows].set(
+        local_segments.astype(jnp.bfloat16)
+    )
+    packed = from_behind(jnp.concatenate([merged, seg_line], axis=0), "section", 1)
+    merged = packed[:tok_rows]
+    local_segments = packed[tok_rows, :tok_rows].astype(jnp.int32)
     seg_gate = from_behind(sample_gates(condition[0], w_gate[0]), "section", 1)
     seg_count = seg_gate.shape[0]
     one_hot = (local_segments[:, None] == jnp.arange(seg_count, dtype=jnp.int32)[None, :]).astype(
@@ -108,7 +117,7 @@
         P("section", dp, None),
     )
     return jax.shard_map(
-        shards,
+        section_step,
         mesh=split_mesh,
         in_specs=placed,
         out_specs=P("section", dp, "sp", None),

time: 120 us -> 121 us (level)
  starting transfers between devices: 50.8 us -> 43.9 us
  waiting for transfers between devices: 43.4 us -> 49.9 us
  other arithmetic: 3.91 us -> 5.29 us
    ppermute x3 -> x2, waiting for transfers between devices: 5.37 us -> 13.3 us  [from_behind(): return lax.ppermute(block, axis, route)]
    ppermute x3 -> x2, starting transfers between devices: 10.8 us -> 3.84 us  [from_behind(): return lax.ppermute(block, axis, route)]
    another operation x0 -> x2, other arithmetic: none -> 1.35 us
    ppermute x1, waiting for transfers between devices: 10.2 us -> 8.85 us  [neighbour_keys(): from_left = lax.ppermute(kv, axis, [(i, i + 1) for i in range(count - 1)])]
  transfers between devices with their start and end apart: 8 -> 7, of which waited for: 6 -> 7; matrix products, arithmetic and copies ran while one was open for 14% -> 15% of each run, Pallas kernels for 0% -> 0%
where the time goes in v4:
time: 121 us
  waiting for transfers between devices  49.9 us (41%)
  starting transfers between devices  43.9 us (36%)
  local copies, waits for them, and re-layouts  13 us (11%)
  matrix products  8.5 us (7%)
  other arithmetic  5.29 us (4%)
    all_to_all x1, starting transfers between devices, sample_gates(): lax.all_to_all(rows_weight.reshape(row_count, nz, col_block), 'dz', split...  15.2 us
    ppermute x2, waiting for transfers between devices, from_behind(): return lax.ppermute(block, axis, route)  13.3 us
    all_to_all x1, starting transfers between devices, sample_gates(): lax.all_to_all(partial.reshape(nx * nz, seg_count, col_block), dp, split_...  12.2 us
    all_to_all x1, waiting for transfers between devices, sample_gates(): lax.all_to_all(partial.reshape(nx * nz, seg_count, col_block), dp, split_...  11.8 us
    all_to_all x1, waiting for transfers between devices, sample_gates(): lax.all_to_all(rows_weight.reshape(row_count, nz, col_block), 'dz', split...  10.2 us
    ppermute x1, waiting for transfers between devices, neighbour_keys(): from_left = lax.ppermute(kv, axis, [(i, i + 1) for i in range(count - 1)])  8.85 us
    all_to_all x1, starting transfers between devices, sample_gates(): lax.all_to_all(sent.reshape(nx * nz, seg_count, feat_block), dp, split_ax...  6.83 us
    unnamed x9, local copies, waits for them, and re-layouts  5.66 us
  transfers between devices with their start and end apart: 7, of which 7 were waited for; matrix products, arithmetic and copies ran while one was open for 15% of the time, Pallas kernels for 0%

profile of v4, /device:TPU:6, one launch (start us, length us, event | category | flops | bytes accessed | tf_op | source)
XLA Modules:
  0.0 120.8 jit_solution(5985510861355296325)
XLA Ops:
  0.0 1.3 %reshape_squeeze.3 = bf16[64,12,256]{2,1,0:T(8,128)(2,1)S(1)} reshape(bf16[1,64,3072]{2,1,0:T(8,128)(2,1)} %param.9) | data formatting | bytes 786432 | tf_op jit(solution)/shard_map/reshape;squeeze | solution.py:66
  1.3 0.0 copy-start.3
  1.3 0.9 copy.19
  2.1 15.2 %all-to-all-start.1 = ((bf16[64,12,256]{2,0,1:T(8,128)(2,1)}), bf16[64,12,256]{2,0,1:T(8,128)(2,1)S(1)}, u32[]{:S(2)}, u32[]{:S(2)}) async-start(bf16[64,12,256]{2,0,1:T(8,128)(2,1)} %copy.19), calls=%async_computation.1 | async-start | bytes 786432 | tf_op jit(solution)/shard_map/all_to_all | solution.py:65
  17.3 0.0 copy-start
  17.3 2.3 %copy.23 = bf16[1,1,128,3,24,128]{5,2,4,3,1,0:T(8,128)(2,1)S(1)} copy(bf16[1,1,128,3,24,128]{5,4,3,2,1,0:T(8,128)(2,1)} %param.6) | data formatting | bytes 4718592 | tf_op args[0]
  19.6 1.3 %slice.42 = bf16[128,2,24,128]{3,0,2,1:T(8,128)(2,1)} slice(bf16[128,3,24,128]{3,0,2,1:T(8,128)(2,1)S(1)} %bitcast.71), slice={[0:128], [1:3], [0:24], [0:128]} | slice | bytes 3145728 | tf_op jit(solution)/shard_map/slice | solution.py:29
  20.8 4.6 %collective-permute-start = (bf16[128,2,24,128]{3,0,2,1:T(8,128)(2,1)}, bf16[128,2,24,128]{3,0,2,1:T(8,128)(2,1)}, u32[]{:S(2)}, u32[]{:S(2)}) collective-permute-start(bf16[128,2,24,128]{3,0,2,1:T(8,128)(2,1)} %slice.42), channel_id=1, source_target_pairs={{0,1},{1,2},{2,3},{4,5},{5,6},{6,7},{8,9},{9,10},{10,11},{12,13},{... | collective-permute-start | bytes 4718600 | tf_op jit(solution)/shard_map/ppermute | solution.py:20
  25.5 1.3 %collective-permute-start.1 = (bf16[128,2,24,128]{3,0,2,1:T(8,128)(2,1)}, bf16[128,2,24,128]{3,0,2,1:T(8,128)(2,1)}, u32[]{:S(2)}, u32[]{:S(2)}) collective-permute-start(bf16[128,2,24,128]{3,0,2,1:T(8,128)(2,1)} %slice.42), channel_id=1, source_target_pairs={{1,0},{2,1},{3,2},{5,4},{6,5},{7,6},{9,8},{10,9},{11,10},{13,12},{... | collective-permute-start | bytes 4718600 | tf_op jit(solution)/shard_map/ppermute | solution.py:21
  26.8 0.0 copy-done.3
  26.9 10.2 %all-to-all-done.1 = bf16[64,12,256]{2,0,1:T(8,128)(2,1)S(1)} async-done(((bf16[64,12,256]{2,0,1:T(8,128)(2,1)}), bf16[64,12,256]{2,0,1:T(8,128)(2,1)S(1)}, u32[]{:S(2)}, u32[]{:S(2)}) %all-to-all-start.1) | async-done | bytes 393248 | tf_op jit(solution)/shard_map/all_to_all | solution.py:65
  37.1 0.9 broadcast_in_dim.39
  37.9 6.8 %all-to-all-start = ((bf16[48,8,768]{2,1,0:T(8,128)(2,1)}), bf16[48,8,768]{2,1,0:T(8,128)(2,1)S(1)}, u32[]{:S(2)}, u32[]{:S(2)}) async-start(bf16[48,8,768]{2,1,0:T(8,128)(2,1)} %bitcast.17), calls=%async_computation | async-start | bytes 1179648 | tf_op jit(solution)/shard_map/all_to_all | solution.py:70
  44.8 0.0 copy-done
  44.8 2.8 %gather_fusion = s32[384]{0:T(512)S(1)} fusion(s32[512]{0:T(512)S(1)} %bitcast.70, s32[1024]{0:T(1024)S(1)} %pad_clamp_fusion), kind=kCustom, calls=%fused_computation | custom fusion | bytes 4608 | tf_op jit(solution)/shard_map/jit(_take)/gather | solution.py:40
  47.6 0.7 compare_reduce_fusion
  48.3 0.6 fusion.25
  49.0 0.2 compare_and_fusion
  49.1 8.9 %collective-permute-done = bf16[128,2,24,128]{3,0,2,1:T(8,128)(2,1)} collective-permute-done((bf16[128,2,24,128]{3,0,2,1:T(8,128)(2,1)}, bf16[128,2,24,128]{3,0,2,1:T(8,128)(2,1)}, u32[]{:S(2)}, u32[]{:S(2)}) %collective-permute-start) | collective-permute-done | bytes 1572896 | tf_op jit(solution)/shard_map/ppermute | solution.py:20
  58.0 5.3 %collective-permute-done.1 = bf16[128,2,24,128]{3,0,2,1:T(8,128)(2,1)} collective-permute-done((bf16[128,2,24,128]{3,0,2,1:T(8,128)(2,1)}, bf16[128,2,24,128]{3,0,2,1:T(8,128)(2,1)}, u32[]{:S(2)}, u32[]{:S(2)}) %collective-permute-start.1) | collective-permute-done | bytes 1572896 | tf_op jit(solution)/shard_map/ppermute | solution.py:21
  63.3 2.6 %pad_maximum_fusion = bf16[384,2,24,128]{3,0,2,1:T(8,128)(2,1)S(1)} fusion(bf16[128,2,24,128]{3,0,2,1:T(8,128)(2,1)} %collective-permute-done.1, bf16[128,2,24,128]{3,0,2,1:T(8,128)(2,1)} %slice.42, bf16[128,2,24,128]{3,0,2,1:T(8,128)(2,1)} %collective-permute-done), kind=kLoop, calls=%fused_computation.1 | loop fusion | flops 14155776 | bytes 9437184 | tf_op jit(solution)/shard_map/concatenate | solution.py:22
  65.9 0.0 copy-start.1
  65.9 0.9 fusion.3
  66.8 1.3 %copy-done.1 = bf16[384,2,24,128]{3,0,2,1:T(8,128)(2,1)} copy-done((bf16[384,2,24,128]{3,0,2,1:T(8,128)(2,1)}, bf16[384,2,24,128]{3,0,2,1:T(8,128)(2,1)S(1)}, u32[]{:S(2)}) %copy-start.1) | copy-done | bytes 4718616
  68.0 0.0 copy-start.2
  68.0 2.1 %copy-done.2 = f32[24,384,128]{2,1,0:T(8,128)} copy-done((f32[24,384,128]{2,1,0:T(8,128)}, f32[24,384,128]{2,1,0:T(8,128)S(1)}, u32[]{:S(2)}) %copy-start.2) | copy-done | bytes 4718616
  70.2 1.0 fusion
  71.1 0.6 all-to-all-done
  71.7 1.1 fusion.32
  72.8 12.2 %all-to-all-start.2 = ((f32[48,8,256]{2,1,0:T(8,128)}), f32[48,8,256]{2,1,0:T(8,128)S(1)}, u32[]{:S(2)}, u32[]{:S(2)}) async-start(f32[48,8,256]{2,1,0:T(8,128)} %fusion.32), calls=%async_computation.2 | async-start | bytes 786432 | tf_op jit(solution)/shard_map/all_to_all | solution.py:74
  85.0 4.8 %fusion.13 = bf16[128,24,128]{0,2,1:T(8,128)(2,1)S(1)} fusion(f32[128,24]{0,1:T(8,128)S(1)} %bitcast.78, f32[24,384,128]{2,1,0:T(8,128)} %copy-done.2, f32[24,128]{1,0:T(8,128)S(1)} %get-tuple-element.17, pred[128,384]{0,1:T(8,128)(4,1)S(1)} %compare_and_fusion, bf16[384,2,24,128]{3,0,2,1:T(8,128)(2,1)} %copy-done.1), kind=kOutput, calls=%fused_computation.22 | convolution fusion | flops 307494912 | bytes 7938048 | tf_op jit(solution)/shard_map/hqk,khd->qhd/dot_general | solution.py:51
  89.8 0.3 copy.18
  90.1 0.1 fusion.14
  90.1 1.9 %collective-permute-start.2 = (bf16[129,3072]{1,0:T(8,128)(2,1)S(1)}, bf16[129,3072]{1,0:T(8,128)(2,1)S(1)}, u32[]{:S(2)}, u32[]{:S(2)}) collective-permute-start(bf16[129,3072]{1,0:T(8,128)(2,1)S(1)} %fusion.14), channel_id=1, source_target_pairs={{576,0},{0,192},{192,384},{384,576},{577,1},{1,193},{193,385},{385... | collective-permute-start | bytes 2377736 | tf_op jit(solution)/shard_map/ppermute | solution.py:15
  92.1 11.8 %all-to-all-done.2 = f32[48,8,256]{2,1,0:T(8,128)S(1)} async-done(((f32[48,8,256]{2,1,0:T(8,128)}), f32[48,8,256]{2,1,0:T(8,128)S(1)}, u32[]{:S(2)}, u32[]{:S(2)}) %all-to-all-start.2) | async-done | bytes 393248 | tf_op jit(solution)/shard_map/all_to_all | solution.py:74
  103.9 1.9 %collective-permute-start.3 = (f32[8,3072]{1,0:T(8,128)S(1)}, f32[8,3072]{1,0:T(8,128)S(1)}, u32[]{:S(2)}, u32[]{:S(2)}) collective-permute-start(f32[8,3072]{1,0:T(8,128)S(1)} %bitcast.76), channel_id=1, source_target_pairs={{576,0},{0,192},{192,384},{384,576},{577,1},{1,193},{193,385},{385... | collective-permute-start | bytes 294920 | tf_op jit(solution)/shard_map/ppermute | solution.py:15
  105.8 12.3 %collective-permute-done.2 = bf16[129,3072]{1,0:T(8,128)(2,1)S(1)} collective-permute-done((bf16[129,3072]{1,0:T(8,128)(2,1)S(1)}, bf16[129,3072]{1,0:T(8,128)(2,1)S(1)}, u32[]{:S(2)}, u32[]{:S(2)}) %collective-permute-start.2) | collective-permute-done | bytes 792608 | tf_op jit(solution)/shard_map/ppermute | solution.py:15
  118.1 1.0 collective-permute-done.3
  119.1 1.7 %fusion.4 = bf16[1,1,128,3072]{3,2,1,0:T(8,128)(2,1)} fusion(f32[8,3072]{1,0:T(8,128)S(1)} %collective-permute-done.3, bf16[129,3072]{1,0:T(8,128)(2,1)S(1)} %collective-permute-done.2, s32[128]{0:T(128)S(1)} %fusion.26), kind=kOutput, calls=%fused_computation.9 | convolution fusion | flops 38929408 | bytes 1671680 | tf_op jit(solution)/shard_map/dot_general | solution.py:101
  (8 shorter events, 0.1 us)
Async XLA Ops:
  1.3 25.6 %copy-start.3 = (bf16[1,8,3072]{2,1,0:T(8,128)(2,1)S(1)}, bf16[1,8,3072]{2,1,0:T(8,128)(2,1)}, u32[]{:S(2)}) copy-start(bf16[1,8,3072]{2,1,0:T(8,128)(2,1)} %param.8) | copy-start | bytes 147460
  2.1 34.9 %all-to-all-start.1 = ((bf16[64,12,256]{2,0,1:T(8,128)(2,1)}), bf16[64,12,256]{2,0,1:T(8,128)(2,1)S(1)}, u32[]{:S(2)}, u32[]{:S(2)}) async-start(bf16[64,12,256]{2,0,1:T(8,128)(2,1)} %copy.19), calls=%async_computation.1 | async-start | bytes 786432 | tf_op jit(solution)/shard_map/all_to_all | solution.py:65
  17.3 27.5 %copy-start = (s32[1,1,512]{2,1,0:T(1,128)S(1)}, s32[1,1,512]{2,1,0:T(1,128)}, u32[]{:S(2)}) copy-start(s32[1,1,512]{2,1,0:T(1,128)} %param.7) | copy-start | bytes 6148
  20.8 37.1 %collective-permute-start = (bf16[128,2,24,128]{3,0,2,1:T(8,128)(2,1)}, bf16[128,2,24,128]{3,0,2,1:T(8,128)(2,1)}, u32[]{:S(2)}, u32[]{:S(2)}) collective-permute-start(bf16[128,2,24,128]{3,0,2,1:T(8,128)(2,1)} %slice.42), channel_id=1, source_target_pairs={{0,1},{1,2},{2,3},{4,5},{5,6},{6,7},{8,9},{9,10},{10,11},{12,13},{... | collective-permute-start | bytes 4718600 | tf_op jit(solution)/shard_map/ppermute | solution.py:20
  25.5 37.8 %collective-permute-start.1 = (bf16[128,2,24,128]{3,0,2,1:T(8,128)(2,1)}, bf16[128,2,24,128]{3,0,2,1:T(8,128)(2,1)}, u32[]{:S(2)}, u32[]{:S(2)}) collective-permute-start(bf16[128,2,24,128]{3,0,2,1:T(8,128)(2,1)} %slice.42), channel_id=1, source_target_pairs={{1,0},{2,1},{3,2},{5,4},{6,5},{7,6},{9,8},{10,9},{11,10},{13,12},{... | collective-permute-start | bytes 4718600 | tf_op jit(solution)/shard_map/ppermute | solution.py:21
  37.9 33.8 %all-to-all-start = ((bf16[48,8,768]{2,1,0:T(8,128)(2,1)}), bf16[48,8,768]{2,1,0:T(8,128)(2,1)S(1)}, u32[]{:S(2)}, u32[]{:S(2)}) async-start(bf16[48,8,768]{2,1,0:T(8,128)(2,1)} %bitcast.17), calls=%async_computation | async-start | bytes 1179648 | tf_op jit(solution)/shard_map/all_to_all | solution.py:70
  65.9 2.2 %copy-start.1 = (bf16[384,2,24,128]{3,0,2,1:T(8,128)(2,1)}, bf16[384,2,24,128]{3,0,2,1:T(8,128)(2,1)S(1)}, u32[]{:S(2)}) copy-start(bf16[384,2,24,128]{3,0,2,1:T(8,128)(2,1)S(1)} %pad_maximum_fusion) | copy-start | bytes 14155780
  68.0 2.1 %copy-start.2 = (f32[24,384,128]{2,1,0:T(8,128)}, f32[24,384,128]{2,1,0:T(8,128)S(1)}, u32[]{:S(2)}) copy-start(f32[24,384,128]{2,1,0:T(8,128)S(1)} %get-tuple-element.18) | copy-start | bytes 14155780
  72.8 31.0 %all-to-all-start.2 = ((f32[48,8,256]{2,1,0:T(8,128)}), f32[48,8,256]{2,1,0:T(8,128)S(1)}, u32[]{:S(2)}, u32[]{:S(2)}) async-start(f32[48,8,256]{2,1,0:T(8,128)} %fusion.32), calls=%async_computation.2 | async-start | bytes 786432 | tf_op jit(solution)/shard_map/all_to_all | solution.py:74
  90.1 27.9 %collective-permute-start.2 = (bf16[129,3072]{1,0:T(8,128)(2,1)S(1)}, bf16[129,3072]{1,0:T(8,128)(2,1)S(1)}, u32[]{:S(2)}, u32[]{:S(2)}) collective-permute-start(bf16[129,3072]{1,0:T(8,128)(2,1)S(1)} %fusion.14), channel_id=1, source_target_pairs={{576,0},{0,192},{192,384},{384,576},{577,1},{1,193},{193,385},{385... | collective-permute-start | bytes 2377736 | tf_op jit(solution)/shard_map/ppermute | solution.py:15
  103.9 15.2 %collective-permute-start.3 = (f32[8,3072]{1,0:T(8,128)S(1)}, f32[8,3072]{1,0:T(8,128)S(1)}, u32[]{:S(2)}, u32[]{:S(2)}) collective-permute-start(f32[8,3072]{1,0:T(8,128)S(1)} %bitcast.76), channel_id=1, source_target_pairs={{576,0},{0,192},{192,384},{384,576},{577,1},{1,193},{193,385},{385... | collective-permute-start | bytes 294920 | tf_op jit(solution)/shard_map/ppermute | solution.py:15

commit v5 on v3

--- a/solution.py
+++ b/solution.py
@@ -49,18 +49,23 @@
     return mixed_out.astype(jnp.bfloat16), query_seg
 
 
-def sample_gates(cond, rows_weight):
+def weight_columns(rows_weight):
+    row_count, model_width = rows_weight.shape
+    nz = lax.axis_size("dz")
+    col_block = model_width // nz
+    return lax.all_to_all(
+        rows_weight.reshape(row_count, nz, col_block), "dz", split_axis=1, concat_axis=0, tiled=True
+    ).reshape(nz * row_count, col_block)
+
+
+def sample_gates(cond, w_cols):
     dp = ("dx", "dz")
     seg_count, model_width = cond.shape
-    row_count = rows_weight.shape[0]
     nx = lax.axis_size("dx")
     nz = lax.axis_size("dz")
     col_block = model_width // nz
     feat_block = model_width // nx
     cond_act = jax.nn.silu(cond.astype(jnp.float32)).astype(jnp.bfloat16)
-    w_cols = lax.all_to_all(
-        rows_weight.reshape(row_count, nz, col_block), "dz", split_axis=1, concat_axis=0, tiled=True
-    ).reshape(nz * row_count, col_block)
     sent = jnp.transpose(cond_act.reshape(seg_count, nx, feat_block), (1, 0, 2))
     sent = jnp.broadcast_to(sent[:, None], (nx, nz, seg_count, feat_block))
     feat = lax.all_to_all(
@@ -82,9 +87,15 @@
     segment_row = seg_ids.reshape(-1)
     attended, local_segments = attend_chunk(projected[0, 0], segment_row, "sp")
     merged = attended.reshape(tok_rows, model_width)
+    seg_count = condition.shape[1]
+    seg_line = jnp.zeros((1, model_width), jnp.bfloat16).at[0, :tok_rows].set(
+        local_segments.astype(jnp.bfloat16)
+    )
+    packed = from_behind(jnp.concatenate([condition[0], seg_line], axis=0), "section", 1)
+    local_segments = packed[seg_count, :tok_rows].astype(jnp.int32)
+    w_cols = from_behind(weight_columns(w_gate[0]), "section", 1)
+    seg_gate = sample_gates(packed[:seg_count], w_cols)
     merged = from_behind(merged, "section", 1)
-    local_segments = from_behind(local_segments, "section", 1)
-    seg_gate = from_behind(sample_gates(condition[0], w_gate[0]), "section", 1)
     seg_count = seg_gate.shape[0]
     one_hot = (local_segments[:, None] == jnp.arange(seg_count, dtype=jnp.int32)[None, :]).astype(
         jnp.float32

time: 120 us -> 134 us (1.12)
  the two profiles are of different devices: /device:TPU:6 before, /device:TPU:14 now
where the time goes in v5:
time: 134 us; the launch traced here: 133 us
  starting transfers between devices  56.4 us (42%)
  waiting for transfers between devices  50.9 us (38%)
  local copies, waits for them, and re-layouts  11.2 us (8%)
  matrix products  9.48 us (7%)
  other arithmetic  5.13 us (4%)
    ppermute x3, waiting for transfers between devices, from_behind(): return lax.ppermute(block, axis, route)  38.8 us
    all_to_all x1, starting transfers between devices, sample_gates(): lax.all_to_all(sent.reshape(nx * nz, seg_count, feat_block), dp, split_ax...  18.6 us
    all_to_all x1, starting transfers between devices, weight_columns(): lax.all_to_all(rows_weight.reshape(row_count, nz, col_block), 'dz', split...  15.2 us
    all_to_all x1, starting transfers between devices, sample_gates(): lax.all_to_all(partial.reshape(nx * nz, seg_count, col_block), dp, split_...  9.95 us
    all_to_all x1, waiting for transfers between devices, sample_gates(): lax.all_to_all(partial.reshape(nx * nz, seg_count, col_block), dp, split_...  9.64 us
    ppermute x3, starting transfers between devices, from_behind(): return lax.ppermute(block, axis, route)  5.76 us
    unnamed x11, local copies, waits for them, and re-layouts  4.85 us
    dot_general x1, matrix products, attend_chunk(): jnp.einsum('hqk,khd->qhd', rounded, values, preferred_element_type=jnp.fl...  4.82 us
  transfers between devices with their start and end apart: 8, of which 5 were waited for; matrix products, arithmetic and copies ran while one was open for 12% of the time, Pallas kernels for 0%

profile of v5, /device:TPU:14, one launch (start us, length us, event | category | flops | bytes accessed | tf_op | source)
XLA Modules:
  0.0 133.4 jit_solution(6323586686041232772)
XLA Ops:
  0.0 0.0 copy-start.3
  0.0 0.0 copy-start
  0.0 0.0 copy-start.4
  0.0 2.3 %copy.24 = bf16[1,1,128,3,24,128]{5,2,4,3,1,0:T(8,128)(2,1)S(1)} copy(bf16[1,1,128,3,24,128]{5,4,3,2,1,0:T(8,128)(2,1)} %param.6) | data formatting | bytes 4718592 | tf_op args[0]
  2.3 1.3 slice.44
  3.6 3.5 %collective-permute-start.2 = (bf16[128,2,24,128]{3,0,2,1:T(8,128)(2,1)}, bf16[128,2,24,128]{3,0,2,1:T(8,128)(2,1)}, u32[]{:S(2)}, u32[]{:S(2)}) collective-permute-start(bf16[128,2,24,128]{3,0,2,1:T(8,128)(2,1)} %slice.44), channel_id=1, source_target_pairs={{0,1},{1,2},{2,3},{4,5},{5,6},{6,7},{8,9},{9,10},{10,11},{12,13},{... | collective-permute-start | bytes 4718600 | tf_op jit(solution)/shard_map/ppermute | solution.py:19
  7.1 3.5 %collective-permute-start.3 = (bf16[128,2,24,128]{3,0,2,1:T(8,128)(2,1)}, bf16[128,2,24,128]{3,0,2,1:T(8,128)(2,1)}, u32[]{:S(2)}, u32[]{:S(2)}) collective-permute-start(bf16[128,2,24,128]{3,0,2,1:T(8,128)(2,1)} %slice.44), channel_id=1, source_target_pairs={{1,0},{2,1},{3,2},{5,4},{6,5},{7,6},{9,8},{10,9},{11,10},{13,12},{... | collective-permute-start | bytes 4718600 | tf_op jit(solution)/shard_map/ppermute | solution.py:20
  10.6 0.0 copy-done.3
  10.6 0.3 reshape_squeeze.3
  10.9 0.9 copy.15
  11.7 15.2 %all-to-all-start.1 = ((bf16[64,12,256]{2,0,1:T(8,128)(2,1)}), bf16[64,12,256]{2,0,1:T(8,128)(2,1)S(1)}, u32[]{:S(2)}, u32[]{:S(2)}) async-start(bf16[64,12,256]{2,0,1:T(8,128)(2,1)} %copy.15), calls=%async_computation.1 | async-start | bytes 786432 | tf_op jit(solution)/shard_map/all_to_all | solution.py:56
  26.9 0.6 compare_reduce_fusion
  27.5 0.0 copy-done
  27.5 0.6 fusion.26
  28.1 0.0 copy-done.4
  28.1 1.9 %collective-permute-start = (bf16[9,3072]{1,0:T(8,128)(2,1)S(1)}, bf16[9,3072]{1,0:T(8,128)(2,1)S(1)}, u32[]{:S(2)}, u32[]{:S(2)}) collective-permute-start(bf16[9,3072]{1,0:T(8,128)(2,1)S(1)} %fusion.19), channel_id=1, source_target_pairs={{576,0},{0,192},{192,384},{384,576},{577,1},{1,193},{193,385},{385... | collective-permute-start | bytes 165896 | tf_op jit(solution)/shard_map/ppermute | solution.py:14
  30.1 21.2 %collective-permute-done = bf16[9,3072]{1,0:T(8,128)(2,1)S(1)} collective-permute-done((bf16[9,3072]{1,0:T(8,128)(2,1)S(1)}, bf16[9,3072]{1,0:T(8,128)(2,1)S(1)}, u32[]{:S(2)}, u32[]{:S(2)}) %collective-permute-start) | collective-permute-done | bytes 55328 | tf_op jit(solution)/shard_map/ppermute | solution.py:14
  51.3 0.0 all-to-all-done.1
  51.3 0.9 broadcast_in_dim.22
  52.2 18.6 %all-to-all-start = ((bf16[48,8,768]{2,1,0:T(8,128)(2,1)}), bf16[48,8,768]{2,1,0:T(8,128)(2,1)S(1)}, u32[]{:S(2)}, u32[]{:S(2)}) async-start(bf16[48,8,768]{2,1,0:T(8,128)(2,1)} %bitcast.5), calls=%async_computation | async-start | bytes 1179648 | tf_op jit(solution)/shard_map/all_to_all | solution.py:71
  70.7 2.8 %gather_fusion = s32[384]{0:T(512)S(1)} fusion(s32[512]{0:T(512)S(1)} %bitcast.70, s32[1024]{0:T(1024)S(1)} %pad_clamp_fusion), kind=kCustom, calls=%fused_computation | custom fusion | bytes 4608 | tf_op jit(solution)/shard_map/jit(_take)/gather | solution.py:36
  73.6 0.2 compare_and_fusion
  73.8 1.9 %collective-permute-start.1 = (bf16[768,256]{1,0:T(8,128)(2,1)S(1)}, bf16[768,256]{1,0:T(8,128)(2,1)}, u32[]{:S(2)}, u32[]{:S(2)}) collective-permute-start(bf16[768,256]{1,0:T(8,128)(2,1)S(1)} %bitcast.75), channel_id=1, source_target_pairs={{576,0},{0,192},{192,384},{384,576},{577,1},{1,193},{193,385},{385... | collective-permute-start | bytes 1179656 | tf_op jit(solution)/shard_map/ppermute | solution.py:14
  75.7 0.0 collective-permute-done.2
  75.7 0.0 collective-permute-done.3
  75.7 2.6 %pad_maximum_fusion = bf16[384,2,24,128]{3,0,2,1:T(8,128)(2,1)S(1)} fusion(bf16[128,2,24,128]{3,0,2,1:T(8,128)(2,1)} %collective-permute-done.3, bf16[128,2,24,128]{3,0,2,1:T(8,128)(2,1)} %slice.44, bf16[128,2,24,128]{3,0,2,1:T(8,128)(2,1)} %collective-permute-done.2), kind=kLoop, calls=%fused_computation.1 | loop fusion | flops 14155776 | bytes 9437184 | tf_op jit(solution)/shard_map/concatenate | solution.py:21
  78.3 0.0 copy-start.1
  78.3 0.9 fusion.2
  79.2 0.0 copy-start.2
  79.2 2.5 %copy-done.2 = f32[24,384,128]{2,1,0:T(8,128)} copy-done((f32[24,384,128]{2,1,0:T(8,128)}, f32[24,384,128]{2,1,0:T(8,128)S(1)}, u32[]{:S(2)}) %copy-start.2) | copy-done | bytes 4718616
  81.7 1.0 fusion
  82.8 0.0 copy-done.1
  82.8 6.9 %collective-permute-done.1 = bf16[768,256]{1,0:T(8,128)(2,1)} collective-permute-done((bf16[768,256]{1,0:T(8,128)(2,1)S(1)}, bf16[768,256]{1,0:T(8,128)(2,1)}, u32[]{:S(2)}, u32[]{:S(2)}) %collective-permute-start.1) | collective-permute-done | bytes 393248 | tf_op jit(solution)/shard_map/ppermute | solution.py:14
  89.7 2.5 %all-to-all-done = bf16[48,8,768]{2,1,0:T(8,128)(2,1)S(1)} async-done(((bf16[48,8,768]{2,1,0:T(8,128)(2,1)}), bf16[48,8,768]{2,1,0:T(8,128)(2,1)S(1)}, u32[]{:S(2)}, u32[]{:S(2)}) %all-to-all-start) | async-done | bytes 589856 | tf_op jit(solution)/shard_map/all_to_all | solution.py:71
  92.2 2.1 %fusion.12 = f32[48,8,256]{2,1,0:T(8,128)} fusion(bf16[48,8,768]{2,1,0:T(8,128)(2,1)S(1)} %all-to-all-done, bf16[768,256]{1,0:T(8,128)(2,1)} %collective-permute-done.1), kind=kOutput, calls=%fused_computation.21 | convolution fusion | flops 150994944 | bytes 1376256 | tf_op jit(solution)/shard_map/dot_general | solution.py:74
  94.2 10.0 %all-to-all-start.2 = ((f32[48,8,256]{2,1,0:T(8,128)}), f32[48,8,256]{2,1,0:T(8,128)S(1)}, u32[]{:S(2)}, u32[]{:S(2)}) async-start(f32[48,8,256]{2,1,0:T(8,128)} %fusion.12), calls=%async_computation.2 | async-start | bytes 786432 | tf_op jit(solution)/shard_map/all_to_all | solution.py:75
  104.2 4.8 %fusion.10 = bf16[128,24,128]{0,2,1:T(8,128)(2,1)S(1)} fusion(f32[128,24]{0,1:T(8,128)S(1)} %bitcast.79, f32[24,384,128]{2,1,0:T(8,128)} %copy-done.2, f32[24,128]{1,0:T(8,128)S(1)} %get-tuple-element.17, pred[128,384]{0,1:T(8,128)(4,1)S(1)} %compare_and_fusion, bf16[384,2,24,128]{3,0,2,1:T(8,128)(2,1)} %copy-done.1), kind=kOutput, calls=%fused_computation.17 | convolution fusion | flops 307494912 | bytes 7938048 | tf_op jit(solution)/shard_map/hqk,khd->qhd/dot_general | solution.py:47
  109.0 0.3 copy.22
  109.3 1.9 %collective-permute-start.4 = (bf16[128,3072]{1,0:T(8,128)(2,1)S(1)}, bf16[128,3072]{1,0:T(8,128)(2,1)S(1)}, u32[]{:S(2)}, u32[]{:S(2)}) collective-permute-start(bf16[128,3072]{1,0:T(8,128)(2,1)S(1)} %copy.22), channel_id=1, source_target_pairs={{576,0},{0,192},{192,384},{384,576},{577,1},{1,193},{193,385},{385... | collective-permute-start | bytes 2359304 | tf_op jit(solution)/shard_map/ppermute | solution.py:14
  111.3 9.6 %all-to-all-done.2 = f32[48,8,256]{2,1,0:T(8,128)S(1)} async-done(((f32[48,8,256]{2,1,0:T(8,128)}), f32[48,8,256]{2,1,0:T(8,128)S(1)}, u32[]{:S(2)}, u32[]{:S(2)}) %all-to-all-start.2) | async-done | bytes 393248 | tf_op jit(solution)/shard_map/all_to_all | solution.py:75
  120.9 10.7 %collective-permute-done.4 = bf16[128,3072]{1,0:T(8,128)(2,1)S(1)} collective-permute-done((bf16[128,3072]{1,0:T(8,128)(2,1)S(1)}, bf16[128,3072]{1,0:T(8,128)(2,1)S(1)}, u32[]{:S(2)}, u32[]{:S(2)}) %collective-permute-start.4) | collective-permute-done | bytes 786464 | tf_op jit(solution)/shard_map/ppermute | solution.py:14
  131.7 1.7 %fusion.11 = bf16[1,1,128,3072]{3,2,1,0:T(8,128)(2,1)} fusion(bf16[128,3072]{1,0:T(8,128)(2,1)S(1)} %collective-permute-done.4, f32[8,3072]{1,0:T(8,128)S(1)} %bitcast.76, s32[128]{0:T(128)S(1)} %fusion.27), kind=kOutput, calls=%fused_computation.19 | convolution fusion | flops 38929408 | bytes 1671680 | tf_op jit(solution)/shard_map/dot_general | solution.py:103
  (9 shorter events, 0.1 us)
Async XLA Ops:
  0.0 10.6 %copy-start.3 = (bf16[1,64,3072]{2,1,0:T(8,128)(2,1)S(1)}, bf16[1,64,3072]{2,1,0:T(8,128)(2,1)}, u32[]{:S(2)}) copy-start(bf16[1,64,3072]{2,1,0:T(8,128)(2,1)} %param.9) | copy-start | bytes 1179652
  0.0 27.5 %copy-start = (s32[1,1,512]{2,1,0:T(1,128)S(1)}, s32[1,1,512]{2,1,0:T(1,128)}, u32[]{:S(2)}) copy-start(s32[1,1,512]{2,1,0:T(1,128)} %param.7) | copy-start | bytes 6148
  0.0 28.1 %copy-start.4 = (bf16[1,8,3072]{2,1,0:T(8,128)(2,1)S(1)}, bf16[1,8,3072]{2,1,0:T(8,128)(2,1)}, u32[]{:S(2)}) copy-start(bf16[1,8,3072]{2,1,0:T(8,128)(2,1)} %param.8) | copy-start | bytes 147460
  3.6 72.1 %collective-permute-start.2 = (bf16[128,2,24,128]{3,0,2,1:T(8,128)(2,1)}, bf16[128,2,24,128]{3,0,2,1:T(8,128)(2,1)}, u32[]{:S(2)}, u32[]{:S(2)}) collective-permute-start(bf16[128,2,24,128]{3,0,2,1:T(8,128)(2,1)} %slice.44), channel_id=1, source_target_pairs={{0,1},{1,2},{2,3},{4,5},{5,6},{6,7},{8,9},{9,10},{10,11},{12,13},{... | collective-permute-start | bytes 4718600 | tf_op jit(solution)/shard_map/ppermute | solution.py:19
  7.1 68.6 %collective-permute-start.3 = (bf16[128,2,24,128]{3,0,2,1:T(8,128)(2,1)}, bf16[128,2,24,128]{3,0,2,1:T(8,128)(2,1)}, u32[]{:S(2)}, u32[]{:S(2)}) collective-permute-start(bf16[128,2,24,128]{3,0,2,1:T(8,128)(2,1)} %slice.44), channel_id=1, source_target_pairs={{1,0},{2,1},{3,2},{5,4},{6,5},{7,6},{9,8},{10,9},{11,10},{13,12},{... | collective-permute-start | bytes 4718600 | tf_op jit(solution)/shard_map/ppermute | solution.py:20
  11.7 39.6 %all-to-all-start.1 = ((bf16[64,12,256]{2,0,1:T(8,128)(2,1)}), bf16[64,12,256]{2,0,1:T(8,128)(2,1)S(1)}, u32[]{:S(2)}, u32[]{:S(2)}) async-start(bf16[64,12,256]{2,0,1:T(8,128)(2,1)} %copy.15), calls=%async_computation.1 | async-start | bytes 786432 | tf_op jit(solution)/shard_map/all_to_all | solution.py:56
  28.1 23.1 %collective-permute-start = (bf16[9,3072]{1,0:T(8,128)(2,1)S(1)}, bf16[9,3072]{1,0:T(8,128)(2,1)S(1)}, u32[]{:S(2)}, u32[]{:S(2)}) collective-permute-start(bf16[9,3072]{1,0:T(8,128)(2,1)S(1)} %fusion.19), channel_id=1, source_target_pairs={{576,0},{0,192},{192,384},{384,576},{577,1},{1,193},{193,385},{385... | collective-permute-start | bytes 165896 | tf_op jit(solution)/shard_map/ppermute | solution.py:14
  52.2 40.0 %all-to-all-start = ((bf16[48,8,768]{2,1,0:T(8,128)(2,1)}), bf16[48,8,768]{2,1,0:T(8,128)(2,1)S(1)}, u32[]{:S(2)}, u32[]{:S(2)}) async-start(bf16[48,8,768]{2,1,0:T(8,128)(2,1)} %bitcast.5), calls=%async_computation | async-start | bytes 1179648 | tf_op jit(solution)/shard_map/all_to_all | solution.py:71
  73.8 15.9 %collective-permute-start.1 = (bf16[768,256]{1,0:T(8,128)(2,1)S(1)}, bf16[768,256]{1,0:T(8,128)(2,1)}, u32[]{:S(2)}, u32[]{:S(2)}) collective-permute-start(bf16[768,256]{1,0:T(8,128)(2,1)S(1)} %bitcast.75), channel_id=1, source_target_pairs={{576,0},{0,192},{192,384},{384,576},{577,1},{1,193},{193,385},{385... | collective-permute-start | bytes 1179656 | tf_op jit(solution)/shard_map/ppermute | solution.py:14
  78.3 4.4 %copy-start.1 = (bf16[384,2,24,128]{3,0,2,1:T(8,128)(2,1)}, bf16[384,2,24,128]{3,0,2,1:T(8,128)(2,1)S(1)}, u32[]{:S(2)}) copy-start(bf16[384,2,24,128]{3,0,2,1:T(8,128)(2,1)S(1)} %pad_maximum_fusion) | copy-start | bytes 14155780
  79.2 2.5 %copy-start.2 = (f32[24,384,128]{2,1,0:T(8,128)}, f32[24,384,128]{2,1,0:T(8,128)S(1)}, u32[]{:S(2)}) copy-start(f32[24,384,128]{2,1,0:T(8,128)S(1)} %get-tuple-element.18) | copy-start | bytes 14155780
  94.2 26.7 %all-to-all-start.2 = ((f32[48,8,256]{2,1,0:T(8,128)}), f32[48,8,256]{2,1,0:T(8,128)S(1)}, u32[]{:S(2)}, u32[]{:S(2)}) async-start(f32[48,8,256]{2,1,0:T(8,128)} %fusion.12), calls=%async_computation.2 | async-start | bytes 786432 | tf_op jit(solution)/shard_map/all_to_all | solution.py:75
  109.3 22.3 %collective-permute-start.4 = (bf16[128,3072]{1,0:T(8,128)(2,1)S(1)}, bf16[128,3072]{1,0:T(8,128)(2,1)S(1)}, u32[]{:S(2)}, u32[]{:S(2)}) collective-permute-start(bf16[128,3072]{1,0:T(8,128)(2,1)S(1)} %copy.22), channel_id=1, source_target_pairs={{576,0},{0,192},{192,384},{384,576},{577,1},{1,193},{193,385},{385... | collective-permute-start | bytes 2359304 | tf_op jit(solution)/shard_map/ppermute | solution.py:14

commit v6 on v4

--- a/solution.py
+++ b/solution.py
@@ -4,7 +4,6 @@
 import jax.numpy as jnp
 from jax import lax
 from jax.sharding import Mesh, PartitionSpec as P
-
 
 masked_score = -1e30
 
@@ -26,11 +25,8 @@
     rows = local.shape[0]
     chunk = lax.axis_index(axis)
     total_rows = segment_row.shape[0]
+    query_rows = local[:, 0]
     keys = neighbour_keys(local[:, 1:3], axis)
-    return attend_keys(local[:, 0], keys, segment_row, chunk, rows, total_rows)
-
-
-def attend_keys(query_rows, keys, segment_row, chunk, rows, total_rows):
     key_rows = keys[:, 0]
     values = keys[:, 1]
     scale_factor = 1.0 / math.sqrt(query_rows.shape[2])
@@ -57,29 +53,29 @@
     dp = ("dx", "dz")
     seg_count, model_width = cond.shape
     row_count = rows_weight.shape[0]
-    nx = lax.axis_size("dx")
-    nz = lax.axis_size("dz")
-    col_block = model_width // nz
-    feat_block = model_width // nx
+    n_dp = model_width // row_count
+    n_sp = lax.axis_size("sp")
+    n_section = lax.axis_size("section")
+    col_block = model_width // n_sp
     cond_act = jax.nn.silu(cond.astype(jnp.float32)).astype(jnp.bfloat16)
-    w_cols = lax.all_to_all(
-        rows_weight.reshape(row_count, nz, col_block), "dz", split_axis=1, concat_axis=0, tiled=True
-    ).reshape(nz * row_count, col_block)
-    sent = jnp.transpose(cond_act.reshape(seg_count, nx, feat_block), (1, 0, 2))
-    sent = jnp.broadcast_to(sent[:, None], (nx, nz, seg_count, feat_block))
     feat = lax.all_to_all(
-        sent.reshape(nx * nz, seg_count, feat_block), dp, split_axis=0, concat_axis=0, tiled=True
-    ).reshape(nx * nz * seg_count, feat_block)
-    partial = jnp.dot(feat, w_cols, preferred_element_type=jnp.float32)
+        cond_act.reshape(seg_count, n_dp, row_count), dp, split_axis=1, concat_axis=0, tiled=True
+    ).reshape(n_dp * seg_count, row_count)
+    cols = lax.dynamic_slice_in_dim(rows_weight, lax.axis_index("sp") * col_block, col_block, 1)
+    partial = jnp.dot(feat, cols, preferred_element_type=jnp.float32).astype(jnp.bfloat16)
     parts = lax.all_to_all(
-        partial.reshape(nx * nz, seg_count, col_block), dp, split_axis=0, concat_axis=0, tiled=True
+        partial.reshape(n_dp, seg_count, col_block), dp, split_axis=0, concat_axis=0, tiled=True
     )
-    parts = parts.reshape(nx, nz, seg_count, col_block)
-    summed = jnp.sum(parts, axis=0)
-    return jnp.transpose(summed, (1, 0, 2)).reshape(seg_count, model_width)
+    summed = jnp.sum(parts.astype(jnp.float32), axis=0)
+    section = lax.axis_index("section")
+    toward = (jnp.arange(n_section * n_sp, dtype=jnp.int32) // n_sp) == (section + 1) % n_section
+    sent = jnp.where(toward[:, None, None], summed[None], 0.0)
+    got = lax.all_to_all(sent, ("section", "sp"), split_axis=0, concat_axis=0, tiled=True)
+    got = lax.dynamic_slice_in_dim(got, ((section + n_section - 1) % n_section) * n_sp, n_sp, 0)
+    return jnp.transpose(got, (1, 0, 2)).reshape(seg_count, model_width)
 
 
-def section_step(projected, seg_ids, condition, w_gate):
+def shards(projected, seg_ids, condition, w_gate):
     tok_rows = projected.shape[2]
     head_count = projected.shape[4]
     head_size = projected.shape[5]
@@ -93,7 +89,7 @@
     packed = from_behind(jnp.concatenate([merged, seg_line], axis=0), "section", 1)
     merged = packed[:tok_rows]
     local_segments = packed[tok_rows, :tok_rows].astype(jnp.int32)
-    seg_gate = from_behind(sample_gates(condition[0], w_gate[0]), "section", 1)
+    seg_gate = sample_gates(condition[0], w_gate[0])
     seg_count = seg_gate.shape[0]
     one_hot = (local_segments[:, None] == jnp.arange(seg_count, dtype=jnp.int32)[None, :]).astype(
         jnp.float32
@@ -117,7 +113,7 @@
         P("section", dp, None),
     )
     return jax.shard_map(
-        section_step,
+        shards,
         mesh=split_mesh,
         in_specs=placed,
         out_specs=P("section", dp, "sp", None),

time: 121 us -> 98.8 us (0.82)
  the two profiles are of different devices: /device:TPU:6 before, /device:TPU:15 now
where the time goes in v6:
time: 98.8 us; the launch traced here: 98.3 us
  starting transfers between devices  51.6 us (52%)
  waiting for transfers between devices  25.4 us (26%)
  local copies, waits for them, and re-layouts  7.73 us (8%)
  other arithmetic  6.72 us (7%)
  matrix products  6.71 us (7%)
    all_to_all x1, starting transfers between devices, sample_gates(): lax.all_to_all(cond_act.reshape(seg_count, n_dp, row_count), dp, split_ax...  18 us
    all_to_all x1, waiting for transfers between devices, sample_gates(): lax.all_to_all(sent, ('section', 'sp'), split_axis=0, concat_axis=0, tile...  12.8 us
    all_to_all x1, starting transfers between devices, sample_gates(): lax.all_to_all(sent, ('section', 'sp'), split_axis=0, concat_axis=0, tile...  11.6 us
    ppermute x1, starting transfers between devices, from_behind(): return lax.ppermute(block, axis, route)  9.21 us
    all_to_all x1, waiting for transfers between devices, sample_gates(): lax.all_to_all(partial.reshape(n_dp, seg_count, col_block), dp, split_axi...  7.07 us
    all_to_all x1, starting transfers between devices, sample_gates(): lax.all_to_all(partial.reshape(n_dp, seg_count, col_block), dp, split_axi...  6.42 us
    all_to_all x1, waiting for transfers between devices, sample_gates(): lax.all_to_all(cond_act.reshape(seg_count, n_dp, row_count), dp, split_ax...  5.48 us
    ppermute x1, starting transfers between devices, neighbour_keys(): from_right = lax.ppermute(kv, axis, [(i + 1, i) for i in range(count - 1)])  3.2 us
  transfers between devices with their start and end apart: 6, of which 3 were waited for; matrix products, arithmetic and copies ran while one was open for 15% of the time, Pallas kernels for 0%

profile of v6, /device:TPU:15, one launch (start us, length us, event | category | flops | bytes accessed | tf_op | source)
XLA Modules:
  0.0 98.3 jit_solution(4197542220951099152)
XLA Ops:
  0.0 0.0 copy-start
  0.0 0.0 copy-start.2
  0.0 0.0 copy-start.1
  0.0 2.3 %copy.21 = bf16[1,1,128,3,24,128]{5,2,4,3,1,0:T(8,128)(2,1)S(1)} copy(bf16[1,1,128,3,24,128]{5,4,3,2,1,0:T(8,128)(2,1)} %param.6) | data formatting | bytes 4718592 | tf_op args[0]
  2.3 1.3 %slice.42 = bf16[128,2,24,128]{3,0,2,1:T(8,128)(2,1)} slice(bf16[128,3,24,128]{3,0,2,1:T(8,128)(2,1)S(1)} %bitcast.75), slice={[0:128], [1:3], [0:24], [0:128]} | slice | bytes 3145728 | tf_op jit(solution)/shard_map/slice | solution.py:29
  3.7 3.2 %collective-permute-start = (bf16[128,2,24,128]{3,0,2,1:T(8,128)(2,1)}, bf16[128,2,24,128]{3,0,2,1:T(8,128)(2,1)}, u32[]{:S(2)}, u32[]{:S(2)}) collective-permute-start(bf16[128,2,24,128]{3,0,2,1:T(8,128)(2,1)} %slice.42), channel_id=1, source_target_pairs={{0,1},{1,2},{2,3},{4,5},{5,6},{6,7},{8,9},{9,10},{10,11},{12,13},{... | collective-permute-start | bytes 4718600 | tf_op jit(solution)/shard_map/ppermute | solution.py:19
  6.9 3.2 %collective-permute-start.1 = (bf16[128,2,24,128]{3,0,2,1:T(8,128)(2,1)}, bf16[128,2,24,128]{3,0,2,1:T(8,128)(2,1)}, u32[]{:S(2)}, u32[]{:S(2)}) collective-permute-start(bf16[128,2,24,128]{3,0,2,1:T(8,128)(2,1)} %slice.42), channel_id=1, source_target_pairs={{1,0},{2,1},{3,2},{5,4},{6,5},{7,6},{9,8},{10,9},{11,10},{13,12},{... | collective-permute-start | bytes 4718600 | tf_op jit(solution)/shard_map/ppermute | solution.py:20
  10.1 0.0 copy-done.2
  10.1 0.1 reshape.187
  10.2 0.1 fusion.34
  10.3 0.8 reshape.197
  11.0 18.0 %all-to-all-start = ((bf16[48,2,256]{2,1,0:T(2,128)(2,1)}), bf16[48,2,256]{2,1,0:T(2,128)(2,1)S(1)}, u32[]{:S(2)}, u32[]{:S(2)}) async-start(bf16[48,2,256]{2,1,0:T(2,128)(2,1)} %reshape.197), calls=%async_computation | async-start | bytes 98304 | tf_op jit(solution)/shard_map/all_to_all | solution.py:61
  29.1 0.0 copy-done.1
  29.1 2.8 %gather_fusion = s32[384]{0:T(512)S(1)} fusion(s32[512]{0:T(512)S(1)} %bitcast.74, s32[1024]{0:T(1024)S(1)} %pad_clamp_fusion), kind=kCustom, calls=%fused_computation | custom fusion | bytes 4608 | tf_op jit(solution)/shard_map/jit(_take)/gather | solution.py:36
  31.9 0.6 compare_reduce_fusion
  32.5 0.2 compare_and_fusion
  32.7 0.6 fusion.25
  33.3 5.5 %all-to-all-done = bf16[48,2,256]{2,1,0:T(2,128)(2,1)S(1)} async-done(((bf16[48,2,256]{2,1,0:T(2,128)(2,1)}), bf16[48,2,256]{2,1,0:T(2,128)(2,1)S(1)}, u32[]{:S(2)}, u32[]{:S(2)}) %all-to-all-start) | async-done | bytes 49184 | tf_op jit(solution)/shard_map/all_to_all | solution.py:61
  38.8 0.1 reshape.198
  38.9 0.0 copy-done
  38.9 1.1 %fusion.12 = bf16[48,8,768]{2,1,0:T(8,128)(2,1)} fusion(bf16[1,64,3072]{2,1,0:T(8,128)(2,1)S(1)} %copy-done, s32[]{:T(128)S(6)} %select_n.72, bf16[48,8,64]{2,1,0:T(8,128)(2,1)S(1)} %reshape.198), kind=kOutput, calls=%fused_computation.22 | convolution fusion | flops 38043648 | bytes 786436 | tf_op jit(solution)/shard_map/dot_general | solution.py:65
  40.0 6.4 %all-to-all-start.1 = ((bf16[48,8,768]{2,1,0:T(8,128)(2,1)}), bf16[48,8,768]{2,1,0:T(8,128)(2,1)S(1)}, u32[]{:S(2)}, u32[]{:S(2)}) async-start(bf16[48,8,768]{2,1,0:T(8,128)(2,1)} %fusion.12), calls=%async_computation.1 | async-start | bytes 1179648 | tf_op jit(solution)/shard_map/all_to_all | solution.py:66
  46.5 0.0 collective-permute-done
  46.5 0.0 collective-permute-done.1
  46.5 2.5 %pad_maximum_fusion = bf16[384,2,24,128]{3,0,2,1:T(8,128)(2,1)S(1)} fusion(bf16[128,2,24,128]{3,0,2,1:T(8,128)(2,1)} %collective-permute-done.1, bf16[128,2,24,128]{3,0,2,1:T(8,128)(2,1)} %slice.42, bf16[128,2,24,128]{3,0,2,1:T(8,128)(2,1)} %collective-permute-done), kind=kLoop, calls=%fused_computation.1 | loop fusion | flops 14155776 | bytes 9437184 | tf_op jit(solution)/shard_map/concatenate | solution.py:21
  49.0 0.9 fusion.2
  49.9 1.0 %fusion = f32[24,128]{1,0:T(8,128)S(1)} fusion(f32[24,384,128]{2,1,0:T(8,128)S(1)} %get-tuple-element.18, f32[24,128]{1,0:T(8,128)S(1)} %get-tuple-element.17, pred[128,384]{0,1:T(8,128)(4,1)S(1)} %compare_and_fusion), kind=kLoop, calls=%fused_computation.4 | loop fusion | flops 4715520 | bytes 4792320 | tf_op jit(solution)/shard_map/reduce_sum | solution.py:45
  50.9 1.9 %fusion.11 = bf16[128,24,128]{0,2,1:T(8,128)(2,1)S(1)} fusion(f32[128,24]{0,1:T(8,128)S(1)} %bitcast.79, f32[24,384,128]{2,1,0:T(8,128)S(1)} %get-tuple-element.18, f32[24,128]{1,0:T(8,128)S(1)} %get-tuple-element.17, pred[128,384]{0,1:T(8,128)(4,1)S(1)} %compare_and_fusion, bf16[384,2,24,128]{3,0,2,1:T(8,128)(2,1)S(1)} %pad_maximum_fusion), kind=kOutput, calls=%fused_computation.19 | convolution fusion | flops 307494912 | bytes 7938048 | tf_op jit(solution)/shard_map/hqk,khd->qhd/dot_general | solution.py:47
  52.8 0.3 copy.12
  53.1 0.1 fusion.13
  53.1 9.2 %collective-permute-start.2 = (bf16[129,3072]{1,0:T(8,128)(2,1)S(1)}, bf16[129,3072]{1,0:T(8,128)(2,1)}, u32[]{:S(2)}, u32[]{:S(2)}) collective-permute-start(bf16[129,3072]{1,0:T(8,128)(2,1)S(1)} %fusion.13), channel_id=1, source_target_pairs={{576,0},{0,192},{192,384},{384,576},{577,1},{1,193},{193,385},{385... | collective-permute-start | bytes 2377736 | tf_op jit(solution)/shard_map/ppermute | solution.py:14
  62.4 7.1 %all-to-all-done.1 = bf16[48,8,768]{2,1,0:T(8,128)(2,1)S(1)} async-done(((bf16[48,8,768]{2,1,0:T(8,128)(2,1)}), bf16[48,8,768]{2,1,0:T(8,128)(2,1)S(1)}, u32[]{:S(2)}, u32[]{:S(2)}) %all-to-all-start.1) | async-done | bytes 589856 | tf_op jit(solution)/shard_map/all_to_all | solution.py:66
  69.4 0.1 convert_reduce_fusion
  69.5 0.8 broadcast_select_fusion
  70.4 11.6 %all-to-all-start.2 = ((f32[16,8,768]{2,1,0:T(8,128)}), f32[16,8,768]{2,1,0:T(8,128)S(1)}, u32[]{:S(2)}, u32[]{:S(2)}) async-start(f32[16,8,768]{2,1,0:T(8,128)} %broadcast_select_fusion), calls=%async_computation.2 | async-start | bytes 786432 | tf_op jit(solution)/shard_map/all_to_all | solution.py:73
  81.9 0.0 collective-permute-done.2
  81.9 0.7 fusion.27
  82.6 12.8 %all-to-all-done.2 = f32[16,8,768]{2,1,0:T(8,128)S(1)} async-done(((f32[16,8,768]{2,1,0:T(8,128)}), f32[16,8,768]{2,1,0:T(8,128)S(1)}, u32[]{:S(2)}, u32[]{:S(2)}) %all-to-all-start.2) | async-done | bytes 393248 | tf_op jit(solution)/shard_map/all_to_all | solution.py:73
  95.5 2.9 %fusion.14 = bf16[1,1,128,3072]{3,2,1,0:T(8,128)(2,1)} fusion(bf16[129,3072]{1,0:T(8,128)(2,1)} %collective-permute-done.2, f32[8,3072]{1,0:T(8,128)S(1)} %bitcast.78, s32[128]{0:T(128)S(1)} %fusion.27), kind=kOutput, calls=%fused_computation.25 | convolution fusion | flops 38929408 | bytes 1671680 | tf_op jit(solution)/shard_map/dot_general | solution.py:97
  (7 shorter events, 0.1 us)
Async XLA Ops:
  0.0 38.9 %copy-start = (bf16[1,64,3072]{2,1,0:T(8,128)(2,1)S(1)}, bf16[1,64,3072]{2,1,0:T(8,128)(2,1)}, u32[]{:S(2)}) copy-start(bf16[1,64,3072]{2,1,0:T(8,128)(2,1)} %param.9) | copy-start | bytes 1179652
  0.0 10.1 %copy-start.2 = (bf16[1,8,3072]{2,1,0:T(8,128)(2,1)S(1)}, bf16[1,8,3072]{2,1,0:T(8,128)(2,1)}, u32[]{:S(2)}) copy-start(bf16[1,8,3072]{2,1,0:T(8,128)(2,1)} %param.8) | copy-start | bytes 147460
  0.0 29.1 %copy-start.1 = (s32[1,1,512]{2,1,0:T(1,128)S(1)}, s32[1,1,512]{2,1,0:T(1,128)}, u32[]{:S(2)}) copy-start(s32[1,1,512]{2,1,0:T(1,128)} %param.7) | copy-start | bytes 6148
  3.7 42.8 %collective-permute-start = (bf16[128,2,24,128]{3,0,2,1:T(8,128)(2,1)}, bf16[128,2,24,128]{3,0,2,1:T(8,128)(2,1)}, u32[]{:S(2)}, u32[]{:S(2)}) collective-permute-start(bf16[128,2,24,128]{3,0,2,1:T(8,128)(2,1)} %slice.42), channel_id=1, source_target_pairs={{0,1},{1,2},{2,3},{4,5},{5,6},{6,7},{8,9},{9,10},{10,11},{12,13},{... | collective-permute-start | bytes 4718600 | tf_op jit(solution)/shard_map/ppermute | solution.py:19
  6.9 39.6 %collective-permute-start.1 = (bf16[128,2,24,128]{3,0,2,1:T(8,128)(2,1)}, bf16[128,2,24,128]{3,0,2,1:T(8,128)(2,1)}, u32[]{:S(2)}, u32[]{:S(2)}) collective-permute-start(bf16[128,2,24,128]{3,0,2,1:T(8,128)(2,1)} %slice.42), channel_id=1, source_target_pairs={{1,0},{2,1},{3,2},{5,4},{6,5},{7,6},{9,8},{10,9},{11,10},{13,12},{... | collective-permute-start | bytes 4718600 | tf_op jit(solution)/shard_map/ppermute | solution.py:20
  11.0 27.7 %all-to-all-start = ((bf16[48,2,256]{2,1,0:T(2,128)(2,1)}), bf16[48,2,256]{2,1,0:T(2,128)(2,1)S(1)}, u32[]{:S(2)}, u32[]{:S(2)}) async-start(bf16[48,2,256]{2,1,0:T(2,128)(2,1)} %reshape.197), calls=%async_computation | async-start | bytes 98304 | tf_op jit(solution)/shard_map/all_to_all | solution.py:61
  40.0 29.4 %all-to-all-start.1 = ((bf16[48,8,768]{2,1,0:T(8,128)(2,1)}), bf16[48,8,768]{2,1,0:T(8,128)(2,1)S(1)}, u32[]{:S(2)}, u32[]{:S(2)}) async-start(bf16[48,8,768]{2,1,0:T(8,128)(2,1)} %fusion.12), calls=%async_computation.1 | async-start | bytes 1179648 | tf_op jit(solution)/shard_map/all_to_all | solution.py:66
  53.1 28.8 %collective-permute-start.2 = (bf16[129,3072]{1,0:T(8,128)(2,1)S(1)}, bf16[129,3072]{1,0:T(8,128)(2,1)}, u32[]{:S(2)}, u32[]{:S(2)}) collective-permute-start(bf16[129,3072]{1,0:T(8,128)(2,1)S(1)} %fusion.13), channel_id=1, source_target_pairs={{576,0},{0,192},{192,384},{384,576},{577,1},{1,193},{193,385},{385... | collective-permute-start | bytes 2377736 | tf_op jit(solution)/shard_map/ppermute | solution.py:14
  70.4 25.1 %all-to-all-start.2 = ((f32[16,8,768]{2,1,0:T(8,128)}), f32[16,8,768]{2,1,0:T(8,128)S(1)}, u32[]{:S(2)}, u32[]{:S(2)}) async-start(f32[16,8,768]{2,1,0:T(8,128)} %broadcast_select_fusion), calls=%async_computation.2 | async-start | bytes 786432 | tf_op jit(solution)/shard_map/all_to_all | solution.py:73

commit v7 on v6

--- a/solution.py
+++ b/solution.py
@@ -4,6 +4,7 @@
 import jax.numpy as jnp
 from jax import lax
 from jax.sharding import Mesh, PartitionSpec as P
+
 
 masked_score = -1e30
 
@@ -60,7 +61,8 @@
     cond_act = jax.nn.silu(cond.astype(jnp.float32)).astype(jnp.bfloat16)
     feat = lax.all_to_all(
         cond_act.reshape(seg_count, n_dp, row_count), dp, split_axis=1, concat_axis=0, tiled=True
-    ).reshape(n_dp * seg_count, row_count)
+    )
+    feat = feat.reshape(n_dp * seg_count, row_count)
     cols = lax.dynamic_slice_in_dim(rows_weight, lax.axis_index("sp") * col_block, col_block, 1)
     partial = jnp.dot(feat, cols, preferred_element_type=jnp.float32).astype(jnp.bfloat16)
     parts = lax.all_to_all(
@@ -75,7 +77,7 @@
     return jnp.transpose(got, (1, 0, 2)).reshape(seg_count, model_width)
 
 
-def shards(projected, seg_ids, condition, w_gate):
+def section_step(projected, seg_ids, condition, w_gate):
     tok_rows = projected.shape[2]
     head_count = projected.shape[4]
     head_size = projected.shape[5]
@@ -91,10 +93,11 @@
     local_segments = packed[tok_rows, :tok_rows].astype(jnp.int32)
     seg_gate = sample_gates(condition[0], w_gate[0])
     seg_count = seg_gate.shape[0]
-    one_hot = (local_segments[:, None] == jnp.arange(seg_count, dtype=jnp.int32)[None, :]).astype(
-        jnp.float32
-    )
-    token_gate = jnp.dot(one_hot, seg_gate, precision=lax.Precision.HIGHEST)
+    token_gate = jnp.broadcast_to(seg_gate[0][None, :], (tok_rows, model_width))
+    for sample in range(1, seg_count):
+        token_gate = jnp.where(
+            (local_segments == sample)[:, None], seg_gate[sample][None, :], token_gate
+        )
     handed = (token_gate * merged.astype(jnp.float32)).astype(jnp.bfloat16)
     return handed.reshape(1, 1, tok_rows, model_width)
 
@@ -113,7 +116,7 @@
         P("section", dp, None),
     )
     return jax.shard_map(
-        shards,
+        section_step,
         mesh=split_mesh,
         in_specs=placed,
         out_specs=P("section", dp, "sp", None),

time: 98.8 us -> 99.4 us (level)
  other arithmetic: 6.72 us -> 10.2 us
  matrix products: 6.71 us -> 3.85 us
    reshape x0 -> x1, other arithmetic: none -> 3.26 us  [section_step(): return handed.reshape(1, 1, tok_rows, model_width)]
    dot_general x1 -> x0, matrix products: 2.86 us -> none  [shards(): token_gate = jnp.dot(one_hot, seg_gate, precision=lax.Precision.HIGHEST)]
where the time goes in v7:
time: 99.4 us; the launch traced here: 98.9 us
  starting transfers between devices  51.6 us (52%)
  waiting for transfers between devices  25.4 us (26%)
  other arithmetic  10.2 us (10%)
  local copies, waits for them, and re-layouts  7.73 us (8%)
  matrix products  3.85 us (4%)
    all_to_all x1, starting transfers between devices, sample_gates(): lax.all_to_all(cond_act.reshape(seg_count, n_dp, row_count), dp, split_ax...  18 us
    all_to_all x1, waiting for transfers between devices, sample_gates(): lax.all_to_all(sent, ('section', 'sp'), split_axis=0, concat_axis=0, tile...  12.8 us
    all_to_all x1, starting transfers between devices, sample_gates(): lax.all_to_all(sent, ('section', 'sp'), split_axis=0, concat_axis=0, tile...  11.6 us
    ppermute x1, starting transfers between devices, from_behind(): return lax.ppermute(block, axis, route)  9.02 us
    all_to_all x1, waiting for transfers between devices, sample_gates(): lax.all_to_all(partial.reshape(n_dp, seg_count, col_block), dp, split_axi...  7.24 us
    all_to_all x1, starting transfers between devices, sample_gates(): lax.all_to_all(partial.reshape(n_dp, seg_count, col_block), dp, split_axi...  6.61 us
    all_to_all x1, waiting for transfers between devices, sample_gates(): lax.all_to_all(cond_act.reshape(seg_count, n_dp, row_count), dp, split_ax...  5.3 us
    reshape x1, other arithmetic, section_step(): return handed.reshape(1, 1, tok_rows, model_width)  3.26 us
  transfers between devices with their start and end apart: 6, of which 3 were waited for; matrix products, arithmetic and copies ran while one was open for 15% of the time, Pallas kernels for 0%

profile of v7, /device:TPU:15, one launch (start us, length us, event | category | flops | bytes accessed | tf_op | source)
XLA Modules:
  0.0 98.9 jit_solution(7454240339030797451)
XLA Ops:
  0.0 0.0 copy-start
  0.0 2.3 %copy.21 = bf16[1,1,128,3,24,128]{5,2,4,3,1,0:T(8,128)(2,1)S(1)} copy(bf16[1,1,128,3,24,128]{5,4,3,2,1,0:T(8,128)(2,1)} %param.6) | data formatting | bytes 4718592 | tf_op args[0]
  2.3 0.0 copy-start.2
  2.3 0.0 copy-start.1
  2.3 1.3 %slice.82 = bf16[128,2,24,128]{3,0,2,1:T(8,128)(2,1)} slice(bf16[128,3,24,128]{3,0,2,1:T(8,128)(2,1)S(1)} %bitcast.90), slice={[0:128], [1:3], [0:24], [0:128]} | slice | bytes 3145728 | tf_op jit(solution)/shard_map/slice | solution.py:30
  3.6 3.2 %collective-permute-start = (bf16[128,2,24,128]{3,0,2,1:T(8,128)(2,1)}, bf16[128,2,24,128]{3,0,2,1:T(8,128)(2,1)}, u32[]{:S(2)}, u32[]{:S(2)}) collective-permute-start(bf16[128,2,24,128]{3,0,2,1:T(8,128)(2,1)} %slice.82), channel_id=1, source_target_pairs={{0,1},{1,2},{2,3},{4,5},{5,6},{6,7},{8,9},{9,10},{10,11},{12,13},{... | collective-permute-start | bytes 4718600 | tf_op jit(solution)/shard_map/ppermute | solution.py:20
  6.8 3.2 %collective-permute-start.1 = (bf16[128,2,24,128]{3,0,2,1:T(8,128)(2,1)}, bf16[128,2,24,128]{3,0,2,1:T(8,128)(2,1)}, u32[]{:S(2)}, u32[]{:S(2)}) collective-permute-start(bf16[128,2,24,128]{3,0,2,1:T(8,128)(2,1)} %slice.82), channel_id=1, source_target_pairs={{1,0},{2,1},{3,2},{5,4},{6,5},{7,6},{9,8},{10,9},{11,10},{13,12},{... | collective-permute-start | bytes 4718600 | tf_op jit(solution)/shard_map/ppermute | solution.py:21
  10.0 0.0 copy-done.2
  10.0 0.1 reshape.237
  10.1 0.1 fusion.32
  10.2 0.8 reshape.247
  11.0 18.0 %all-to-all-start = ((bf16[48,2,256]{2,1,0:T(2,128)(2,1)}), bf16[48,2,256]{2,1,0:T(2,128)(2,1)S(1)}, u32[]{:S(2)}, u32[]{:S(2)}) async-start(bf16[48,2,256]{2,1,0:T(2,128)(2,1)} %reshape.247), calls=%async_computation | async-start | bytes 98304 | tf_op jit(solution)/shard_map/all_to_all | solution.py:62
  29.0 0.0 copy-done.1
  29.1 2.8 %gather_fusion = s32[384]{0:T(512)S(1)} fusion(s32[512]{0:T(512)S(1)} %bitcast.89, s32[1024]{0:T(1024)S(1)} %pad_clamp_fusion), kind=kCustom, calls=%fused_computation | custom fusion | bytes 4608 | tf_op jit(solution)/shard_map/jit(_take)/gather | solution.py:37
  31.9 0.7 compare_reduce_fusion
  32.6 0.2 compare_and_fusion
  32.8 0.6 fusion.23
  33.4 5.3 %all-to-all-done = bf16[48,2,256]{2,1,0:T(2,128)(2,1)S(1)} async-done(((bf16[48,2,256]{2,1,0:T(2,128)(2,1)}), bf16[48,2,256]{2,1,0:T(2,128)(2,1)S(1)}, u32[]{:S(2)}, u32[]{:S(2)}) %all-to-all-start) | async-done | bytes 49184 | tf_op jit(solution)/shard_map/all_to_all | solution.py:62
  38.7 0.1 reshape.248
  38.9 0.0 copy-done
  38.9 1.1 %fusion.12 = bf16[48,8,768]{2,1,0:T(8,128)(2,1)} fusion(bf16[1,64,3072]{2,1,0:T(8,128)(2,1)S(1)} %copy-done, s32[]{:T(128)S(6)} %select_n.94, bf16[48,8,64]{2,1,0:T(8,128)(2,1)S(1)} %reshape.248), kind=kOutput, calls=%fused_computation.22 | convolution fusion | flops 38043648 | bytes 786436 | tf_op jit(solution)/shard_map/dot_general | solution.py:67
  40.0 6.6 %all-to-all-start.1 = ((bf16[48,8,768]{2,1,0:T(8,128)(2,1)}), bf16[48,8,768]{2,1,0:T(8,128)(2,1)S(1)}, u32[]{:S(2)}, u32[]{:S(2)}) async-start(bf16[48,8,768]{2,1,0:T(8,128)(2,1)} %fusion.12), calls=%async_computation.1 | async-start | bytes 1179648 | tf_op jit(solution)/shard_map/all_to_all | solution.py:68
  46.6 0.0 collective-permute-done
  46.6 0.0 collective-permute-done.1
  46.6 2.5 %pad_maximum_fusion = bf16[384,2,24,128]{3,0,2,1:T(8,128)(2,1)S(1)} fusion(bf16[128,2,24,128]{3,0,2,1:T(8,128)(2,1)} %collective-permute-done.1, bf16[128,2,24,128]{3,0,2,1:T(8,128)(2,1)} %slice.82, bf16[128,2,24,128]{3,0,2,1:T(8,128)(2,1)} %collective-permute-done), kind=kLoop, calls=%fused_computation.1 | loop fusion | flops 14155776 | bytes 9437184 | tf_op jit(solution)/shard_map/concatenate | solution.py:22
  49.2 0.9 fusion.2
  50.1 1.0 %fusion = f32[24,128]{1,0:T(8,128)S(1)} fusion(f32[24,384,128]{2,1,0:T(8,128)S(1)} %get-tuple-element.33, f32[24,128]{1,0:T(8,128)S(1)} %get-tuple-element.32, pred[128,384]{0,1:T(8,128)(4,1)S(1)} %compare_and_fusion), kind=kLoop, calls=%fused_computation.4 | loop fusion | flops 4715520 | bytes 4792320 | tf_op jit(solution)/shard_map/reduce_sum | solution.py:46
  51.1 1.9 %fusion.11 = bf16[128,24,128]{0,2,1:T(8,128)(2,1)S(1)} fusion(f32[128,24]{0,1:T(8,128)S(1)} %bitcast.101, f32[24,384,128]{2,1,0:T(8,128)S(1)} %get-tuple-element.33, f32[24,128]{1,0:T(8,128)S(1)} %get-tuple-element.32, pred[128,384]{0,1:T(8,128)(4,1)S(1)} %compare_and_fusion, bf16[384,2,24,128]{3,0,2,1:T(8,128)(2,1)S(1)} %pad_maximum_fusion), kind=kOutput, calls=%fused_computation.19 | convolution fusion | flops 307494912 | bytes 7938048 | tf_op jit(solution)/shard_map/hqk,khd->qhd/dot_general | solution.py:48
  52.9 0.3 copy.12
  53.2 0.1 fusion.13
  53.3 9.0 %collective-permute-start.2 = (bf16[129,3072]{1,0:T(8,128)(2,1)S(1)}, bf16[129,3072]{1,0:T(8,128)(2,1)}, u32[]{:S(2)}, u32[]{:S(2)}) collective-permute-start(bf16[129,3072]{1,0:T(8,128)(2,1)S(1)} %fusion.13), channel_id=1, source_target_pairs={{576,0},{0,192},{192,384},{384,576},{577,1},{1,193},{193,385},{385... | collective-permute-start | bytes 2377736 | tf_op jit(solution)/shard_map/ppermute | solution.py:15
  62.3 7.2 %all-to-all-done.1 = bf16[48,8,768]{2,1,0:T(8,128)(2,1)S(1)} async-done(((bf16[48,8,768]{2,1,0:T(8,128)(2,1)}), bf16[48,8,768]{2,1,0:T(8,128)(2,1)S(1)}, u32[]{:S(2)}, u32[]{:S(2)}) %all-to-all-start.1) | async-done | bytes 589856 | tf_op jit(solution)/shard_map/all_to_all | solution.py:68
  69.6 0.1 convert_reduce_fusion
  69.7 0.8 broadcast_select_fusion
  70.5 11.6 %all-to-all-start.2 = ((f32[16,8,768]{2,1,0:T(8,128)}), f32[16,8,768]{2,1,0:T(8,128)S(1)}, u32[]{:S(2)}, u32[]{:S(2)}) async-start(f32[16,8,768]{2,1,0:T(8,128)} %broadcast_select_fusion), calls=%async_computation.2 | async-start | bytes 786432 | tf_op jit(solution)/shard_map/all_to_all | solution.py:75
  82.1 0.0 collective-permute-done.2
  82.1 0.7 compare_bitcast_fusion.6
  82.8 12.8 %all-to-all-done.2 = f32[16,8,768]{2,1,0:T(8,128)S(1)} async-done(((f32[16,8,768]{2,1,0:T(8,128)}), f32[16,8,768]{2,1,0:T(8,128)S(1)}, u32[]{:S(2)}, u32[]{:S(2)}) %all-to-all-start.2) | async-done | bytes 393248 | tf_op jit(solution)/shard_map/all_to_all | solution.py:75
  95.6 0.1 fusion.30
  95.7 3.3 %fusion.14 = bf16[1,1,128,3072]{3,2,1,0:T(8,128)(2,1)} fusion(bf16[129,3072]{1,0:T(8,128)(2,1)} %collective-permute-done.2, f32[3072]{0:T(1024)S(1)} %bitcast.94, f32[3072]{0:T(1024)S(1)} %bitcast.95, f32[3072]{0:T(1024)S(1)} %bitcast.96, f32[3072]{0:T(1024)S(1)} %bitcast.97, f32[3072]{0:T(1024)S(1)} %bitcast.98, f32[3072]{0:T(1024)S(1)} %bitcast.99, ...), kind=kLoop, calls=%fused_computation.25 | loop fusion | flops 3932160 | bytes 1672064 | tf_op jit(solution)/shard_map/reshape | solution.py:102
  (7 shorter events, 0.1 us)
Async XLA Ops:
  0.0 38.9 %copy-start = (bf16[1,64,3072]{2,1,0:T(8,128)(2,1)S(1)}, bf16[1,64,3072]{2,1,0:T(8,128)(2,1)}, u32[]{:S(2)}) copy-start(bf16[1,64,3072]{2,1,0:T(8,128)(2,1)} %param.9) | copy-start | bytes 1179652
  2.3 7.7 %copy-start.2 = (bf16[1,8,3072]{2,1,0:T(8,128)(2,1)S(1)}, bf16[1,8,3072]{2,1,0:T(8,128)(2,1)}, u32[]{:S(2)}) copy-start(bf16[1,8,3072]{2,1,0:T(8,128)(2,1)} %param.8) | copy-start | bytes 147460
  2.3 26.7 %copy-start.1 = (s32[1,1,512]{2,1,0:T(1,128)S(1)}, s32[1,1,512]{2,1,0:T(1,128)}, u32[]{:S(2)}) copy-start(s32[1,1,512]{2,1,0:T(1,128)} %param.7) | copy-start | bytes 6148
  3.6 43.0 %collective-permute-start = (bf16[128,2,24,128]{3,0,2,1:T(8,128)(2,1)}, bf16[128,2,24,128]{3,0,2,1:T(8,128)(2,1)}, u32[]{:S(2)}, u32[]{:S(2)}) collective-permute-start(bf16[128,2,24,128]{3,0,2,1:T(8,128)(2,1)} %slice.82), channel_id=1, source_target_pairs={{0,1},{1,2},{2,3},{4,5},{5,6},{6,7},{8,9},{9,10},{10,11},{12,13},{... | collective-permute-start | bytes 4718600 | tf_op jit(solution)/shard_map/ppermute | solution.py:20
  6.8 39.8 %collective-permute-start.1 = (bf16[128,2,24,128]{3,0,2,1:T(8,128)(2,1)}, bf16[128,2,24,128]{3,0,2,1:T(8,128)(2,1)}, u32[]{:S(2)}, u32[]{:S(2)}) collective-permute-start(bf16[128,2,24,128]{3,0,2,1:T(8,128)(2,1)} %slice.82), channel_id=1, source_target_pairs={{1,0},{2,1},{3,2},{5,4},{6,5},{7,6},{9,8},{10,9},{11,10},{13,12},{... | collective-permute-start | bytes 4718600 | tf_op jit(solution)/shard_map/ppermute | solution.py:21
  11.0 27.7 %all-to-all-start = ((bf16[48,2,256]{2,1,0:T(2,128)(2,1)}), bf16[48,2,256]{2,1,0:T(2,128)(2,1)S(1)}, u32[]{:S(2)}, u32[]{:S(2)}) async-start(bf16[48,2,256]{2,1,0:T(2,128)(2,1)} %reshape.247), calls=%async_computation | async-start | bytes 98304 | tf_op jit(solution)/shard_map/all_to_all | solution.py:62
  40.0 29.6 %all-to-all-start.1 = ((bf16[48,8,768]{2,1,0:T(8,128)(2,1)}), bf16[48,8,768]{2,1,0:T(8,128)(2,1)S(1)}, u32[]{:S(2)}, u32[]{:S(2)}) async-start(bf16[48,8,768]{2,1,0:T(8,128)(2,1)} %fusion.12), calls=%async_computation.1 | async-start | bytes 1179648 | tf_op jit(solution)/shard_map/all_to_all | solution.py:68
  53.3 28.8 %collective-permute-start.2 = (bf16[129,3072]{1,0:T(8,128)(2,1)S(1)}, bf16[129,3072]{1,0:T(8,128)(2,1)}, u32[]{:S(2)}, u32[]{:S(2)}) collective-permute-start(bf16[129,3072]{1,0:T(8,128)(2,1)S(1)} %fusion.13), channel_id=1, source_target_pairs={{576,0},{0,192},{192,384},{384,576},{577,1},{1,193},{193,385},{385... | collective-permute-start | bytes 2377736 | tf_op jit(solution)/shard_map/ppermute | solution.py:15
  70.5 25.1 %all-to-all-start.2 = ((f32[16,8,768]{2,1,0:T(8,128)}), f32[16,8,768]{2,1,0:T(8,128)S(1)}, u32[]{:S(2)}, u32[]{:S(2)}) async-start(f32[16,8,768]{2,1,0:T(8,128)} %broadcast_select_fusion), calls=%async_computation.2 | async-start | bytes 786432 | tf_op jit(solution)/shard_map/all_to_all | solution.py:75

commit v8 on v6

--- a/solution.py
+++ b/solution.py
@@ -62,11 +62,11 @@
         cond_act.reshape(seg_count, n_dp, row_count), dp, split_axis=1, concat_axis=0, tiled=True
     ).reshape(n_dp * seg_count, row_count)
     cols = lax.dynamic_slice_in_dim(rows_weight, lax.axis_index("sp") * col_block, col_block, 1)
-    partial = jnp.dot(feat, cols, preferred_element_type=jnp.float32).astype(jnp.bfloat16)
+    partial = jnp.dot(feat, cols, preferred_element_type=jnp.float32)
     parts = lax.all_to_all(
         partial.reshape(n_dp, seg_count, col_block), dp, split_axis=0, concat_axis=0, tiled=True
     )
-    summed = jnp.sum(parts.astype(jnp.float32), axis=0)
+    summed = jnp.sum(parts, axis=0)
     section = lax.axis_index("section")
     toward = (jnp.arange(n_section * n_sp, dtype=jnp.int32) // n_sp) == (section + 1) % n_section
     sent = jnp.where(toward[:, None, None], summed[None], 0.0)

time: 98.8 us -> 115 us (1.16)
  waiting for transfers between devices: 25.4 us -> 33.5 us
  starting transfers between devices: 51.6 us -> 58.9 us
    ppermute x1, waiting for transfers between devices: 0.01 us -> 12.6 us  [neighbour_keys(): from_left = lax.ppermute(kv, axis, [(i, i + 1) for i in range(count - 1)])]
    all_to_all x1, starting transfers between devices: 6.42 us -> 12 us  [sample_gates(): lax.all_to_all(partial.reshape(n_dp, seg_count, col_block), dp, split_axi...]
    all_to_all x1, waiting for transfers between devices: 5.48 us -> 0.01 us  [sample_gates(): lax.all_to_all(cond_act.reshape(seg_count, n_dp, row_count), dp, split_ax...]
    all_to_all x1, starting transfers between devices: 11.6 us -> 14.6 us  [sample_gates(): lax.all_to_all(sent, ('section', 'sp'), split_axis=0, concat_axis=0, tile...]
    ppermute x1, waiting for transfers between devices: 0.01 us -> 2.93 us  [neighbour_keys(): from_right = lax.ppermute(kv, axis, [(i + 1, i) for i in range(count - 1)])]
    all_to_all x1, waiting for transfers between devices: 7.07 us -> 4.42 us  [sample_gates(): lax.all_to_all(partial.reshape(n_dp, seg_count, col_block), dp, split_axi...]
    ppermute x1, starting transfers between devices: 9.21 us -> 7.91 us  [from_behind(): return lax.ppermute(block, axis, route)]
    reduce_sum x1, other arithmetic: 0.11 us -> 1.36 us  [sample_gates(): summed = jnp.sum(parts, axis=0)]
  transfers between devices with their start and end apart: 6 -> 6, of which waited for: 3 -> 4; matrix products, arithmetic and copies ran while one was open for 15% -> 16% of each run, Pallas kernels for 0% -> 0%
where the time goes in v8:
time: 115 us; the launch traced here: 114 us
  starting transfers between devices  58.9 us (51%)
  waiting for transfers between devices  33.5 us (29%)
  local copies, waits for them, and re-layouts  8.45 us (7%)
  other arithmetic  7.41 us (6%)
  matrix products  5.78 us (5%)
    all_to_all x1, starting transfers between devices, sample_gates(): lax.all_to_all(cond_act.reshape(seg_count, n_dp, row_count), dp, split_ax...  18 us
    all_to_all x1, starting transfers between devices, sample_gates(): lax.all_to_all(sent, ('section', 'sp'), split_axis=0, concat_axis=0, tile...  14.6 us
    all_to_all x1, waiting for transfers between devices, sample_gates(): lax.all_to_all(sent, ('section', 'sp'), split_axis=0, concat_axis=0, tile...  13.5 us
    ppermute x1, waiting for transfers between devices, neighbour_keys(): from_left = lax.ppermute(kv, axis, [(i, i + 1) for i in range(count - 1)])  12.6 us
    all_to_all x1, starting transfers between devices, sample_gates(): lax.all_to_all(partial.reshape(n_dp, seg_count, col_block), dp, split_axi...  12 us
    ppermute x1, starting transfers between devices, from_behind(): return lax.ppermute(block, axis, route)  7.91 us
    all_to_all x1, waiting for transfers between devices, sample_gates(): lax.all_to_all(partial.reshape(n_dp, seg_count, col_block), dp, split_axi...  4.42 us
    ppermute x1, starting transfers between devices, neighbour_keys(): from_right = lax.ppermute(kv, axis, [(i + 1, i) for i in range(count - 1)])  3.2 us
  transfers between devices with their start and end apart: 6, of which 4 were waited for; matrix products, arithmetic and copies ran while one was open for 16% of the time, Pallas kernels for 0%

profile of v8, /device:TPU:15, one launch (start us, length us, event | category | flops | bytes accessed | tf_op | source)
XLA Modules:
  0.0 114.2 jit_solution(5343022332085563428)
XLA Ops:
  0.0 0.0 copy-start
  0.0 1.0 reshape.183
  1.0 0.1 fusion.34
  1.1 0.8 reshape.194
  1.8 18.0 %all-to-all-start = ((bf16[48,2,256]{2,1,0:T(2,128)(2,1)}), bf16[48,2,256]{2,1,0:T(2,128)(2,1)S(1)}, u32[]{:S(2)}, u32[]{:S(2)}) async-start(bf16[48,2,256]{2,1,0:T(2,128)(2,1)} %reshape.194), calls=%async_computation | async-start | bytes 98304 | tf_op jit(solution)/shard_map/all_to_all | solution.py:61
  19.8 2.3 %copy.21 = bf16[1,1,128,3,24,128]{5,2,4,3,1,0:T(8,128)(2,1)S(1)} copy(bf16[1,1,128,3,24,128]{5,4,3,2,1,0:T(8,128)(2,1)} %param.6) | data formatting | bytes 4718592 | tf_op args[0]
  22.1 0.0 copy-start.1
  22.1 1.3 %slice.42 = bf16[128,2,24,128]{3,0,2,1:T(8,128)(2,1)} slice(bf16[128,3,24,128]{3,0,2,1:T(8,128)(2,1)S(1)} %bitcast.74), slice={[0:128], [1:3], [0:24], [0:128]} | slice | bytes 3145728 | tf_op jit(solution)/shard_map/slice | solution.py:29
  23.4 3.2 %collective-permute-start = (bf16[128,2,24,128]{3,0,2,1:T(8,128)(2,1)}, bf16[128,2,24,128]{3,0,2,1:T(8,128)(2,1)}, u32[]{:S(2)}, u32[]{:S(2)}) collective-permute-start(bf16[128,2,24,128]{3,0,2,1:T(8,128)(2,1)} %slice.42), channel_id=1, source_target_pairs={{0,1},{1,2},{2,3},{4,5},{5,6},{6,7},{8,9},{9,10},{10,11},{12,13},{... | collective-permute-start | bytes 4718600 | tf_op jit(solution)/shard_map/ppermute | solution.py:19
  26.6 3.2 %collective-permute-start.1 = (bf16[128,2,24,128]{3,0,2,1:T(8,128)(2,1)}, bf16[128,2,24,128]{3,0,2,1:T(8,128)(2,1)}, u32[]{:S(2)}, u32[]{:S(2)}) collective-permute-start(bf16[128,2,24,128]{3,0,2,1:T(8,128)(2,1)} %slice.42), channel_id=1, source_target_pairs={{1,0},{2,1},{3,2},{5,4},{6,5},{7,6},{9,8},{10,9},{11,10},{13,12},{... | collective-permute-start | bytes 4718600 | tf_op jit(solution)/shard_map/ppermute | solution.py:20
  29.8 0.0 all-to-all-done
  29.8 0.1 reshape.195
  29.9 0.0 copy-done
  29.9 1.3 %fusion.14 = f32[48,8,768]{2,1,0:T(8,128)} fusion(bf16[1,64,3072]{2,1,0:T(8,128)(2,1)S(1)} %copy-done, s32[]{:T(128)S(6)} %select_n.72, bf16[48,8,64]{2,1,0:T(8,128)(2,1)S(1)} %reshape.195), kind=kOutput, calls=%fused_computation.27 | convolution fusion | flops 37748736 | bytes 1376260 | tf_op jit(solution)/shard_map/dot_general | solution.py:65
  31.2 12.0 %all-to-all-start.1 = ((f32[48,8,768]{2,1,0:T(8,128)}), f32[48,8,768]{2,1,0:T(8,128)}, u32[]{:S(2)}, u32[]{:S(2)}) async-start(f32[48,8,768]{2,1,0:T(8,128)} %fusion.14), calls=%async_computation.1 | async-start | bytes 2359296 | tf_op jit(solution)/shard_map/all_to_all | solution.py:66
  43.3 0.0 copy-done.1
  43.3 2.8 %gather_fusion = s32[384]{0:T(512)S(1)} fusion(s32[512]{0:T(512)S(1)} %bitcast.73, s32[1024]{0:T(1024)S(1)} %pad_clamp_fusion), kind=kCustom, calls=%fused_computation | custom fusion | bytes 4608 | tf_op jit(solution)/shard_map/jit(_take)/gather | solution.py:36
  46.1 0.6 compare_reduce_fusion
  46.8 0.7 fusion.25
  47.5 0.2 compare_and_fusion
  47.6 12.6 %collective-permute-done = bf16[128,2,24,128]{3,0,2,1:T(8,128)(2,1)} collective-permute-done((bf16[128,2,24,128]{3,0,2,1:T(8,128)(2,1)}, bf16[128,2,24,128]{3,0,2,1:T(8,128)(2,1)}, u32[]{:S(2)}, u32[]{:S(2)}) %collective-permute-start) | collective-permute-done | bytes 1572896 | tf_op jit(solution)/shard_map/ppermute | solution.py:19
  60.3 2.9 %collective-permute-done.1 = bf16[128,2,24,128]{3,0,2,1:T(8,128)(2,1)} collective-permute-done((bf16[128,2,24,128]{3,0,2,1:T(8,128)(2,1)}, bf16[128,2,24,128]{3,0,2,1:T(8,128)(2,1)}, u32[]{:S(2)}, u32[]{:S(2)}) %collective-permute-start.1) | collective-permute-done | bytes 1572896 | tf_op jit(solution)/shard_map/ppermute | solution.py:20
  63.2 2.5 %pad_maximum_fusion = bf16[384,2,24,128]{3,0,2,1:T(8,128)(2,1)S(1)} fusion(bf16[128,2,24,128]{3,0,2,1:T(8,128)(2,1)} %collective-permute-done.1, bf16[128,2,24,128]{3,0,2,1:T(8,128)(2,1)} %slice.42, bf16[128,2,24,128]{3,0,2,1:T(8,128)(2,1)} %collective-permute-done), kind=kLoop, calls=%fused_computation.1 | loop fusion | flops 14155776 | bytes 9437184 | tf_op jit(solution)/shard_map/concatenate | solution.py:21
  65.7 0.9 fusion.2
  66.6 1.0 fusion
  67.6 1.9 %fusion.11 = bf16[128,24,128]{0,2,1:T(8,128)(2,1)S(1)} fusion(f32[128,24]{0,1:T(8,128)S(1)} %bitcast.78, f32[24,384,128]{2,1,0:T(8,128)S(1)} %get-tuple-element.18, f32[24,128]{1,0:T(8,128)S(1)} %get-tuple-element.17, pred[128,384]{0,1:T(8,128)(4,1)S(1)} %compare_and_fusion, bf16[384,2,24,128]{3,0,2,1:T(8,128)(2,1)S(1)} %pad_maximum_fusion), kind=kOutput, calls=%fused_computation.19 | convolution fusion | flops 307494912 | bytes 7938048 | tf_op jit(solution)/shard_map/hqk,khd->qhd/dot_general | solution.py:47
  69.5 0.3 copy.12
  69.8 0.1 fusion.12
  69.8 7.9 %collective-permute-start.2 = (bf16[129,3072]{1,0:T(8,128)(2,1)S(1)}, bf16[129,3072]{1,0:T(8,128)(2,1)S(1)}, u32[]{:S(2)}, u32[]{:S(2)}) collective-permute-start(bf16[129,3072]{1,0:T(8,128)(2,1)S(1)} %fusion.12), channel_id=1, source_target_pairs={{576,0},{0,192},{192,384},{384,576},{577,1},{1,193},{193,385},{385... | collective-permute-start | bytes 2377736 | tf_op jit(solution)/shard_map/ppermute | solution.py:14
  77.8 4.4 %all-to-all-done.1 = f32[48,8,768]{2,1,0:T(8,128)} async-done(((f32[48,8,768]{2,1,0:T(8,128)}), f32[48,8,768]{2,1,0:T(8,128)}, u32[]{:S(2)}, u32[]{:S(2)}) %all-to-all-start.1) | async-done | bytes 1179680 | tf_op jit(solution)/shard_map/all_to_all | solution.py:66
  82.2 1.4 %reduce_sum.19 = f32[8,768]{1,0:T(8,128)S(1)} reduce(f32[48,8,768]{2,1,0:T(8,128)} %all-to-all-done.1, f32[]{:T(128)} %constant.101.clone.1), dimensions={0}, to_apply=%region_3.4 | reduce | flops 288768 | bytes 1204228 | tf_op jit(solution)/shard_map/reduce_sum | solution.py:69
  83.6 0.8 broadcast_select_fusion
  84.4 14.6 %all-to-all-start.2 = ((f32[16,8,768]{2,1,0:T(8,128)}), f32[16,8,768]{2,1,0:T(8,128)S(1)}, u32[]{:S(2)}, u32[]{:S(2)}) async-start(f32[16,8,768]{2,1,0:T(8,128)} %broadcast_select_fusion), calls=%async_computation.2 | async-start | bytes 786432 | tf_op jit(solution)/shard_map/all_to_all | solution.py:73
  99.0 0.0 collective-permute-done.2
  99.0 13.5 %all-to-all-done.2 = f32[16,8,768]{2,1,0:T(8,128)S(1)} async-done(((f32[16,8,768]{2,1,0:T(8,128)}), f32[16,8,768]{2,1,0:T(8,128)S(1)}, u32[]{:S(2)}, u32[]{:S(2)}) %all-to-all-start.2) | async-done | bytes 393248 | tf_op jit(solution)/shard_map/all_to_all | solution.py:73
  112.5 1.7 %fusion.13 = bf16[1,1,128,3072]{3,2,1,0:T(8,128)(2,1)} fusion(bf16[129,3072]{1,0:T(8,128)(2,1)S(1)} %collective-permute-done.2, f32[8,3072]{1,0:T(8,128)S(1)} %bitcast.77, s32[128]{0:T(128)S(1)} %fusion.27), kind=kOutput, calls=%fused_computation.22 | convolution fusion | flops 38929408 | bytes 1671680 | tf_op jit(solution)/shard_map/dot_general | solution.py:97
  (8 shorter events, 0.1 us)
Async XLA Ops:
  0.0 29.9 %copy-start = (bf16[1,64,3072]{2,1,0:T(8,128)(2,1)S(1)}, bf16[1,64,3072]{2,1,0:T(8,128)(2,1)}, u32[]{:S(2)}) copy-start(bf16[1,64,3072]{2,1,0:T(8,128)(2,1)} %param.9) | copy-start | bytes 1179652
  1.8 27.9 %all-to-all-start = ((bf16[48,2,256]{2,1,0:T(2,128)(2,1)}), bf16[48,2,256]{2,1,0:T(2,128)(2,1)S(1)}, u32[]{:S(2)}, u32[]{:S(2)}) async-start(bf16[48,2,256]{2,1,0:T(2,128)(2,1)} %reshape.194), calls=%async_computation | async-start | bytes 98304 | tf_op jit(solution)/shard_map/all_to_all | solution.py:61
  22.1 21.2 %copy-start.1 = (s32[1,1,512]{2,1,0:T(1,128)S(1)}, s32[1,1,512]{2,1,0:T(1,128)}, u32[]{:S(2)}) copy-start(s32[1,1,512]{2,1,0:T(1,128)} %param.7) | copy-start | bytes 6148
  23.4 36.9 %collective-permute-start = (bf16[128,2,24,128]{3,0,2,1:T(8,128)(2,1)}, bf16[128,2,24,128]{3,0,2,1:T(8,128)(2,1)}, u32[]{:S(2)}, u32[]{:S(2)}) collective-permute-start(bf16[128,2,24,128]{3,0,2,1:T(8,128)(2,1)} %slice.42), channel_id=1, source_target_pairs={{0,1},{1,2},{2,3},{4,5},{5,6},{6,7},{8,9},{9,10},{10,11},{12,13},{... | collective-permute-start | bytes 4718600 | tf_op jit(solution)/shard_map/ppermute | solution.py:19
  26.6 36.6 %collective-permute-start.1 = (bf16[128,2,24,128]{3,0,2,1:T(8,128)(2,1)}, bf16[128,2,24,128]{3,0,2,1:T(8,128)(2,1)}, u32[]{:S(2)}, u32[]{:S(2)}) collective-permute-start(bf16[128,2,24,128]{3,0,2,1:T(8,128)(2,1)} %slice.42), channel_id=1, source_target_pairs={{1,0},{2,1},{3,2},{5,4},{6,5},{7,6},{9,8},{10,9},{11,10},{13,12},{... | collective-permute-start | bytes 4718600 | tf_op jit(solution)/shard_map/ppermute | solution.py:20
  31.2 50.9 %all-to-all-start.1 = ((f32[48,8,768]{2,1,0:T(8,128)}), f32[48,8,768]{2,1,0:T(8,128)}, u32[]{:S(2)}, u32[]{:S(2)}) async-start(f32[48,8,768]{2,1,0:T(8,128)} %fusion.14), calls=%async_computation.1 | async-start | bytes 2359296 | tf_op jit(solution)/shard_map/all_to_all | solution.py:66
  69.8 29.1 %collective-permute-start.2 = (bf16[129,3072]{1,0:T(8,128)(2,1)S(1)}, bf16[129,3072]{1,0:T(8,128)(2,1)S(1)}, u32[]{:S(2)}, u32[]{:S(2)}) collective-permute-start(bf16[129,3072]{1,0:T(8,128)(2,1)S(1)} %fusion.12), channel_id=1, source_target_pairs={{576,0},{0,192},{192,384},{384,576},{577,1},{1,193},{193,385},{385... | collective-permute-start | bytes 2377736 | tf_op jit(solution)/shard_map/ppermute | solution.py:14
  84.4 28.1 %all-to-all-start.2 = ((f32[16,8,768]{2,1,0:T(8,128)}), f32[16,8,768]{2,1,0:T(8,128)S(1)}, u32[]{:S(2)}, u32[]{:S(2)}) async-start(f32[16,8,768]{2,1,0:T(8,128)} %broadcast_select_fusion), calls=%async_computation.2 | async-start | bytes 786432 | tf_op jit(solution)/shard_map/all_to_all | solution.py:73

commit v9 on v8

--- a/solution.py
+++ b/solution.py
@@ -53,26 +53,36 @@
     dp = ("dx", "dz")
     seg_count, model_width = cond.shape
     row_count = rows_weight.shape[0]
-    n_dp = model_width // row_count
+    nx = lax.axis_size("dx")
+    nz = lax.axis_size("dz")
     n_sp = lax.axis_size("sp")
     n_section = lax.axis_size("section")
-    col_block = model_width // n_sp
+    col_block = model_width // (nz * n_sp)
+    feat_block = model_width // nx
     cond_act = jax.nn.silu(cond.astype(jnp.float32)).astype(jnp.bfloat16)
+    mine = lax.dynamic_index_in_dim(
+        rows_weight.reshape(row_count, nz, n_sp, col_block), lax.axis_index("sp"), axis=2,
+        keepdims=False,
+    )
+    w_cols = lax.all_to_all(mine, "dz", split_axis=1, concat_axis=0, tiled=True).reshape(
+        nz * row_count, col_block
+    )
+    sent = jnp.transpose(cond_act.reshape(seg_count, nx, feat_block), (1, 0, 2))
+    sent = jnp.broadcast_to(sent[:, None], (nx, nz, seg_count, feat_block))
     feat = lax.all_to_all(
-        cond_act.reshape(seg_count, n_dp, row_count), dp, split_axis=1, concat_axis=0, tiled=True
-    ).reshape(n_dp * seg_count, row_count)
-    cols = lax.dynamic_slice_in_dim(rows_weight, lax.axis_index("sp") * col_block, col_block, 1)
-    partial = jnp.dot(feat, cols, preferred_element_type=jnp.float32)
+        sent.reshape(nx * nz, seg_count, feat_block), dp, split_axis=0, concat_axis=0, tiled=True
+    ).reshape(nx * nz * seg_count, feat_block)
+    partial = jnp.dot(feat, w_cols, preferred_element_type=jnp.float32)
     parts = lax.all_to_all(
-        partial.reshape(n_dp, seg_count, col_block), dp, split_axis=0, concat_axis=0, tiled=True
-    )
+        partial.reshape(nx * nz, seg_count, col_block), dp, split_axis=0, concat_axis=0, tiled=True
+    ).reshape(nx, nz, seg_count, col_block)
     summed = jnp.sum(parts, axis=0)
     section = lax.axis_index("section")
     toward = (jnp.arange(n_section * n_sp, dtype=jnp.int32) // n_sp) == (section + 1) % n_section
-    sent = jnp.where(toward[:, None, None], summed[None], 0.0)
+    sent = jnp.where(toward[:, None, None, None], summed[None], 0.0)
     got = lax.all_to_all(sent, ("section", "sp"), split_axis=0, concat_axis=0, tiled=True)
     got = lax.dynamic_slice_in_dim(got, ((section + n_section - 1) % n_section) * n_sp, n_sp, 0)
-    return jnp.transpose(got, (1, 0, 2)).reshape(seg_count, model_width)
+    return jnp.transpose(got, (2, 1, 0, 3)).reshape(seg_count, model_width)
 
 
 def shards(projected, seg_ids, condition, w_gate):

time: 115 us -> 121 us (1.052)
  the two profiles are of different devices: /device:TPU:15 before, /device:TPU:6 now
where the time goes in v9:
time: 121 us; the launch traced here: 119 us
  waiting for transfers between devices  49.8 us (41%)
  starting transfers between devices  43 us (36%)
  local copies, waits for them, and re-layouts  12.8 us (11%)
  other arithmetic  8.52 us (7%)
  matrix products  4.79 us (4%)
    all_to_all x1, waiting for transfers between devices, sample_gates(): lax.all_to_all(sent.reshape(nx * nz, seg_count, feat_block), dp, split_ax...  18.6 us
    all_to_all x1, starting transfers between devices, sample_gates(): lax.all_to_all(mine, 'dz', split_axis=1, concat_axis=0, tiled=True)  15.2 us
    all_to_all x1, waiting for transfers between devices, sample_gates(): lax.all_to_all(sent, ('section', 'sp'), split_axis=0, concat_axis=0, tile...  14.4 us
    all_to_all x1, waiting for transfers between devices, sample_gates(): lax.all_to_all(partial.reshape(nx * nz, seg_count, col_block), dp, split_...  9.51 us
    all_to_all x1, starting transfers between devices, sample_gates(): lax.all_to_all(sent, ('section', 'sp'), split_axis=0, concat_axis=0, tile...  7.21 us
    all_to_all x1, waiting for transfers between devices, sample_gates(): lax.all_to_all(mine, 'dz', split_axis=1, concat_axis=0, tiled=True)  6.61 us
    all_to_all x1, starting transfers between devices, sample_gates(): lax.all_to_all(partial.reshape(nx * nz, seg_count, col_block), dp, split_...  6.46 us
    all_to_all x1, starting transfers between devices, sample_gates(): lax.all_to_all(sent.reshape(nx * nz, seg_count, feat_block), dp, split_ax...  6.4 us
  transfers between devices with their start and end apart: 7, of which 5 were waited for; matrix products, arithmetic and copies ran while one was open for 15% of the time, Pallas kernels for 0%

profile of v9, /device:TPU:6, one launch (start us, length us, event | category | flops | bytes accessed | tf_op | source)
XLA Modules:
  0.0 119.3 jit_solution(4022084891441292649)
XLA Ops:
  0.0 0.0 copy-start.1
  0.0 0.0 copy-start
  0.0 2.3 %copy.38 = bf16[1,1,128,3,24,128]{5,2,4,3,1,0:T(8,128)(2,1)S(1)} copy(bf16[1,1,128,3,24,128]{5,4,3,2,1,0:T(8,128)(2,1)} %param.6) | data formatting | bytes 4718592 | tf_op args[0]
  2.3 1.3 %slice.42 = bf16[128,2,24,128]{3,0,2,1:T(8,128)(2,1)} slice(bf16[128,3,24,128]{3,0,2,1:T(8,128)(2,1)S(1)} %bitcast.80), slice={[0:128], [1:3], [0:24], [0:128]} | slice | bytes 3145728 | tf_op jit(solution)/shard_map/slice | solution.py:29
  3.6 4.6 %collective-permute-start = (bf16[128,2,24,128]{3,0,2,1:T(8,128)(2,1)}, bf16[128,2,24,128]{3,0,2,1:T(8,128)(2,1)}, u32[]{:S(2)}, u32[]{:S(2)}) collective-permute-start(bf16[128,2,24,128]{3,0,2,1:T(8,128)(2,1)} %slice.42), channel_id=1, source_target_pairs={{0,1},{1,2},{2,3},{4,5},{5,6},{6,7},{8,9},{9,10},{10,11},{12,13},{... | collective-permute-start | bytes 4718600 | tf_op jit(solution)/shard_map/ppermute | solution.py:19
  8.2 1.3 %collective-permute-start.1 = (bf16[128,2,24,128]{3,0,2,1:T(8,128)(2,1)}, bf16[128,2,24,128]{3,0,2,1:T(8,128)(2,1)}, u32[]{:S(2)}, u32[]{:S(2)}) collective-permute-start(bf16[128,2,24,128]{3,0,2,1:T(8,128)(2,1)} %slice.42), channel_id=1, source_target_pairs={{1,0},{2,1},{3,2},{5,4},{6,5},{7,6},{9,8},{10,9},{11,10},{13,12},{... | collective-permute-start | bytes 4718600 | tf_op jit(solution)/shard_map/ppermute | solution.py:20
  9.5 0.0 copy-done.1
  9.5 0.5 reshape_squeeze.3
  10.0 0.4 constant_dynamic-slice_fusion
  10.5 0.8 reshape.206
  11.3 15.2 %all-to-all-start.1 = ((bf16[12,2,2048]{2,1,0:T(2,128)(2,1)}), bf16[12,2,2048]{2,1,0:T(2,128)(2,1)S(1)}, u32[]{:S(2)}, u32[]{:S(2)}) async-start(bf16[12,2,2048]{2,1,0:T(2,128)(2,1)} %reshape.206), calls=%async_computation.1 | async-start | bytes 196608 | tf_op jit(solution)/shard_map/all_to_all | solution.py:67
  26.5 0.0 copy-done
  26.5 2.8 %gather_fusion = s32[384]{0:T(512)S(1)} fusion(s32[512]{0:T(512)S(1)} %bitcast.79, s32[1024]{0:T(1024)S(1)} %pad_clamp_fusion), kind=kCustom, calls=%fused_computation | custom fusion | bytes 4608 | tf_op jit(solution)/shard_map/jit(_take)/gather | solution.py:36
  29.3 0.6 compare_reduce_fusion
  30.0 0.2 compare_and_fusion
  30.1 0.6 fusion.25
  30.7 0.8 fusion.19
  31.5 6.6 %all-to-all-done.1 = bf16[12,2,2048]{2,1,0:T(2,128)(2,1)S(1)} async-done(((bf16[12,2,2048]{2,1,0:T(2,128)(2,1)}), bf16[12,2,2048]{2,1,0:T(2,128)(2,1)S(1)}, u32[]{:S(2)}, u32[]{:S(2)}) %all-to-all-start.1) | async-done | bytes 98336 | tf_op jit(solution)/shard_map/all_to_all | solution.py:67
  38.2 0.9 broadcast_in_dim.62
  39.0 6.4 %all-to-all-start = ((bf16[48,8,768]{2,1,0:T(8,128)(2,1)}), bf16[48,8,768]{2,1,0:T(8,128)(2,1)S(1)}, u32[]{:S(2)}, u32[]{:S(2)}) async-start(bf16[48,8,768]{2,1,0:T(8,128)(2,1)} %bitcast.17), calls=%async_computation | async-start | bytes 1179648 | tf_op jit(solution)/shard_map/all_to_all | solution.py:72
  45.4 0.2 reshape.207
  45.6 0.0 collective-permute-done
  45.6 0.6 collective-permute-done.1
  46.2 2.5 %pad_maximum_fusion = bf16[384,2,24,128]{3,0,2,1:T(8,128)(2,1)S(1)} fusion(bf16[128,2,24,128]{3,0,2,1:T(8,128)(2,1)} %collective-permute-done.1, bf16[128,2,24,128]{3,0,2,1:T(8,128)(2,1)} %slice.42, bf16[128,2,24,128]{3,0,2,1:T(8,128)(2,1)} %collective-permute-done), kind=kLoop, calls=%fused_computation.1 | loop fusion | flops 14155776 | bytes 9437184 | tf_op jit(solution)/shard_map/concatenate | solution.py:21
  48.8 0.9 fusion.2
  49.7 1.0 fusion
  50.7 1.9 %fusion.11 = bf16[128,24,128]{0,2,1:T(8,128)(2,1)S(1)} fusion(f32[128,24]{0,1:T(8,128)S(1)} %bitcast.87, f32[24,384,128]{2,1,0:T(8,128)S(1)} %get-tuple-element.18, f32[24,128]{1,0:T(8,128)S(1)} %get-tuple-element.17, pred[128,384]{0,1:T(8,128)(4,1)S(1)} %compare_and_fusion, bf16[384,2,24,128]{3,0,2,1:T(8,128)(2,1)S(1)} %pad_maximum_fusion), kind=kOutput, calls=%fused_computation.19 | convolution fusion | flops 307494912 | bytes 7938048 | tf_op jit(solution)/shard_map/hqk,khd->qhd/dot_general | solution.py:47
  52.6 0.3 copy.26
  52.8 18.6 %all-to-all-done = bf16[48,8,768]{2,1,0:T(8,128)(2,1)S(1)} async-done(((bf16[48,8,768]{2,1,0:T(8,128)(2,1)}), bf16[48,8,768]{2,1,0:T(8,128)(2,1)S(1)}, u32[]{:S(2)}, u32[]{:S(2)}) %all-to-all-start) | async-done | bytes 589856 | tf_op jit(solution)/shard_map/all_to_all | solution.py:72
  71.5 0.3 fusion.34
  71.8 0.8 reshape.208
  72.6 6.5 %all-to-all-start.2 = ((f32[48,1,512]{2,1,0:T(1,128)}), f32[48,1,512]{2,1,0:T(1,128)S(1)}, u32[]{:S(2)}, u32[]{:S(2)}) async-start(f32[48,1,512]{2,1,0:T(1,128)} %reshape.208), calls=%async_computation.2 | async-start | bytes 196608 | tf_op jit(solution)/shard_map/all_to_all | solution.py:76
  79.1 0.1 fusion.12
  79.1 1.9 %collective-permute-start.2 = (bf16[129,3072]{1,0:T(8,128)(2,1)S(1)}, bf16[129,3072]{1,0:T(8,128)(2,1)S(1)}, u32[]{:S(2)}, u32[]{:S(2)}) collective-permute-start(bf16[129,3072]{1,0:T(8,128)(2,1)S(1)} %fusion.12), channel_id=1, source_target_pairs={{576,0},{0,192},{192,384},{384,576},{577,1},{1,193},{193,385},{385... | collective-permute-start | bytes 2377736 | tf_op jit(solution)/shard_map/ppermute | solution.py:14
  81.1 9.5 %all-to-all-done.2 = f32[48,1,512]{2,1,0:T(1,128)S(1)} async-done(((f32[48,1,512]{2,1,0:T(1,128)}), f32[48,1,512]{2,1,0:T(1,128)S(1)}, u32[]{:S(2)}, u32[]{:S(2)}) %all-to-all-start.2) | async-done | bytes 98336 | tf_op jit(solution)/shard_map/all_to_all | solution.py:76
  90.6 0.6 broadcast.245
  91.2 0.9 reduce.10
  92.1 0.1 reshape.209
  92.2 0.1 broadcast_select_fusion
  92.4 1.2 %reshape.210 = f32[16,1,6144]{2,1,0:T(1,128)} reshape(f32[16,12,8,64]{3,2,1,0:T(8,128)S(1)} %broadcast_select_fusion) | data formatting | bytes 786432
  93.6 7.2 %all-to-all-start.3 = ((f32[16,1,6144]{2,1,0:T(1,128)}), f32[16,1,6144]{2,1,0:T(1,128)S(1)}, u32[]{:S(2)}, u32[]{:S(2)}) async-start(f32[16,1,6144]{2,1,0:T(1,128)} %reshape.210), calls=%async_computation.3 | async-start | bytes 786432 | tf_op jit(solution)/shard_map/all_to_all | solution.py:83
  100.8 0.0 collective-permute-done.2
  100.8 14.4 %all-to-all-done.3 = f32[16,1,6144]{2,1,0:T(1,128)S(1)} async-done(((f32[16,1,6144]{2,1,0:T(1,128)}), f32[16,1,6144]{2,1,0:T(1,128)S(1)}, u32[]{:S(2)}, u32[]{:S(2)}) %all-to-all-start.3) | async-done | bytes 393248 | tf_op jit(solution)/shard_map/all_to_all | solution.py:83
  115.2 1.6 %reduce.11 = f32[16,6144]{1,0:T(8,128)S(1)} reduce(f32[16,1,6144]{2,1,0:T(1,128)S(1)} %all-to-all-done.3, f32[]{:T(128)} %broadcast.245), dimensions={1}, to_apply=%all_to_all.25.reduce_sub_computation | reduce | bytes 786436 | tf_op jit(solution)/shard_map/all_to_all | solution.py:83
  116.9 0.3 reshape.211
  117.2 0.1 copy.29
  117.3 0.2 reshape.192
  117.5 1.7 %fusion.13 = bf16[1,1,128,3072]{3,2,1,0:T(8,128)(2,1)} fusion(bf16[129,3072]{1,0:T(8,128)(2,1)S(1)} %collective-permute-done.2, f32[8,3072]{1,0:T(8,128)S(1)} %reshape.192, s32[128]{0:T(128)S(1)} %fusion.27), kind=kOutput, calls=%fused_computation.22 | convolution fusion | flops 38929408 | bytes 1671680 | tf_op jit(solution)/shard_map/dot_general | solution.py:107
  (10 shorter events, 0.1 us)
Async XLA Ops:
  0.0 9.5 %copy-start.1 = (bf16[1,64,3072]{2,1,0:T(8,128)(2,1)S(1)}, bf16[1,64,3072]{2,1,0:T(8,128)(2,1)}, u32[]{:S(2)}) copy-start(bf16[1,64,3072]{2,1,0:T(8,128)(2,1)} %param.9) | copy-start | bytes 1179652
  0.0 26.5 %copy-start = (s32[1,1,512]{2,1,0:T(1,128)S(1)}, s32[1,1,512]{2,1,0:T(1,128)}, u32[]{:S(2)}) copy-start(s32[1,1,512]{2,1,0:T(1,128)} %param.7) | copy-start | bytes 6148
  3.6 42.0 %collective-permute-start = (bf16[128,2,24,128]{3,0,2,1:T(8,128)(2,1)}, bf16[128,2,24,128]{3,0,2,1:T(8,128)(2,1)}, u32[]{:S(2)}, u32[]{:S(2)}) collective-permute-start(bf16[128,2,24,128]{3,0,2,1:T(8,128)(2,1)} %slice.42), channel_id=1, source_target_pairs={{0,1},{1,2},{2,3},{4,5},{5,6},{6,7},{8,9},{9,10},{10,11},{12,13},{... | collective-permute-start | bytes 4718600 | tf_op jit(solution)/shard_map/ppermute | solution.py:19
  8.2 38.1 %collective-permute-start.1 = (bf16[128,2,24,128]{3,0,2,1:T(8,128)(2,1)}, bf16[128,2,24,128]{3,0,2,1:T(8,128)(2,1)}, u32[]{:S(2)}, u32[]{:S(2)}) collective-permute-start(bf16[128,2,24,128]{3,0,2,1:T(8,128)(2,1)} %slice.42), channel_id=1, source_target_pairs={{1,0},{2,1},{3,2},{5,4},{6,5},{7,6},{9,8},{10,9},{11,10},{13,12},{... | collective-permute-start | bytes 4718600 | tf_op jit(solution)/shard_map/ppermute | solution.py:20
  11.3 26.8 %all-to-all-start.1 = ((bf16[12,2,2048]{2,1,0:T(2,128)(2,1)}), bf16[12,2,2048]{2,1,0:T(2,128)(2,1)S(1)}, u32[]{:S(2)}, u32[]{:S(2)}) async-start(bf16[12,2,2048]{2,1,0:T(2,128)(2,1)} %reshape.206), calls=%async_computation.1 | async-start | bytes 196608 | tf_op jit(solution)/shard_map/all_to_all | solution.py:67
  39.0 32.5 %all-to-all-start = ((bf16[48,8,768]{2,1,0:T(8,128)(2,1)}), bf16[48,8,768]{2,1,0:T(8,128)(2,1)S(1)}, u32[]{:S(2)}, u32[]{:S(2)}) async-start(bf16[48,8,768]{2,1,0:T(8,128)(2,1)} %bitcast.17), calls=%async_computation | async-start | bytes 1179648 | tf_op jit(solution)/shard_map/all_to_all | solution.py:72
  72.6 18.0 %all-to-all-start.2 = ((f32[48,1,512]{2,1,0:T(1,128)}), f32[48,1,512]{2,1,0:T(1,128)S(1)}, u32[]{:S(2)}, u32[]{:S(2)}) async-start(f32[48,1,512]{2,1,0:T(1,128)} %reshape.208), calls=%async_computation.2 | async-start | bytes 196608 | tf_op jit(solution)/shard_map/all_to_all | solution.py:76
  79.1 21.7 %collective-permute-start.2 = (bf16[129,3072]{1,0:T(8,128)(2,1)S(1)}, bf16[129,3072]{1,0:T(8,128)(2,1)S(1)}, u32[]{:S(2)}, u32[]{:S(2)}) collective-permute-start(bf16[129,3072]{1,0:T(8,128)(2,1)S(1)} %fusion.12), channel_id=1, source_target_pairs={{576,0},{0,192},{192,384},{384,576},{577,1},{1,193},{193,385},{385... | collective-permute-start | bytes 2377736 | tf_op jit(solution)/shard_map/ppermute | solution.py:14
  93.6 21.7 %all-to-all-start.3 = ((f32[16,1,6144]{2,1,0:T(1,128)}), f32[16,1,6144]{2,1,0:T(1,128)S(1)}, u32[]{:S(2)}, u32[]{:S(2)}) async-start(f32[16,1,6144]{2,1,0:T(1,128)} %reshape.210), calls=%async_computation.3 | async-start | bytes 786432 | tf_op jit(solution)/shard_map/all_to_all | solution.py:83

commit v10 on v9

--- a/solution.py
+++ b/solution.py
@@ -64,14 +64,21 @@
         rows_weight.reshape(row_count, nz, n_sp, col_block), lax.axis_index("sp"), axis=2,
         keepdims=False,
     )
-    w_cols = lax.all_to_all(mine, "dz", split_axis=1, concat_axis=0, tiled=True).reshape(
-        nz * row_count, col_block
+    act_part = jnp.transpose(cond_act.reshape(seg_count, nx, feat_block), (1, 0, 2))
+    act_part = jnp.broadcast_to(
+        act_part.reshape(nx, 1, seg_count * feat_block), (nx, nz, seg_count * feat_block)
     )
-    sent = jnp.transpose(cond_act.reshape(seg_count, nx, feat_block), (1, 0, 2))
-    sent = jnp.broadcast_to(sent[:, None], (nx, nz, seg_count, feat_block))
-    feat = lax.all_to_all(
-        sent.reshape(nx * nz, seg_count, feat_block), dp, split_axis=0, concat_axis=0, tiled=True
-    ).reshape(nx * nz * seg_count, feat_block)
+    w_part = jnp.transpose(mine, (1, 0, 2)).reshape(1, nz, row_count * col_block)
+    my_x = lax.axis_index("dx")
+    same_x = (jnp.arange(nx, dtype=jnp.int32) == my_x)[:, None, None]
+    w_part = jnp.where(same_x, w_part, jnp.zeros_like(w_part))
+    sent = jnp.concatenate([act_part, w_part], axis=2).reshape(nx * nz, -1)
+    got = lax.all_to_all(sent, dp, split_axis=0, concat_axis=0, tiled=True)
+    act_size = seg_count * feat_block
+    feat = got[:, :act_size].reshape(nx * nz * seg_count, feat_block)
+    w_cols = lax.dynamic_index_in_dim(
+        got[:, act_size:].reshape(nx, nz, row_count * col_block), my_x, axis=0, keepdims=False
+    ).reshape(nz * row_count, col_block)
     partial = jnp.dot(feat, w_cols, preferred_element_type=jnp.float32)
     parts = lax.all_to_all(
         partial.reshape(nx * nz, seg_count, col_block), dp, split_axis=0, concat_axis=0, tiled=True

time: 121 us -> 132 us (1.091)
  the two profiles are of different devices: /device:TPU:6 before, /device:TPU:9 now
where the time goes in v10:
time: 132 us
  starting transfers between devices  52.5 us (40%)
  waiting for transfers between devices  40.9 us (31%)
  local copies, waits for them, and re-layouts  20.2 us (15%)
  other arithmetic  12.9 us (10%)
  matrix products  4.78 us (4%)
    all_to_all x1, waiting for transfers between devices, sample_gates(): got = lax.all_to_all(sent, dp, split_axis=0, concat_axis=0, tiled=True)  23 us
    all_to_all x1, starting transfers between devices, sample_gates(): got = lax.all_to_all(sent, dp, split_axis=0, concat_axis=0, tiled=True)  18.2 us
    all_to_all x1, waiting for transfers between devices, sample_gates(): lax.all_to_all(sent, ('section', 'sp'), split_axis=0, concat_axis=0, tile...  13.1 us
    all_to_all x1, starting transfers between devices, sample_gates(): lax.all_to_all(partial.reshape(nx * nz, seg_count, col_block), dp, split_...  11.2 us
    all_to_all x1, starting transfers between devices, sample_gates(): lax.all_to_all(sent, ('section', 'sp'), split_axis=0, concat_axis=0, tile...  10.6 us
    unnamed x16, local copies, waits for them, and re-layouts  9.94 us
    ppermute x1, starting transfers between devices, from_behind(): return lax.ppermute(block, axis, route)  7.21 us
    all_to_all x1, waiting for transfers between devices, sample_gates(): lax.all_to_all(partial.reshape(nx * nz, seg_count, col_block), dp, split_...  4.55 us
  transfers between devices with their start and end apart: 6, of which 4 were waited for; matrix products, arithmetic and copies ran while one was open for 21% of the time, Pallas kernels for 0%

profile of v10, /device:TPU:9, one launch (start us, length us, event | category | flops | bytes accessed | tf_op | source)
XLA Modules:
  0.0 131.7 jit_solution(5899388280750901112)
XLA Ops:
  0.0 2.3 %copy.56 = bf16[1,1,128,3,24,128]{5,2,4,3,1,0:T(8,128)(2,1)S(1)} copy(bf16[1,1,128,3,24,128]{5,4,3,2,1,0:T(8,128)(2,1)} %param.6) | data formatting | bytes 4718592 | tf_op args[0]
  2.3 1.3 slice.50
  3.6 1.9 %collective-permute-start.1 = (bf16[128,2,24,128]{3,0,2,1:T(8,128)(2,1)}, bf16[128,2,24,128]{3,0,2,1:T(8,128)(2,1)}, u32[]{:S(2)}, u32[]{:S(2)}) collective-permute-start(bf16[128,2,24,128]{3,0,2,1:T(8,128)(2,1)} %slice.50), channel_id=1, source_target_pairs={{1,0},{2,1},{3,2},{5,4},{6,5},{7,6},{9,8},{10,9},{11,10},{13,12},{... | collective-permute-start | bytes 4718600 | tf_op jit(solution)/shard_map/ppermute | solution.py:20
  5.5 3.4 %collective-permute-start = (bf16[128,2,24,128]{3,0,2,1:T(8,128)(2,1)}, bf16[128,2,24,128]{3,0,2,1:T(8,128)(2,1)}, u32[]{:S(2)}, u32[]{:S(2)}) collective-permute-start(bf16[128,2,24,128]{3,0,2,1:T(8,128)(2,1)} %slice.50), channel_id=1, source_target_pairs={{0,1},{1,2},{2,3},{4,5},{5,6},{6,7},{8,9},{9,10},{10,11},{12,13},{... | collective-permute-start | bytes 4718600 | tf_op jit(solution)/shard_map/ppermute | solution.py:19
  8.9 0.5 reshape_squeeze.3
  9.4 0.4 constant_dynamic-slice_fusion.1
  9.8 0.2 broadcast_in_dim.102
  10.1 0.9 broadcast_in_dim.104
  11.1 0.8 fusion.21
  12.0 1.0 concatenate.16
  13.0 1.1 broadcast_select_fusion.1
  14.1 1.1 maximum_bitcast_fusion
  15.2 0.5 broadcast.256
  15.8 2.0 %reduce.10 = bf16[48,10240]{1,0:T(8,128)(2,1)} reduce(bf16[48,1,10240]{2,0,1:T(8,128)(2,1)S(1)} %maximum_bitcast_fusion, bf16[]{:T(256)} %broadcast.256), dimensions={1}, to_apply=%copy.43.reduce_sub_computation | reduce | bytes 1966082 | tf_op jit(solution)/shard_map/all_to_all | solution.py:76
  17.8 3.7 %reshape.221 = bf16[48,2,5120]{2,1,0:T(2,128)(2,1)} reshape(bf16[48,10240]{1,0:T(8,128)(2,1)} %reduce.10) | data formatting | bytes 1966080
  21.5 18.2 %all-to-all-start = ((bf16[48,2,5120]{2,1,0:T(2,128)(2,1)}), bf16[48,2,5120]{2,1,0:T(2,128)(2,1)S(1)}, u32[]{:S(2)}, u32[]{:S(2)}) async-start(bf16[48,2,5120]{2,1,0:T(2,128)(2,1)} %reshape.221), calls=%async_computation | async-start | bytes 1966080 | tf_op jit(solution)/shard_map/all_to_all | solution.py:76
  39.7 2.8 %gather_fusion = s32[384]{0:T(512)S(1)} fusion(s32[512]{0:T(512)S(1)} %bitcast.77, s32[1024]{0:T(1024)S(1)} %pad_clamp_fusion), kind=kCustom, calls=%fused_computation | custom fusion | bytes 4608 | tf_op jit(solution)/shard_map/jit(_take)/gather | solution.py:36
  42.5 0.6 compare_reduce_fusion
  43.2 0.7 fusion.27
  43.9 0.2 compare_and_fusion
  44.1 2.5 %pad_maximum_fusion = bf16[384,2,24,128]{3,0,2,1:T(8,128)(2,1)S(1)} fusion(bf16[128,2,24,128]{3,0,2,1:T(8,128)(2,1)} %collective-permute-done.1, bf16[128,2,24,128]{3,0,2,1:T(8,128)(2,1)} %slice.50, bf16[128,2,24,128]{3,0,2,1:T(8,128)(2,1)} %collective-permute-done), kind=kLoop, calls=%fused_computation.1 | loop fusion | flops 14155776 | bytes 9437184 | tf_op jit(solution)/shard_map/concatenate | solution.py:21
  46.6 0.9 fusion.2
  47.5 1.0 fusion
  48.5 1.9 %fusion.11 = bf16[128,24,128]{0,2,1:T(8,128)(2,1)S(1)} fusion(f32[128,24]{0,1:T(8,128)S(1)} %bitcast.89, f32[24,384,128]{2,1,0:T(8,128)S(1)} %get-tuple-element.18, f32[24,128]{1,0:T(8,128)S(1)} %get-tuple-element.17, pred[128,384]{0,1:T(8,128)(4,1)S(1)} %compare_and_fusion, bf16[384,2,24,128]{3,0,2,1:T(8,128)(2,1)S(1)} %pad_maximum_fusion), kind=kOutput, calls=%fused_computation.19 | convolution fusion | flops 307494912 | bytes 7938048 | tf_op jit(solution)/shard_map/hqk,khd->qhd/dot_general | solution.py:47
  50.4 1.2 copy.41
  51.5 23.0 %all-to-all-done = bf16[48,2,5120]{2,1,0:T(2,128)(2,1)S(1)} async-done(((bf16[48,2,5120]{2,1,0:T(2,128)(2,1)}), bf16[48,2,5120]{2,1,0:T(2,128)(2,1)S(1)}, u32[]{:S(2)}, u32[]{:S(2)}) %all-to-all-start) | async-done | bytes 983072 | tf_op jit(solution)/shard_map/all_to_all | solution.py:76
  74.6 0.8 reshape.222
  75.4 0.6 copy.57
  76.1 0.1 copy.52
  76.3 0.2 reshape.205
  76.5 0.3 fusion.14
  76.8 0.8 reshape.223
  77.6 11.2 %all-to-all-start.1 = ((f32[48,1,512]{2,1,0:T(1,128)}), f32[48,1,512]{2,1,0:T(1,128)S(1)}, u32[]{:S(2)}, u32[]{:S(2)}) async-start(f32[48,1,512]{2,1,0:T(1,128)} %reshape.223), calls=%async_computation.1 | async-start | bytes 196608 | tf_op jit(solution)/shard_map/all_to_all | solution.py:83
  88.9 7.2 %collective-permute-start.2 = (bf16[129,3072]{1,0:T(8,128)(2,1)S(1)}, bf16[129,3072]{1,0:T(8,128)(2,1)S(1)}, u32[]{:S(2)}, u32[]{:S(2)}) collective-permute-start(bf16[129,3072]{1,0:T(8,128)(2,1)S(1)} %fusion.12), channel_id=1, source_target_pairs={{576,0},{0,192},{192,384},{384,576},{577,1},{1,193},{193,385},{385... | collective-permute-start | bytes 2377736 | tf_op jit(solution)/shard_map/ppermute | solution.py:14
  96.1 4.6 %all-to-all-done.1 = f32[48,1,512]{2,1,0:T(1,128)S(1)} async-done(((f32[48,1,512]{2,1,0:T(1,128)}), f32[48,1,512]{2,1,0:T(1,128)S(1)}, u32[]{:S(2)}, u32[]{:S(2)}) %all-to-all-start.1) | async-done | bytes 98336 | tf_op jit(solution)/shard_map/all_to_all | solution.py:83
  100.7 0.6 broadcast.257
  101.3 0.9 reduce.11
  102.2 0.1 reshape.224
  102.3 0.1 broadcast_select_fusion
  102.5 1.2 reshape.225
  103.7 10.6 %all-to-all-start.2 = ((f32[16,1,6144]{2,1,0:T(1,128)}), f32[16,1,6144]{2,1,0:T(1,128)S(1)}, u32[]{:S(2)}, u32[]{:S(2)}) async-start(f32[16,1,6144]{2,1,0:T(1,128)} %reshape.225), calls=%async_computation.2 | async-start | bytes 786432 | tf_op jit(solution)/shard_map/all_to_all | solution.py:90
  114.3 0.2 collective-permute-done.2
  114.5 13.1 %all-to-all-done.2 = f32[16,1,6144]{2,1,0:T(1,128)S(1)} async-done(((f32[16,1,6144]{2,1,0:T(1,128)}), f32[16,1,6144]{2,1,0:T(1,128)S(1)}, u32[]{:S(2)}, u32[]{:S(2)}) %all-to-all-start.2) | async-done | bytes 393248 | tf_op jit(solution)/shard_map/all_to_all | solution.py:90
  127.6 1.6 %reduce.12 = f32[16,6144]{1,0:T(8,128)S(1)} reduce(f32[16,1,6144]{2,1,0:T(1,128)S(1)} %all-to-all-done.2, f32[]{:T(128)} %broadcast.257), dimensions={1}, to_apply=%all_to_all.18.reduce_sub_computation | reduce | bytes 786436 | tf_op jit(solution)/shard_map/all_to_all | solution.py:90
  129.3 0.3 reshape.226
  129.6 0.1 copy.45
  129.7 0.2 reshape.207
  129.9 1.7 %fusion.13 = bf16[1,1,128,3072]{3,2,1,0:T(8,128)(2,1)} fusion(bf16[129,3072]{1,0:T(8,128)(2,1)S(1)} %collective-permute-done.2, f32[8,3072]{1,0:T(8,128)S(1)} %reshape.207, s32[128]{0:T(128)S(1)} %fusion.29), kind=kOutput, calls=%fused_computation.24 | convolution fusion | flops 38929408 | bytes 1671680 | tf_op jit(solution)/shard_map/dot_general | solution.py:114
  (29 shorter events, 0.7 us)
Async XLA Ops:
  0.0 8.9 %copy-start.2 = (bf16[1,64,3072]{2,1,0:T(8,128)(2,1)S(1)}, bf16[1,64,3072]{2,1,0:T(8,128)(2,1)}, u32[]{:S(2)}) copy-start(bf16[1,64,3072]{2,1,0:T(8,128)(2,1)} %param.9) | copy-start | bytes 1179652
  3.6 40.5 %collective-permute-start.1 = (bf16[128,2,24,128]{3,0,2,1:T(8,128)(2,1)}, bf16[128,2,24,128]{3,0,2,1:T(8,128)(2,1)}, u32[]{:S(2)}, u32[]{:S(2)}) collective-permute-start(bf16[128,2,24,128]{3,0,2,1:T(8,128)(2,1)} %slice.50), channel_id=1, source_target_pairs={{1,0},{2,1},{3,2},{5,4},{6,5},{7,6},{9,8},{10,9},{11,10},{13,12},{... | collective-permute-start | bytes 4718600 | tf_op jit(solution)/shard_map/ppermute | solution.py:20
  5.5 38.6 %collective-permute-start = (bf16[128,2,24,128]{3,0,2,1:T(8,128)(2,1)}, bf16[128,2,24,128]{3,0,2,1:T(8,128)(2,1)}, u32[]{:S(2)}, u32[]{:S(2)}) collective-permute-start(bf16[128,2,24,128]{3,0,2,1:T(8,128)(2,1)} %slice.50), channel_id=1, source_target_pairs={{0,1},{1,2},{2,3},{4,5},{5,6},{6,7},{8,9},{9,10},{10,11},{12,13},{... | collective-permute-start | bytes 4718600 | tf_op jit(solution)/shard_map/ppermute | solution.py:19
  12.0 27.7 %copy-start = (s32[1,1,512]{2,1,0:T(1,128)S(1)}, s32[1,1,512]{2,1,0:T(1,128)}, u32[]{:S(2)}) copy-start(s32[1,1,512]{2,1,0:T(1,128)} %param.7) | copy-start | bytes 6148
  21.5 53.1 %all-to-all-start = ((bf16[48,2,5120]{2,1,0:T(2,128)(2,1)}), bf16[48,2,5120]{2,1,0:T(2,128)(2,1)S(1)}, u32[]{:S(2)}, u32[]{:S(2)}) async-start(bf16[48,2,5120]{2,1,0:T(2,128)(2,1)} %reshape.221), calls=%async_computation | async-start | bytes 1966080 | tf_op jit(solution)/shard_map/all_to_all | solution.py:76
  75.4 13.4 %copy-start.1 = (bf16[128,3072]{1,0:T(8,128)(2,1)S(1)}, bf16[128,3072]{1,0:T(8,128)(2,1)}, u32[]{:S(2)}) copy-start(bf16[128,3072]{1,0:T(8,128)(2,1)} %copy.41) | copy-start | bytes 2359300
  77.6 23.1 %all-to-all-start.1 = ((f32[48,1,512]{2,1,0:T(1,128)}), f32[48,1,512]{2,1,0:T(1,128)S(1)}, u32[]{:S(2)}, u32[]{:S(2)}) async-start(f32[48,1,512]{2,1,0:T(1,128)} %reshape.223), calls=%async_computation.1 | async-start | bytes 196608 | tf_op jit(solution)/shard_map/all_to_all | solution.py:83
  88.9 25.6 %collective-permute-start.2 = (bf16[129,3072]{1,0:T(8,128)(2,1)S(1)}, bf16[129,3072]{1,0:T(8,128)(2,1)S(1)}, u32[]{:S(2)}, u32[]{:S(2)}) collective-permute-start(bf16[129,3072]{1,0:T(8,128)(2,1)S(1)} %fusion.12), channel_id=1, source_target_pairs={{576,0},{0,192},{192,384},{384,576},{577,1},{1,193},{193,385},{385... | collective-permute-start | bytes 2377736 | tf_op jit(solution)/shard_map/ppermute | solution.py:14
  103.7 23.9 %all-to-all-start.2 = ((f32[16,1,6144]{2,1,0:T(1,128)}), f32[16,1,6144]{2,1,0:T(1,128)S(1)}, u32[]{:S(2)}, u32[]{:S(2)}) async-start(f32[16,1,6144]{2,1,0:T(1,128)} %reshape.225), calls=%async_computation.2 | async-start | bytes 786432 | tf_op jit(solution)/shard_map/all_to_all | solution.py:90
